TPU v7x, 512 devices: a whole 4x8x8 slice. The times are simulated.
512 devices in a mesh: shift: 4 (over x_hi, core), space: 128 (over y, z, x_lo).
Axes of the slice: x: 4 (x_hi: 2, x_lo: 2; x = x_hi * 2 + x_lo), y: 8, z: 8, core: 2. Of those that a mesh axis runs over, the one named last changes fastest.
Arguments:
- labels: int32 [256, 32, 256], P('space'), may hold values from 0 to 7
- conductance: float32 [8], replicated, may hold values from 0.2 to 5
- capacity_table: float32 [8], replicated, may hold values from 0.5 to 2
- shift_values: float32 [8], replicated, may hold values from 0.1 to 4
- prior_basis: float32 [256, 256, 32, 256], P(None, 'space', 'shift'), may hold values from -6 to 6
Outputs:
- new_block: float32 [8, 8, 256, 32, 256], P(None, None, 'space', 'shift')
- coefficients: float32 [64, 256], replicated
- factor: float32 [64, 64], replicated
All inputs are finite; a program needn't handle non-finite values.
Results may differ from a plain program's by a relative error of at most 0.0003.
Values sent between devices are 32-bit elements; how exact they have to be, the bound alone decides.
No kernel may reach another device: no remote copies, remote signals or barrier semaphores. Data moves between devices by JAX's collectives and lax.ppermute only.
A program may use at most 64 MiB of HBM per device.

v0:
```python
import jax
import jax.numpy as jnp
from jax import lax
from jax.sharding import PartitionSpec as P

COLS = 8
SWEEPS = 4


LOWER_BOUND = 0.1
UPPER_BOUND = 2.0


def padded_2(cells, sides, width):
    for axis, dim in sides:
        count = lax.axis_size(axis)
        ends = count - 1
        head = lax.slice_in_dim(cells, 0, width, axis=dim)
        tail = lax.slice_in_dim(cells, cells.shape[dim] - width, cells.shape[dim], axis=dim)
        cells = jnp.concatenate(
            [
                lax.ppermute(tail, axis, [(i, (i + 1) % count) for i in range(ends)]),
                cells,
                lax.ppermute(head, axis, [((i + 1) % count, i) for i in range(ends)]),
            ],
            axis=dim,
        )
    return cells


def allsum(value):
    axes = ("shift", "space")
    total = lax.axis_size("shift") * lax.axis_size("space")
    if total & (total - 1):
        return lax.psum(value, axes)
    for bit in range(total.bit_length() - 1):
        mask = 1 << bit
        value = value + lax.ppermute(value, axes, [(i, i ^ mask) for i in range(total)])
    return value


def pack_symmetric(full, half):
    row = lax.broadcasted_iota(jnp.int32, (half, half), 0)
    col = lax.broadcasted_iota(jnp.int32, (half, half), 1)
    corner = jnp.where(row > col, full[:half, :half], full[half:, half:])
    return jnp.concatenate([full[:half, half:], corner, jnp.diagonal(full[:half, :half])[None]], axis=0)


def unpack_symmetric(packed, half):
    row = lax.broadcasted_iota(jnp.int32, (half, half), 0)
    col = lax.broadcasted_iota(jnp.int32, (half, half), 1)
    upper = packed[:half]
    corner = packed[half : 2 * half]
    first = jnp.where(row > col, corner, corner.T)
    first = jnp.where(row == col, packed[2 * half][None, :], first)
    second = jnp.where(row < col, corner, corner.T)
    return jnp.concatenate(
        [jnp.concatenate([first, upper], axis=1), jnp.concatenate([upper.T, second], axis=1)], axis=0
    )


def lookup(labels, table):
    materials = jnp.arange(table.shape[0], dtype=jnp.int32)
    onehot = (labels[None] == materials[:, None, None, None]).astype(jnp.float32)
    return jnp.sum(onehot * table[:, None, None, None], axis=0)


def conductances(conduct, padded):
    west_face = 0.5 * (conduct + padded[:-2, 1:-1, 1:-1])
    east_face = 0.5 * (conduct + padded[2:, 1:-1, 1:-1])
    south_face = 0.5 * (conduct + padded[1:-1, :-2, 1:-1])
    north_face = 0.5 * (conduct + padded[1:-1, 2:, 1:-1])
    below_face = 0.5 * (conduct + padded[1:-1, 1:-1, :-2])
    above_face = 0.5 * (conduct + padded[1:-1, 1:-1, 2:])
    return (west_face, east_face, south_face, north_face, below_face, above_face)


def neighbours(padded, face_list):
    west_face, east_face, south_face, north_face, below_face, above_face = face_list
    summed = west_face * padded[..., :-2, 1:-1, 1:-1] + east_face * padded[..., 2:, 1:-1, 1:-1]
    summed = (
        summed
        + south_face * padded[..., 1:-1, :-2, 1:-1]
        + north_face * padded[..., 1:-1, 2:, 1:-1]
    )
    summed = (
        summed
        + below_face * padded[..., 1:-1, 1:-1, :-2]
        + above_face * padded[..., 1:-1, 1:-1, 2:]
    )
    return summed


def diagonal_of(face_list, shift_list, capacity):
    west_face, east_face, south_face, north_face, below_face, above_face = face_list
    summed = west_face + east_face + (south_face + north_face) + (below_face + above_face)
    return summed[None, None] + shift_list[:, None, None, None, None] * capacity[None, None]


def chebyshev(source, face_list, diagonal, padder, anchor):
    center = 0.5 * (UPPER_BOUND + LOWER_BOUND)
    spread = 0.5 * (UPPER_BOUND - LOWER_BOUND)
    ratio_value = center / spread
    reciprocal = 1.0 / diagonal
    solution = jnp.zeros_like(source)
    remainder = source
    weight_old = 1.0 / ratio_value
    direction = reciprocal * remainder / center
    for sweep_index in range(SWEEPS):
        solution = solution + direction
        if sweep_index + 1 < SWEEPS:
            padded = padder(direction)
            if sweep_index == 0:
                anchor, padded = lax.optimization_barrier((anchor, padded))
            applied = diagonal * direction - neighbours(padded, face_list)
            remainder = remainder - applied
            weight_new = 1.0 / (2.0 * ratio_value - weight_old)
            direction = weight_new * weight_old * direction + 2.0 * weight_new / spread * (
                reciprocal * remainder
            )
            weight_old = weight_new
    return solution, anchor


def products(left_side, right_side):
    return lax.dot_general(
        left_side, right_side, (((1,), (1,)), ((), ())), precision=lax.Precision.HIGHEST
    )


def matmul(left_side, right_side):
    return jnp.dot(left_side, right_side, precision=lax.Precision.HIGHEST)


def local(labels, conductance, capacity_table, shift_values, prior_basis):
    groups = lax.axis_size("shift")
    shifts_all = shift_values.shape[0]
    per_device = shifts_all // groups
    new_count = shifts_all * COLS
    basis_count = prior_basis.shape[0]
    slab_x = prior_basis.shape[1]
    quarter = prior_basis.shape[2]
    depth = prior_basis.shape[3]
    flat_basis = prior_basis.reshape(basis_count, slab_x * quarter * depth)
    cell_weight = 1.0 / (slab_x * quarter * depth * groups * lax.axis_size("space"))
    tail_columns = prior_basis[basis_count - new_count :]
    conduct = lookup(labels, conductance)
    capacity = lookup(labels, capacity_table)
    rimmed = padded_2(conduct, (("space", 0),), 1)
    face_list = conductances(conduct, jnp.pad(rimmed, ((0, 0), (1, 1), (1, 1))))
    shift_list = lax.dynamic_slice_in_dim(
        shift_values, lax.axis_index("shift") * per_device, per_device, 0
    )
    diagonal = diagonal_of(face_list, shift_list, capacity)
    starting = lax.all_to_all(tail_columns, "shift", split_axis=0, concat_axis=2, tiled=True)
    full_y = starting.shape[2]
    source = starting.reshape(per_device, COLS, slab_x, full_y, depth) * capacity[None, None]

    def padder(field):
        widened = padded_2(field, (("space", 2),), 1)
        return jnp.pad(widened, ((0, 0), (0, 0), (0, 0), (1, 1), (1, 1)))

    half = basis_count // 2
    packed = pack_symmetric(products(flat_basis, flat_basis), half)
    fields, packed = chebyshev(source, face_list, diagonal, padder, packed)
    merged = fields.reshape(per_device * COLS, slab_x, full_y, depth)
    regrouped = lax.all_to_all(merged, "shift", split_axis=2, concat_axis=0, tiled=True)
    columns = regrouped.reshape(new_count, slab_x * quarter * depth)
    own = jnp.concatenate([products(columns, flat_basis), products(columns, columns)], axis=1)
    total = allsum(jnp.concatenate([own.reshape(-1, half), packed], axis=0)) * cell_weight
    sums = total[: own.size // half].reshape(own.shape)
    basis_gram = unpack_symmetric(total[own.size // half :], half)
    first_proj = sums[:, :basis_count]
    second_proj = first_proj - matmul(first_proj, basis_gram)
    coefficients = first_proj + second_proj
    columns = columns - matmul(coefficients, flat_basis)
    gram_matrix = (
        sums[:, basis_count:]
        - products(coefficients, first_proj)
        - products(first_proj, coefficients)
        + products(matmul(coefficients, basis_gram), coefficients)
    )
    factor = jnp.linalg.cholesky(gram_matrix)
    orthonormal = lax.linalg.triangular_solve(factor, columns, left_side=True, lower=True)
    new_block = orthonormal.reshape(shifts_all, COLS, slab_x, quarter, depth)
    return (new_block, coefficients, factor)


def solution(mesh):
    in_specs = (P("space", None, None), P(), P(), P(), P(None, "space", "shift", None))
    out_specs = (P(None, None, "space", "shift", None), P(), P())
    return jax.shard_map(local, mesh=mesh, in_specs=in_specs, out_specs=out_specs, check_vma=False)
```

profile of v0, /device:TPU:1, one launch (start us, length us, event | category | flops | bytes accessed | tf_op | source)
XLA Modules:
  0.0 287.9 jit_solution(5014721906518438596)
XLA Ops:
  0.6 1.0 select_reduce_fusion.1
  1.7 3.9 %collective-permute-start = (f32[1,32,256]{2,1,0:T(8,128)S(1)}, f32[1,32,256]{2,1,0:T(8,128)S(1)}, u32[]{:S(2)}, u32[]{:S(2)}) collective-permute-start(f32[1,32,256]{2,1,0:T(8,128)S(1)} %get-tuple-element.54), channel_id=1, source_target_pairs={{0,1},{1,2},{2,3},{3,4},{4,5},{5,6},{6,7},{7,8},{8,9},{9,10},{10,1... | collective-permute-start | bytes 98312 | tf_op jit(solution)/shard_map/ppermute | solution.py:22
  5.6 1.3 collective-permute-start.1
  6.9 2.3 slice.161
  9.2 7.7 %all-to-all-start = ((f32[64,2,8,256]{3,2,1,0:T(8,128)}), f32[64,2,8,256]{3,2,1,0:T(8,128)S(1)}, u32[]{:S(2)}, u32[]{:S(2)}) async-start(f32[64,2,8,256]{3,2,1,0:T(8,128)} %slice.161), calls=%async_computation | async-start | bytes 2097152 | tf_op jit(solution)/shard_map/all_to_all | solution.py:155
  16.9 16.9 %fusion.5 = f32[256,256]{1,0:T(8,128)S(1)} fusion(f32[256,2,8,256]{3,2,1,0:T(8,128)} %param.9), kind=kOutput, calls=%fused_computation.17 | convolution fusion | flops 3221225472 | bytes 4456448 | tf_op jit(solution)/shard_map/dot_general | solution.py:126
  34.5 0.2 fusion.34
  34.6 1.1 fusion.66
  35.7 5.1 %collective-permute-start.2 = (f32[2,8,1,32,256]{4,3,2,1,0:T(8,128)}, f32[2,8,1,32,256]{4,3,2,1,0:T(8,128)}, u32[]{:S(2)}, u32[]{:S(2)}) collective-permute-start(f32[2,8,1,32,256]{4,3,2,1,0:T(8,128)} %get-tuple-element.41), channel_id=1, source_target_pairs={{0,1},{1,2},{2,3},{3,4},{4,5},{5,6},{6,7},{7,8},{8,9},{9,10},{10,1... | collective-permute-start | bytes 1572872 | tf_op jit(solution)/shard_map/ppermute | solution.py:22
  40.8 1.3 collective-permute-start.3
  42.2 1.2 gather_fusion
  43.5 19.3 %collective-permute-done.2 = f32[2,8,1,32,256]{4,3,2,1,0:T(8,128)} collective-permute-done((f32[2,8,1,32,256]{4,3,2,1,0:T(8,128)}, f32[2,8,1,32,256]{4,3,2,1,0:T(8,128)}, u32[]{:S(2)}, u32[]{:S(2)}) %collective-permute-start.2) | collective-permute-done | bytes 524320 | tf_op jit(solution)/shard_map/ppermute | solution.py:22
  62.8 2.9 select_maximum_fusion.4
  65.7 1.6 multiply_add_fusion.1
  67.4 4.1 %collective-permute-start.4 = (f32[2,8,1,32,256]{4,3,2,1,0:T(8,128)S(1)}, f32[2,8,1,32,256]{4,3,2,1,0:T(8,128)S(1)}, u32[]{:S(2)}, u32[]{:S(2)}) collective-permute-start(f32[2,8,1,32,256]{4,3,2,1,0:T(8,128)S(1)} %get-tuple-element.39), channel_id=1, source_target_pairs={{0,1},{1,2},{2,3},{3,4},{4,5},{5,6},{6,7},{7,8},{8,9},{9,10},{10,1... | collective-permute-start | bytes 1572872 | tf_op jit(solution)/shard_map/ppermute | solution.py:22
  71.5 1.5 collective-permute-start.5
  73.0 20.1 %collective-permute-done.4 = f32[2,8,1,32,256]{4,3,2,1,0:T(8,128)S(1)} collective-permute-done((f32[2,8,1,32,256]{4,3,2,1,0:T(8,128)S(1)}, f32[2,8,1,32,256]{4,3,2,1,0:T(8,128)S(1)}, u32[]{:S(2)}, u32[]{:S(2)}) %collective-permute-start.4) | collective-permute-done | bytes 524320 | tf_op jit(solution)/shard_map/ppermute | solution.py:22
  93.1 1.8 select_maximum_fusion.2
  94.9 1.2 multiply_add_fusion
  96.2 4.1 %collective-permute-start.6 = (f32[2,8,1,32,256]{4,3,2,1,0:T(8,128)S(1)}, f32[2,8,1,32,256]{4,3,2,1,0:T(8,128)S(1)}, u32[]{:S(2)}, u32[]{:S(2)}) collective-permute-start(f32[2,8,1,32,256]{4,3,2,1,0:T(8,128)S(1)} %get-tuple-element.37), channel_id=1, source_target_pairs={{0,1},{1,2},{2,3},{3,4},{4,5},{5,6},{6,7},{7,8},{8,9},{9,10},{10,1... | collective-permute-start | bytes 1572872 | tf_op jit(solution)/shard_map/ppermute | solution.py:22
  100.4 1.3 collective-permute-start.7
  101.7 19.4 %collective-permute-done.6 = f32[2,8,1,32,256]{4,3,2,1,0:T(8,128)S(1)} collective-permute-done((f32[2,8,1,32,256]{4,3,2,1,0:T(8,128)S(1)}, f32[2,8,1,32,256]{4,3,2,1,0:T(8,128)S(1)}, u32[]{:S(2)}, u32[]{:S(2)}) %collective-permute-start.6) | collective-permute-done | bytes 524320 | tf_op jit(solution)/shard_map/ppermute | solution.py:22
  121.0 1.8 select_maximum_fusion
  122.9 1.4 fusion.15
  124.3 1.8 copy.76
  126.0 7.0 %all-to-all-start.1 = ((f32[16,2,32,256]{3,1,0,2:T(2,128)}), f32[16,2,32,256]{3,1,0,2:T(2,128)S(1)}, u32[]{:S(2)}, u32[]{:S(2)}) async-start(f32[16,2,32,256]{3,1,0,2:T(2,128)} %copy.76), calls=%async_computation.1 | async-start | bytes 2097152 | tf_op jit(solution)/shard_map/all_to_all | solution.py:167
  133.0 7.9 %copy.97 = f32[32,8,16,256]{3,1,2,0:T(8,128)} copy(f32[32,8,16,256]{3,2,1,0:T(8,128)} %bitcast.66) | data formatting | bytes 8388608
  140.9 7.2 %all-to-all-done.1 = f32[16,2,32,256]{3,1,0,2:T(2,128)S(1)} async-done(((f32[16,2,32,256]{3,1,0,2:T(2,128)}), f32[16,2,32,256]{3,1,0,2:T(2,128)S(1)}, u32[]{:S(2)}, u32[]{:S(2)}) %all-to-all-start.1) | async-done | bytes 1048608 | tf_op jit(solution)/shard_map/all_to_all | solution.py:167
  148.1 0.6 copy.108
  148.7 0.1 copy.78
  148.9 0.2 reshape.66
  149.1 1.0 fusion.71
  150.1 6.1 %fusion.70 = f32[64,256]{1,0:T(8,128)S(1)} fusion(f32[64,4096]{1,0:T(8,128)S(1)} %reshape.66, f32[256,4096]{1,0:T(8,128)} %bitcast.64), kind=kOutput, calls=%fused_computation.133 | convolution fusion | flops 805306368 | bytes 5308416 | tf_op jit(solution)/shard_map/dot_general | solution.py:126
  156.3 3.5 %collective-permute-start.8 = (f32[417,128]{1,0:T(8,128)S(1)}, f32[417,128]{1,0:T(8,128)S(1)}, u32[]{:S(2)}, u32[]{:S(2)}) collective-permute-start(f32[417,128]{1,0:T(8,128)S(1)} %constant_dynamic-update-slice_fusion), channel_id=1, source_target_pairs={{0,1},{1,0},{2,3},{3,2},{4,5},{5,4},{6,7},{7,6},{8,9},{9,8},{10,11... | collective-permute-start | bytes 640520 | tf_op jit(solution)/shard_map/ppermute | solution.py:38
  159.8 4.7 %collective-permute-done.8 = f32[417,128]{1,0:T(8,128)S(1)} collective-permute-done((f32[417,128]{1,0:T(8,128)S(1)}, f32[417,128]{1,0:T(8,128)S(1)}, u32[]{:S(2)}, u32[]{:S(2)}) %collective-permute-start.8) | collective-permute-done | bytes 213536 | tf_op jit(solution)/shard_map/ppermute | solution.py:38
  164.6 7.7 %collective-permute-start.9 = (f32[417,128]{1,0:T(8,128)S(1)}, f32[417,128]{1,0:T(8,128)S(1)}, u32[]{:S(2)}, u32[]{:S(2)}) collective-permute-start(f32[417,128]{1,0:T(8,128)S(1)} %add.206), channel_id=1, source_target_pairs={{0,2},{1,3},{2,0},{3,1},{4,6},{5,7},{6,4},{7,5},{8,10},{9,11},{10,... | collective-permute-start | bytes 640520 | tf_op jit(solution)/shard_map/ppermute | solution.py:38
  172.2 3.9 %collective-permute-done.9 = f32[417,128]{1,0:T(8,128)S(1)} collective-permute-done((f32[417,128]{1,0:T(8,128)S(1)}, f32[417,128]{1,0:T(8,128)S(1)}, u32[]{:S(2)}, u32[]{:S(2)}) %collective-permute-start.9) | collective-permute-done | bytes 213536 | tf_op jit(solution)/shard_map/ppermute | solution.py:38
  176.1 5.7 %collective-permute-start.10 = (f32[417,128]{1,0:T(8,128)S(1)}, f32[417,128]{1,0:T(8,128)S(1)}, u32[]{:S(2)}, u32[]{:S(2)}) collective-permute-start(f32[417,128]{1,0:T(8,128)S(1)} %add.207), channel_id=1, source_target_pairs={{0,4},{1,5},{2,6},{3,7},{4,0},{5,1},{6,2},{7,3},{8,12},{9,13},{10,... | collective-permute-start | bytes 640520 | tf_op jit(solution)/shard_map/ppermute | solution.py:38
  181.8 9.5 %collective-permute-done.10 = f32[417,128]{1,0:T(8,128)S(1)} collective-permute-done((f32[417,128]{1,0:T(8,128)S(1)}, f32[417,128]{1,0:T(8,128)S(1)}, u32[]{:S(2)}, u32[]{:S(2)}) %collective-permute-start.10) | collective-permute-done | bytes 213536 | tf_op jit(solution)/shard_map/ppermute | solution.py:38
  191.3 12.4 %collective-permute-start.11 = (f32[417,128]{1,0:T(8,128)S(1)}, f32[417,128]{1,0:T(8,128)S(1)}, u32[]{:S(2)}, u32[]{:S(2)}) collective-permute-start(f32[417,128]{1,0:T(8,128)S(1)} %add.208), channel_id=1, source_target_pairs={{0,8},{1,9},{2,10},{3,11},{4,12},{5,13},{6,14},{7,15},{8,0},{9,1},... | collective-permute-start | bytes 640520 | tf_op jit(solution)/shard_map/ppermute | solution.py:38
  203.7 7.4 %collective-permute-done.11 = f32[417,128]{1,0:T(8,128)S(1)} collective-permute-done((f32[417,128]{1,0:T(8,128)S(1)}, f32[417,128]{1,0:T(8,128)S(1)}, u32[]{:S(2)}, u32[]{:S(2)}) %collective-permute-start.11) | collective-permute-done | bytes 213536 | tf_op jit(solution)/shard_map/ppermute | solution.py:38
  211.1 4.0 %collective-permute-start.12 = (f32[417,128]{1,0:T(8,128)S(1)}, f32[417,128]{1,0:T(8,128)S(1)}, u32[]{:S(2)}, u32[]{:S(2)}) collective-permute-start(f32[417,128]{1,0:T(8,128)S(1)} %add.209), channel_id=1, source_target_pairs={{0,16},{1,17},{2,18},{3,19},{4,20},{5,21},{6,22},{7,23},{8,24},{9,... | collective-permute-start | bytes 640520 | tf_op jit(solution)/shard_map/ppermute | solution.py:38
  215.1 3.3 %collective-permute-done.12 = f32[417,128]{1,0:T(8,128)S(1)} collective-permute-done((f32[417,128]{1,0:T(8,128)S(1)}, f32[417,128]{1,0:T(8,128)S(1)}, u32[]{:S(2)}, u32[]{:S(2)}) %collective-permute-start.12) | collective-permute-done | bytes 213536 | tf_op jit(solution)/shard_map/ppermute | solution.py:38
  218.4 4.4 %collective-permute-start.13 = (f32[417,128]{1,0:T(8,128)S(1)}, f32[417,128]{1,0:T(8,128)S(1)}, u32[]{:S(2)}, u32[]{:S(2)}) collective-permute-start(f32[417,128]{1,0:T(8,128)S(1)} %add.210), channel_id=1, source_target_pairs={{0,32},{1,33},{2,34},{3,35},{4,36},{5,37},{6,38},{7,39},{8,40},{9,... | collective-permute-start | bytes 640520 | tf_op jit(solution)/shard_map/ppermute | solution.py:38
  222.8 5.6 %collective-permute-done.13 = f32[417,128]{1,0:T(8,128)S(1)} collective-permute-done((f32[417,128]{1,0:T(8,128)S(1)}, f32[417,128]{1,0:T(8,128)S(1)}, u32[]{:S(2)}, u32[]{:S(2)}) %collective-permute-start.13) | collective-permute-done | bytes 213536 | tf_op jit(solution)/shard_map/ppermute | solution.py:38
  228.4 14.3 %collective-permute-start.14 = (f32[417,128]{1,0:T(8,128)S(1)}, f32[417,128]{1,0:T(8,128)S(1)}, u32[]{:S(2)}, u32[]{:S(2)}) collective-permute-start(f32[417,128]{1,0:T(8,128)S(1)} %add.211), channel_id=1, source_target_pairs={{0,64},{1,65},{2,66},{3,67},{4,68},{5,69},{6,70},{7,71},{8,72},{9,... | collective-permute-start | bytes 640520 | tf_op jit(solution)/shard_map/ppermute | solution.py:38
  242.7 7.1 %collective-permute-done.14 = f32[417,128]{1,0:T(8,128)S(1)} collective-permute-done((f32[417,128]{1,0:T(8,128)S(1)}, f32[417,128]{1,0:T(8,128)S(1)}, u32[]{:S(2)}, u32[]{:S(2)}) %collective-permute-start.14) | collective-permute-done | bytes 213536 | tf_op jit(solution)/shard_map/ppermute | solution.py:38
  249.9 4.1 %collective-permute-start.15 = (f32[417,128]{1,0:T(8,128)S(1)}, f32[417,128]{1,0:T(8,128)S(1)}, u32[]{:S(2)}, u32[]{:S(2)}) collective-permute-start(f32[417,128]{1,0:T(8,128)S(1)} %add.212), channel_id=1, source_target_pairs={{0,128},{1,129},{2,130},{3,131},{4,132},{5,133},{6,134},{7,135},{8... | collective-permute-start | bytes 640520 | tf_op jit(solution)/shard_map/ppermute | solution.py:38
  254.0 1.1 collective-permute-done.15
  255.1 3.8 %collective-permute-start.16 = (f32[417,128]{1,0:T(8,128)S(1)}, f32[417,128]{1,0:T(8,128)S(1)}, u32[]{:S(2)}, u32[]{:S(2)}) collective-permute-start(f32[417,128]{1,0:T(8,128)S(1)} %add.213), channel_id=1, source_target_pairs={{0,256},{1,257},{2,258},{3,259},{4,260},{5,261},{6,262},{7,263},{8... | collective-permute-start | bytes 640520 | tf_op jit(solution)/shard_map/ppermute | solution.py:38
  258.9 6.2 %collective-permute-done.16 = f32[417,128]{1,0:T(8,128)S(1)} collective-permute-done((f32[417,128]{1,0:T(8,128)S(1)}, f32[417,128]{1,0:T(8,128)S(1)}, u32[]{:S(2)}, u32[]{:S(2)}) %collective-permute-start.16) | collective-permute-done | bytes 213536 | tf_op jit(solution)/shard_map/ppermute | solution.py:38
  265.5 0.4 fusion.8
  265.9 4.8 %convolution_subtract_fusion = f32[64,4096]{1,0:T(8,128)S(1)} fusion(f32[64,4096]{1,0:T(8,128)S(1)} %reshape.66, f32[64,256]{1,0:T(8,128)S(1)} %fusion.8, f32[256,4096]{1,0:T(8,128)} %bitcast.65), kind=kOutput, calls=%fused_computation.5 | convolution fusion | flops 805568512 | bytes 6356992 | tf_op jit(solution)/shard_map/dot_general | solution.py:132
  270.7 0.4 fusion.38
  271.2 0.3 copy.98
  271.5 0.2 convolution_subtract_fusion.3
  271.7 0.2 convolution_subtract_fusion.2
  271.9 0.2 convolution_add_fusion
  272.2 5.8 %cholesky.16 = f32[64,64]{1,0:T(8,128)S(1)} custom-call(f32[64,64]{1,0:T(8,128)S(1)} %fusion.54), custom_call_target="Cholesky" | custom-call | tf_op jit(solution)/shard_map/jit(cholesky)/cholesky | solution.py:183
  278.1 0.6 compare_reduce_fusion
  278.8 1.3 select_bitcast_fusion
  280.0 4.9 %custom-call.6 = f32[1,64,64]{1,2,0:T(8,128)S(1)} custom-call(f32[1,64,64]{2,1,0:T(8,128)S(1)} %get-tuple-element.24), custom_call_target="InvertDiagBlocksLowerTriangular" | custom-call | tf_op jit(solution)/shard_map/triangular_solve | solution.py:184
  285.0 1.6 fusion.31
  286.6 1.3 copy.89
  (49 shorter events, 2.0 us)
Async XLA Ops:
  1.7 32.3 %collective-permute-start = (f32[1,32,256]{2,1,0:T(8,128)S(1)}, f32[1,32,256]{2,1,0:T(8,128)S(1)}, u32[]{:S(2)}, u32[]{:S(2)}) collective-permute-start(f32[1,32,256]{2,1,0:T(8,128)S(1)} %get-tuple-element.54), channel_id=1, source_target_pairs={{0,1},{1,2},{2,3},{3,4},{4,5},{5,6},{6,7},{7,8},{8,9},{9,10},{10,1... | collective-permute-start | bytes 98312 | tf_op jit(solution)/shard_map/ppermute | solution.py:22
  5.6 28.2 %copy-start.1 = (f32[8]{0:T(128)S(1)}, f32[8]{0:T(128)}, u32[]{:S(2)}) copy-start(f32[8]{0:T(128)} %param.8) | copy-start | bytes 100
  5.6 28.3 %collective-permute-start.1 = (f32[1,32,256]{2,1,0:T(8,128)S(1)}, f32[1,32,256]{2,1,0:T(8,128)S(1)}, u32[]{:S(2)}, u32[]{:S(2)}) collective-permute-start(f32[1,32,256]{2,1,0:T(8,128)S(1)} %get-tuple-element.55), channel_id=1, source_target_pairs={{1,0},{2,1},{3,2},{4,3},{5,4},{6,5},{7,6},{8,7},{9,8},{10,9},{11,1... | collective-permute-start | bytes 98312 | tf_op jit(solution)/shard_map/ppermute | solution.py:24
  9.2 25.1 %all-to-all-start = ((f32[64,2,8,256]{3,2,1,0:T(8,128)}), f32[64,2,8,256]{3,2,1,0:T(8,128)S(1)}, u32[]{:S(2)}, u32[]{:S(2)}) async-start(f32[64,2,8,256]{3,2,1,0:T(8,128)} %slice.161), calls=%async_computation | async-start | bytes 2097152 | tf_op jit(solution)/shard_map/all_to_all | solution.py:155
  35.7 27.1 %collective-permute-start.2 = (f32[2,8,1,32,256]{4,3,2,1,0:T(8,128)}, f32[2,8,1,32,256]{4,3,2,1,0:T(8,128)}, u32[]{:S(2)}, u32[]{:S(2)}) collective-permute-start(f32[2,8,1,32,256]{4,3,2,1,0:T(8,128)} %get-tuple-element.41), channel_id=1, source_target_pairs={{0,1},{1,2},{2,3},{3,4},{4,5},{5,6},{6,7},{7,8},{8,9},{9,10},{10,1... | collective-permute-start | bytes 1572872 | tf_op jit(solution)/shard_map/ppermute | solution.py:22
  40.8 22.0 %collective-permute-start.3 = (f32[2,8,1,32,256]{4,3,2,1,0:T(8,128)}, f32[2,8,1,32,256]{4,3,2,1,0:T(8,128)}, u32[]{:S(2)}, u32[]{:S(2)}) collective-permute-start(f32[2,8,1,32,256]{4,3,2,1,0:T(8,128)} %get-tuple-element.42), channel_id=1, source_target_pairs={{1,0},{2,1},{3,2},{4,3},{5,4},{6,5},{7,6},{8,7},{9,8},{10,9},{11,1... | collective-permute-start | bytes 1572872 | tf_op jit(solution)/shard_map/ppermute | solution.py:24
  67.4 25.7 %collective-permute-start.4 = (f32[2,8,1,32,256]{4,3,2,1,0:T(8,128)S(1)}, f32[2,8,1,32,256]{4,3,2,1,0:T(8,128)S(1)}, u32[]{:S(2)}, u32[]{:S(2)}) collective-permute-start(f32[2,8,1,32,256]{4,3,2,1,0:T(8,128)S(1)} %get-tuple-element.39), channel_id=1, source_target_pairs={{0,1},{1,2},{2,3},{3,4},{4,5},{5,6},{6,7},{7,8},{8,9},{9,10},{10,1... | collective-permute-start | bytes 1572872 | tf_op jit(solution)/shard_map/ppermute | solution.py:22
  71.5 21.6 %collective-permute-start.5 = (f32[2,8,1,32,256]{4,3,2,1,0:T(8,128)S(1)}, f32[2,8,1,32,256]{4,3,2,1,0:T(8,128)S(1)}, u32[]{:S(2)}, u32[]{:S(2)}) collective-permute-start(f32[2,8,1,32,256]{4,3,2,1,0:T(8,128)S(1)} %get-tuple-element.40), channel_id=1, source_target_pairs={{1,0},{2,1},{3,2},{4,3},{5,4},{6,5},{7,6},{8,7},{9,8},{10,9},{11,1... | collective-permute-start | bytes 1572872 | tf_op jit(solution)/shard_map/ppermute | solution.py:24
  96.2 24.8 %collective-permute-start.6 = (f32[2,8,1,32,256]{4,3,2,1,0:T(8,128)S(1)}, f32[2,8,1,32,256]{4,3,2,1,0:T(8,128)S(1)}, u32[]{:S(2)}, u32[]{:S(2)}) collective-permute-start(f32[2,8,1,32,256]{4,3,2,1,0:T(8,128)S(1)} %get-tuple-element.37), channel_id=1, source_target_pairs={{0,1},{1,2},{2,3},{3,4},{4,5},{5,6},{6,7},{7,8},{8,9},{9,10},{10,1... | collective-permute-start | bytes 1572872 | tf_op jit(solution)/shard_map/ppermute | solution.py:22
  100.4 20.7 %collective-permute-start.7 = (f32[2,8,1,32,256]{4,3,2,1,0:T(8,128)S(1)}, f32[2,8,1,32,256]{4,3,2,1,0:T(8,128)S(1)}, u32[]{:S(2)}, u32[]{:S(2)}) collective-permute-start(f32[2,8,1,32,256]{4,3,2,1,0:T(8,128)S(1)} %get-tuple-element.38), channel_id=1, source_target_pairs={{1,0},{2,1},{3,2},{4,3},{5,4},{6,5},{7,6},{8,7},{9,8},{10,9},{11,1... | collective-permute-start | bytes 1572872 | tf_op jit(solution)/shard_map/ppermute | solution.py:24
  126.0 22.1 %all-to-all-start.1 = ((f32[16,2,32,256]{3,1,0,2:T(2,128)}), f32[16,2,32,256]{3,1,0,2:T(2,128)S(1)}, u32[]{:S(2)}, u32[]{:S(2)}) async-start(f32[16,2,32,256]{3,1,0,2:T(2,128)} %copy.76), calls=%async_computation.1 | async-start | bytes 2097152 | tf_op jit(solution)/shard_map/all_to_all | solution.py:167
  156.3 8.2 %collective-permute-start.8 = (f32[417,128]{1,0:T(8,128)S(1)}, f32[417,128]{1,0:T(8,128)S(1)}, u32[]{:S(2)}, u32[]{:S(2)}) collective-permute-start(f32[417,128]{1,0:T(8,128)S(1)} %constant_dynamic-update-slice_fusion), channel_id=1, source_target_pairs={{0,1},{1,0},{2,3},{3,2},{4,5},{5,4},{6,7},{7,6},{8,9},{9,8},{10,11... | collective-permute-start | bytes 640520 | tf_op jit(solution)/shard_map/ppermute | solution.py:38
  164.6 11.6 %collective-permute-start.9 = (f32[417,128]{1,0:T(8,128)S(1)}, f32[417,128]{1,0:T(8,128)S(1)}, u32[]{:S(2)}, u32[]{:S(2)}) collective-permute-start(f32[417,128]{1,0:T(8,128)S(1)} %add.206), channel_id=1, source_target_pairs={{0,2},{1,3},{2,0},{3,1},{4,6},{5,7},{6,4},{7,5},{8,10},{9,11},{10,... | collective-permute-start | bytes 640520 | tf_op jit(solution)/shard_map/ppermute | solution.py:38
  176.1 15.2 %collective-permute-start.10 = (f32[417,128]{1,0:T(8,128)S(1)}, f32[417,128]{1,0:T(8,128)S(1)}, u32[]{:S(2)}, u32[]{:S(2)}) collective-permute-start(f32[417,128]{1,0:T(8,128)S(1)} %add.207), channel_id=1, source_target_pairs={{0,4},{1,5},{2,6},{3,7},{4,0},{5,1},{6,2},{7,3},{8,12},{9,13},{10,... | collective-permute-start | bytes 640520 | tf_op jit(solution)/shard_map/ppermute | solution.py:38
  191.3 19.8 %collective-permute-start.11 = (f32[417,128]{1,0:T(8,128)S(1)}, f32[417,128]{1,0:T(8,128)S(1)}, u32[]{:S(2)}, u32[]{:S(2)}) collective-permute-start(f32[417,128]{1,0:T(8,128)S(1)} %add.208), channel_id=1, source_target_pairs={{0,8},{1,9},{2,10},{3,11},{4,12},{5,13},{6,14},{7,15},{8,0},{9,1},... | collective-permute-start | bytes 640520 | tf_op jit(solution)/shard_map/ppermute | solution.py:38
  211.1 7.3 %collective-permute-start.12 = (f32[417,128]{1,0:T(8,128)S(1)}, f32[417,128]{1,0:T(8,128)S(1)}, u32[]{:S(2)}, u32[]{:S(2)}) collective-permute-start(f32[417,128]{1,0:T(8,128)S(1)} %add.209), channel_id=1, source_target_pairs={{0,16},{1,17},{2,18},{3,19},{4,20},{5,21},{6,22},{7,23},{8,24},{9,... | collective-permute-start | bytes 640520 | tf_op jit(solution)/shard_map/ppermute | solution.py:38
  218.4 10.0 %collective-permute-start.13 = (f32[417,128]{1,0:T(8,128)S(1)}, f32[417,128]{1,0:T(8,128)S(1)}, u32[]{:S(2)}, u32[]{:S(2)}) collective-permute-start(f32[417,128]{1,0:T(8,128)S(1)} %add.210), channel_id=1, source_target_pairs={{0,32},{1,33},{2,34},{3,35},{4,36},{5,37},{6,38},{7,39},{8,40},{9,... | collective-permute-start | bytes 640520 | tf_op jit(solution)/shard_map/ppermute | solution.py:38
  228.4 21.4 %collective-permute-start.14 = (f32[417,128]{1,0:T(8,128)S(1)}, f32[417,128]{1,0:T(8,128)S(1)}, u32[]{:S(2)}, u32[]{:S(2)}) collective-permute-start(f32[417,128]{1,0:T(8,128)S(1)} %add.211), channel_id=1, source_target_pairs={{0,64},{1,65},{2,66},{3,67},{4,68},{5,69},{6,70},{7,71},{8,72},{9,... | collective-permute-start | bytes 640520 | tf_op jit(solution)/shard_map/ppermute | solution.py:38
  249.9 5.2 %collective-permute-start.15 = (f32[417,128]{1,0:T(8,128)S(1)}, f32[417,128]{1,0:T(8,128)S(1)}, u32[]{:S(2)}, u32[]{:S(2)}) collective-permute-start(f32[417,128]{1,0:T(8,128)S(1)} %add.212), channel_id=1, source_target_pairs={{0,128},{1,129},{2,130},{3,131},{4,132},{5,133},{6,134},{7,135},{8... | collective-permute-start | bytes 640520 | tf_op jit(solution)/shard_map/ppermute | solution.py:38
  255.1 10.0 %collective-permute-start.16 = (f32[417,128]{1,0:T(8,128)S(1)}, f32[417,128]{1,0:T(8,128)S(1)}, u32[]{:S(2)}, u32[]{:S(2)}) collective-permute-start(f32[417,128]{1,0:T(8,128)S(1)} %add.213), channel_id=1, source_target_pairs={{0,256},{1,257},{2,258},{3,259},{4,260},{5,261},{6,262},{7,263},{8... | collective-permute-start | bytes 640520 | tf_op jit(solution)/shard_map/ppermute | solution.py:38
  265.9 6.0 %copy-start = (f32[64,256]{1,0:T(8,128)}, f32[64,256]{1,0:T(8,128)S(1)}, u32[]{:S(2)}) copy-start(f32[64,256]{1,0:T(8,128)S(1)} %fusion.8) | copy-start | bytes 196612
where the time goes:
time: 289 us; the launch traced here: 288 us
  waiting for transfers between devices  115 us (40%)
  starting transfers between devices  97.1 us (34%)
  matrix products  31.8 us (11%)
  other arithmetic  25.3 us (9%)
  local copies, waits for them, and re-layouts  18 us (6%)
    ppermute x9, starting transfers between devices, allsum(): lax.ppermute(value, axes, [(i, i ^ mask) for i in range(total)])  59.8 us
    ppermute x4, waiting for transfers between devices, padded_2(): lax.ppermute(tail, axis, [(i, (i + 1) % count) for i in range(ends)])  58.8 us
    ppermute x9, waiting for transfers between devices, allsum(): lax.ppermute(value, axes, [(i, i ^ mask) for i in range(total)])  48.6 us
    dot_general x6, matrix products, products(): lax.dot_general(left_side, right_side, (((1,), (1,)), ((), ())), precisio...  24.6 us
    ppermute x4, starting transfers between devices, padded_2(): lax.ppermute(tail, axis, [(i, (i + 1) % count) for i in range(ends)])  17.3 us
    unnamed x10, local copies, waits for them, and re-layouts  9.73 us
    all_to_all x1, starting transfers between devices, local(): lax.all_to_all(tail_columns, 'shift', split_axis=0, concat_axis=2, tiled=...  7.71 us
    all_to_all x1, waiting for transfers between devices, local(): lax.all_to_all(merged, 'shift', split_axis=2, concat_axis=0, tiled=True)  7.17 us
  transfers between devices with their start and end apart: 19, of which 13 were waited for; matrix products, arithmetic and copies ran while one was open for 10% of the time, Pallas kernels for 0%

commit v1 on v0

--- a/solution.py
+++ b/solution.py
@@ -97,7 +97,7 @@
     return summed[None, None] + shift_list[:, None, None, None, None] * capacity[None, None]
 
 
-def chebyshev(source, face_list, diagonal, padder, anchor):
+def chebyshev(source, face_list, diagonal, padder, tie, anchor_of):
     center = 0.5 * (UPPER_BOUND + LOWER_BOUND)
     spread = 0.5 * (UPPER_BOUND - LOWER_BOUND)
     ratio_value = center / spread
@@ -109,9 +109,11 @@
     for sweep_index in range(SWEEPS):
         solution = solution + direction
         if sweep_index + 1 < SWEEPS:
+            if sweep_index == 0:
+                tie, direction = lax.optimization_barrier((tie, direction))
             padded = padder(direction)
             if sweep_index == 0:
-                anchor, padded = lax.optimization_barrier((anchor, padded))
+                anchor, padded = lax.optimization_barrier((anchor_of(tie), padded))
             applied = diagonal * direction - neighbours(padded, face_list)
             remainder = remainder - applied
             weight_new = 1.0 / (2.0 * ratio_value - weight_old)
@@ -161,8 +163,11 @@
         return jnp.pad(widened, ((0, 0), (0, 0), (0, 0), (1, 1), (1, 1)))
 
     half = basis_count // 2
-    packed = pack_symmetric(products(flat_basis, flat_basis), half)
-    fields, packed = chebyshev(source, face_list, diagonal, padder, packed)
+
+    def gram_of(basis):
+        return pack_symmetric(products(basis, basis), half)
+
+    fields, packed = chebyshev(source, face_list, diagonal, padder, flat_basis, gram_of)
     merged = fields.reshape(per_device * COLS, slab_x, full_y, depth)
     regrouped = lax.all_to_all(merged, "shift", split_axis=2, concat_axis=0, tiled=True)
     columns = regrouped.reshape(new_count, slab_x * quarter * depth)

time: 289 us -> 282 us (0.976)
  blocking collectives: 0 us -> 21.9 us
  matrix products: 31.8 us -> 18.4 us
  waiting for transfers between devices: 115 us -> 105 us
  starting transfers between devices: 97.1 us -> 89.9 us
    all_to_all x0 -> x1, blocking collectives: none -> 21.9 us  [local(): lax.all_to_all(merged, 'shift', split_axis=2, concat_axis=0, tiled=True)]
    ppermute x4, waiting for transfers between devices: 58.8 us -> 40.3 us  [padded_2(): lax.ppermute(tail, axis, [(i, (i + 1) % count) for i in range(ends)])]
    dot_general x6, matrix products: 24.6 us -> 11.2 us  [products(): lax.dot_general(left_side, right_side, (((1,), (1,)), ((), ())), precisio...]
    ppermute x4, waiting for transfers between devices: 0.01 us -> 10.8 us  [padded_2(): lax.ppermute(head, axis, [((i + 1) % count, i) for i in range(ends)])]
    all_to_all x1 -> x0, waiting for transfers between devices: 7.17 us -> none  [local(): lax.all_to_all(merged, 'shift', split_axis=2, concat_axis=0, tiled=True)]
    all_to_all x1 -> x0, starting transfers between devices: 6.97 us -> none  [local(): lax.all_to_all(merged, 'shift', split_axis=2, concat_axis=0, tiled=True)]
    all_to_all x1, waiting for transfers between devices: 0.01 us -> 5.96 us  [local(): lax.all_to_all(tail_columns, 'shift', split_axis=0, concat_axis=2, tiled=...]
    unnamed x10 -> x14, local copies, waits for them, and re-layouts: 9.73 us -> 9.75 us
  transfers between devices with their start and end apart: 19 -> 18, of which waited for: 13 -> 14; matrix products, arithmetic and copies ran while one was open for 10% -> 6% of each run, Pallas kernels for 0% -> 0%
where the time goes in v1:
time: 282 us; the launch traced here: 281 us
  waiting for transfers between devices  105 us (37%)
  starting transfers between devices  89.9 us (32%)
  other arithmetic  26.9 us (10%)
  blocking collectives  21.9 us (8%)
  matrix products  18.4 us (7%)
  local copies, waits for them, and re-layouts  17.6 us (6%)
    ppermute x9, starting transfers between devices, allsum(): lax.ppermute(value, axes, [(i, i ^ mask) for i in range(total)])  60.1 us
    ppermute x9, waiting for transfers between devices, allsum(): lax.ppermute(value, axes, [(i, i ^ mask) for i in range(total)])  47.8 us
    ppermute x4, waiting for transfers between devices, padded_2(): lax.ppermute(tail, axis, [(i, (i + 1) % count) for i in range(ends)])  40.3 us
    all_to_all x1, blocking collectives, local(): lax.all_to_all(merged, 'shift', split_axis=2, concat_axis=0, tiled=True)  21.9 us
    ppermute x4, starting transfers between devices, padded_2(): lax.ppermute(tail, axis, [(i, (i + 1) % count) for i in range(ends)])  16.5 us
    dot_general x6, matrix products, products(): lax.dot_general(left_side, right_side, (((1,), (1,)), ((), ())), precisio...  11.2 us
    ppermute x4, waiting for transfers between devices, padded_2(): lax.ppermute(head, axis, [((i + 1) % count, i) for i in range(ends)])  10.8 us
    unnamed x14, local copies, waits for them, and re-layouts  9.75 us
  transfers between devices with their start and end apart: 18, of which 14 were waited for; matrix products, arithmetic and copies ran while one was open for 6% of the time, Pallas kernels for 0%

profile of v1, /device:TPU:1, one launch (start us, length us, event | category | flops | bytes accessed | tf_op | source)
XLA Modules:
  0.0 280.7 jit_solution(4588767790945917110)
XLA Ops:
  0.6 1.0 select_reduce_fusion.1
  1.7 3.9 %collective-permute-start = (f32[1,32,256]{2,1,0:T(8,128)S(1)}, f32[1,32,256]{2,1,0:T(8,128)S(1)}, u32[]{:S(2)}, u32[]{:S(2)}) collective-permute-start(f32[1,32,256]{2,1,0:T(8,128)S(1)} %get-tuple-element.57), channel_id=1, source_target_pairs={{0,1},{1,2},{2,3},{3,4},{4,5},{5,6},{6,7},{7,8},{8,9},{9,10},{10,1... | collective-permute-start | bytes 98312 | tf_op jit(solution)/shard_map/ppermute | solution.py:22
  5.6 1.3 collective-permute-start.1
  6.9 2.3 slice.161
  9.2 7.7 %all-to-all-start = ((f32[64,2,8,256]{3,2,1,0:T(8,128)}), f32[64,2,8,256]{3,2,1,0:T(8,128)S(1)}, u32[]{:S(2)}, u32[]{:S(2)}) async-start(f32[64,2,8,256]{3,2,1,0:T(8,128)} %slice.161), calls=%async_computation | async-start | bytes 2097152 | tf_op jit(solution)/shard_map/all_to_all | solution.py:157
  16.9 0.7 copy.65
  17.7 7.9 %copy.86 = f32[32,8,16,256]{3,1,2,0:T(8,128)} copy(f32[32,8,16,256]{3,2,1,0:T(8,128)} %bitcast.68) | data formatting | bytes 8388608
  26.0 6.0 %all-to-all-done = f32[64,2,8,256]{3,2,1,0:T(8,128)S(1)} async-done(((f32[64,2,8,256]{3,2,1,0:T(8,128)}), f32[64,2,8,256]{3,2,1,0:T(8,128)S(1)}, u32[]{:S(2)}, u32[]{:S(2)}) %all-to-all-start) | async-done | bytes 1048608 | tf_op jit(solution)/shard_map/all_to_all | solution.py:157
  32.3 1.0 fusion.58
  33.3 4.4 %collective-permute-start.2 = (f32[2,8,1,32,256]{4,3,2,1,0:T(8,128)}, f32[2,8,1,32,256]{4,3,2,1,0:T(8,128)S(1)}, u32[]{:S(2)}, u32[]{:S(2)}) collective-permute-start(f32[2,8,1,32,256]{4,3,2,1,0:T(8,128)} %get-tuple-element.47), channel_id=1, source_target_pairs={{0,1},{1,2},{2,3},{3,4},{4,5},{5,6},{6,7},{7,8},{8,9},{9,10},{10,1... | collective-permute-start | bytes 1572872 | tf_op jit(solution)/shard_map/ppermute | solution.py:22
  37.7 1.5 collective-permute-start.3
  39.2 3.5 %fusion.62 = f32[256,256]{1,0:T(8,128)S(1)} fusion(f32[256,4096]{1,0:T(8,128)S(1)} %bitcast.64), kind=kOutput, calls=%fused_computation.128 | convolution fusion | flops 3221225472 | bytes 4456448 | tf_op jit(solution)/shard_map/dot_general | solution.py:128
  42.8 0.6 fusion.59
  43.4 1.2 gather_fusion
  44.7 0.9 pad_maximum_fusion.4
  45.5 14.1 %collective-permute-done.2 = f32[2,8,1,32,256]{4,3,2,1,0:T(8,128)S(1)} collective-permute-done((f32[2,8,1,32,256]{4,3,2,1,0:T(8,128)}, f32[2,8,1,32,256]{4,3,2,1,0:T(8,128)S(1)}, u32[]{:S(2)}, u32[]{:S(2)}) %collective-permute-start.2) | collective-permute-done | bytes 524320 | tf_op jit(solution)/shard_map/ppermute | solution.py:22
  59.6 2.8 select_maximum_fusion.4
  62.4 1.7 multiply_add_fusion.1
  64.2 4.0 %collective-permute-start.4 = (f32[2,8,1,32,256]{4,3,2,1,0:T(8,128)S(1)}, f32[2,8,1,32,256]{4,3,2,1,0:T(8,128)S(1)}, u32[]{:S(2)}, u32[]{:S(2)}) collective-permute-start(f32[2,8,1,32,256]{4,3,2,1,0:T(8,128)S(1)} %get-tuple-element.45), channel_id=1, source_target_pairs={{0,1},{1,2},{2,3},{3,4},{4,5},{5,6},{6,7},{7,8},{8,9},{9,10},{10,1... | collective-permute-start | bytes 1572872 | tf_op jit(solution)/shard_map/ppermute | solution.py:22
  68.2 1.3 collective-permute-start.5
  69.5 19.3 %collective-permute-done.4 = f32[2,8,1,32,256]{4,3,2,1,0:T(8,128)S(1)} collective-permute-done((f32[2,8,1,32,256]{4,3,2,1,0:T(8,128)S(1)}, f32[2,8,1,32,256]{4,3,2,1,0:T(8,128)S(1)}, u32[]{:S(2)}, u32[]{:S(2)}) %collective-permute-start.4) | collective-permute-done | bytes 524320 | tf_op jit(solution)/shard_map/ppermute | solution.py:22
  88.8 1.8 select_maximum_fusion.2
  90.6 1.2 multiply_add_fusion
  92.0 4.1 %collective-permute-start.6 = (f32[2,8,1,32,256]{4,3,2,1,0:T(8,128)S(1)}, f32[2,8,1,32,256]{4,3,2,1,0:T(8,128)S(1)}, u32[]{:S(2)}, u32[]{:S(2)}) collective-permute-start(f32[2,8,1,32,256]{4,3,2,1,0:T(8,128)S(1)} %get-tuple-element.43), channel_id=1, source_target_pairs={{0,1},{1,2},{2,3},{3,4},{4,5},{5,6},{6,7},{7,8},{8,9},{9,10},{10,1... | collective-permute-start | bytes 1572872 | tf_op jit(solution)/shard_map/ppermute | solution.py:22
  96.1 1.5 collective-permute-start.7
  97.6 7.0 %collective-permute-done.6 = f32[2,8,1,32,256]{4,3,2,1,0:T(8,128)S(1)} collective-permute-done((f32[2,8,1,32,256]{4,3,2,1,0:T(8,128)S(1)}, f32[2,8,1,32,256]{4,3,2,1,0:T(8,128)S(1)}, u32[]{:S(2)}, u32[]{:S(2)}) %collective-permute-start.6) | collective-permute-done | bytes 524320 | tf_op jit(solution)/shard_map/ppermute | solution.py:22
  104.6 10.8 %collective-permute-done.7 = f32[2,8,1,32,256]{4,3,2,1,0:T(8,128)S(1)} collective-permute-done((f32[2,8,1,32,256]{4,3,2,1,0:T(8,128)S(1)}, f32[2,8,1,32,256]{4,3,2,1,0:T(8,128)S(1)}, u32[]{:S(2)}, u32[]{:S(2)}) %collective-permute-start.7) | collective-permute-done | bytes 524320 | tf_op jit(solution)/shard_map/ppermute | solution.py:24
  115.4 1.8 select_maximum_fusion
  117.2 1.5 fusion.10
  118.7 0.8 copy.66
  119.5 21.9 %all_to_all.30 = f32[16,2,32,256]{3,1,0,2:T(2,128)S(1)} all-to-all(f32[16,2,32,256]{3,1,0,2:T(2,128)S(1)} %copy.66), channel_id=1, replica_groups=mesh['shift'=4,'space'=128] {'shift'}, dimensions={2} | all-to-all | bytes 2097152 | tf_op jit(solution)/shard_map/all_to_all | solution.py:172
  141.4 0.6 copy.93
  142.4 1.0 fusion.64
  143.3 6.1 %fusion.63 = f32[64,256]{1,0:T(8,128)S(1)} fusion(f32[64,4096]{1,0:T(8,128)S(1)} %reshape.67, f32[256,4096]{1,0:T(8,128)} %bitcast.62), kind=kOutput, calls=%fused_computation.129 | convolution fusion | flops 805306368 | bytes 5308416 | tf_op jit(solution)/shard_map/dot_general | solution.py:128
  149.6 3.6 %collective-permute-start.8 = (f32[417,128]{1,0:T(8,128)S(1)}, f32[417,128]{1,0:T(8,128)S(1)}, u32[]{:S(2)}, u32[]{:S(2)}) collective-permute-start(f32[417,128]{1,0:T(8,128)S(1)} %constant_dynamic-update-slice_fusion), channel_id=1, source_target_pairs={{0,1},{1,0},{2,3},{3,2},{4,5},{5,4},{6,7},{7,6},{8,9},{9,8},{10,11... | collective-permute-start | bytes 640520 | tf_op jit(solution)/shard_map/ppermute | solution.py:38
  153.2 4.6 %collective-permute-done.8 = f32[417,128]{1,0:T(8,128)S(1)} collective-permute-done((f32[417,128]{1,0:T(8,128)S(1)}, f32[417,128]{1,0:T(8,128)S(1)}, u32[]{:S(2)}, u32[]{:S(2)}) %collective-permute-start.8) | collective-permute-done | bytes 213536 | tf_op jit(solution)/shard_map/ppermute | solution.py:38
  157.9 8.7 %collective-permute-start.9 = (f32[417,128]{1,0:T(8,128)S(1)}, f32[417,128]{1,0:T(8,128)S(1)}, u32[]{:S(2)}, u32[]{:S(2)}) collective-permute-start(f32[417,128]{1,0:T(8,128)S(1)} %add.206), channel_id=1, source_target_pairs={{0,2},{1,3},{2,0},{3,1},{4,6},{5,7},{6,4},{7,5},{8,10},{9,11},{10,... | collective-permute-start | bytes 640520 | tf_op jit(solution)/shard_map/ppermute | solution.py:38
  166.6 3.7 %collective-permute-done.9 = f32[417,128]{1,0:T(8,128)S(1)} collective-permute-done((f32[417,128]{1,0:T(8,128)S(1)}, f32[417,128]{1,0:T(8,128)S(1)}, u32[]{:S(2)}, u32[]{:S(2)}) %collective-permute-start.9) | collective-permute-done | bytes 213536 | tf_op jit(solution)/shard_map/ppermute | solution.py:38
  170.3 5.8 %collective-permute-start.10 = (f32[417,128]{1,0:T(8,128)S(1)}, f32[417,128]{1,0:T(8,128)S(1)}, u32[]{:S(2)}, u32[]{:S(2)}) collective-permute-start(f32[417,128]{1,0:T(8,128)S(1)} %add.207), channel_id=1, source_target_pairs={{0,4},{1,5},{2,6},{3,7},{4,0},{5,1},{6,2},{7,3},{8,12},{9,13},{10,... | collective-permute-start | bytes 640520 | tf_op jit(solution)/shard_map/ppermute | solution.py:38
  176.1 9.6 %collective-permute-done.10 = f32[417,128]{1,0:T(8,128)S(1)} collective-permute-done((f32[417,128]{1,0:T(8,128)S(1)}, f32[417,128]{1,0:T(8,128)S(1)}, u32[]{:S(2)}, u32[]{:S(2)}) %collective-permute-start.10) | collective-permute-done | bytes 213536 | tf_op jit(solution)/shard_map/ppermute | solution.py:38
  185.7 11.9 %collective-permute-start.11 = (f32[417,128]{1,0:T(8,128)S(1)}, f32[417,128]{1,0:T(8,128)S(1)}, u32[]{:S(2)}, u32[]{:S(2)}) collective-permute-start(f32[417,128]{1,0:T(8,128)S(1)} %add.208), channel_id=1, source_target_pairs={{0,8},{1,9},{2,10},{3,11},{4,12},{5,13},{6,14},{7,15},{8,0},{9,1},... | collective-permute-start | bytes 640520 | tf_op jit(solution)/shard_map/ppermute | solution.py:38
  197.6 7.1 %collective-permute-done.11 = f32[417,128]{1,0:T(8,128)S(1)} collective-permute-done((f32[417,128]{1,0:T(8,128)S(1)}, f32[417,128]{1,0:T(8,128)S(1)}, u32[]{:S(2)}, u32[]{:S(2)}) %collective-permute-start.11) | collective-permute-done | bytes 213536 | tf_op jit(solution)/shard_map/ppermute | solution.py:38
  204.7 3.1 %collective-permute-start.12 = (f32[417,128]{1,0:T(8,128)S(1)}, f32[417,128]{1,0:T(8,128)S(1)}, u32[]{:S(2)}, u32[]{:S(2)}) collective-permute-start(f32[417,128]{1,0:T(8,128)S(1)} %add.209), channel_id=1, source_target_pairs={{0,16},{1,17},{2,18},{3,19},{4,20},{5,21},{6,22},{7,23},{8,24},{9,... | collective-permute-start | bytes 640520 | tf_op jit(solution)/shard_map/ppermute | solution.py:38
  207.8 3.5 %collective-permute-done.12 = f32[417,128]{1,0:T(8,128)S(1)} collective-permute-done((f32[417,128]{1,0:T(8,128)S(1)}, f32[417,128]{1,0:T(8,128)S(1)}, u32[]{:S(2)}, u32[]{:S(2)}) %collective-permute-start.12) | collective-permute-done | bytes 213536 | tf_op jit(solution)/shard_map/ppermute | solution.py:38
  211.4 4.2 %collective-permute-start.13 = (f32[417,128]{1,0:T(8,128)S(1)}, f32[417,128]{1,0:T(8,128)S(1)}, u32[]{:S(2)}, u32[]{:S(2)}) collective-permute-start(f32[417,128]{1,0:T(8,128)S(1)} %add.210), channel_id=1, source_target_pairs={{0,32},{1,33},{2,34},{3,35},{4,36},{5,37},{6,38},{7,39},{8,40},{9,... | collective-permute-start | bytes 640520 | tf_op jit(solution)/shard_map/ppermute | solution.py:38
  215.5 5.7 %collective-permute-done.13 = f32[417,128]{1,0:T(8,128)S(1)} collective-permute-done((f32[417,128]{1,0:T(8,128)S(1)}, f32[417,128]{1,0:T(8,128)S(1)}, u32[]{:S(2)}, u32[]{:S(2)}) %collective-permute-start.13) | collective-permute-done | bytes 213536 | tf_op jit(solution)/shard_map/ppermute | solution.py:38
  221.3 14.3 %collective-permute-start.14 = (f32[417,128]{1,0:T(8,128)S(1)}, f32[417,128]{1,0:T(8,128)S(1)}, u32[]{:S(2)}, u32[]{:S(2)}) collective-permute-start(f32[417,128]{1,0:T(8,128)S(1)} %add.211), channel_id=1, source_target_pairs={{0,64},{1,65},{2,66},{3,67},{4,68},{5,69},{6,70},{7,71},{8,72},{9,... | collective-permute-start | bytes 640520 | tf_op jit(solution)/shard_map/ppermute | solution.py:38
  235.6 7.4 %collective-permute-done.14 = f32[417,128]{1,0:T(8,128)S(1)} collective-permute-done((f32[417,128]{1,0:T(8,128)S(1)}, f32[417,128]{1,0:T(8,128)S(1)}, u32[]{:S(2)}, u32[]{:S(2)}) %collective-permute-start.14) | collective-permute-done | bytes 213536 | tf_op jit(solution)/shard_map/ppermute | solution.py:38
  243.0 3.8 %collective-permute-start.15 = (f32[417,128]{1,0:T(8,128)S(1)}, f32[417,128]{1,0:T(8,128)S(1)}, u32[]{:S(2)}, u32[]{:S(2)}) collective-permute-start(f32[417,128]{1,0:T(8,128)S(1)} %add.212), channel_id=1, source_target_pairs={{0,128},{1,129},{2,130},{3,131},{4,132},{5,133},{6,134},{7,135},{8... | collective-permute-start | bytes 640520 | tf_op jit(solution)/shard_map/ppermute | solution.py:38
  246.8 1.1 collective-permute-done.15
  247.9 4.7 %collective-permute-start.16 = (f32[417,128]{1,0:T(8,128)S(1)}, f32[417,128]{1,0:T(8,128)S(1)}, u32[]{:S(2)}, u32[]{:S(2)}) collective-permute-start(f32[417,128]{1,0:T(8,128)S(1)} %add.213), channel_id=1, source_target_pairs={{0,256},{1,257},{2,258},{3,259},{4,260},{5,261},{6,262},{7,263},{8... | collective-permute-start | bytes 640520 | tf_op jit(solution)/shard_map/ppermute | solution.py:38
  252.7 5.2 %collective-permute-done.16 = f32[417,128]{1,0:T(8,128)S(1)} collective-permute-done((f32[417,128]{1,0:T(8,128)S(1)}, f32[417,128]{1,0:T(8,128)S(1)}, u32[]{:S(2)}, u32[]{:S(2)}) %collective-permute-start.16) | collective-permute-done | bytes 213536 | tf_op jit(solution)/shard_map/ppermute | solution.py:38
  258.3 0.4 fusion.3
  258.7 4.8 %convolution_subtract_fusion = f32[64,4096]{1,0:T(8,128)S(1)} fusion(f32[64,4096]{1,0:T(8,128)S(1)} %reshape.67, f32[64,256]{1,0:T(8,128)S(1)} %fusion.3, f32[256,4096]{1,0:T(8,128)} %bitcast.63), kind=kOutput, calls=%fused_computation.5 | convolution fusion | flops 805568512 | bytes 6356992 | tf_op jit(solution)/shard_map/dot_general | solution.py:134
  263.5 0.4 fusion.32
  264.0 0.3 copy.87
  264.3 0.2 convolution_subtract_fusion.3
  264.5 0.2 convolution_subtract_fusion.2
  265.1 5.8 %cholesky.16 = f32[64,64]{1,0:T(8,128)S(1)} custom-call(f32[64,64]{1,0:T(8,128)S(1)} %fusion.46), custom_call_target="Cholesky" | custom-call | tf_op jit(solution)/shard_map/jit(cholesky)/cholesky | solution.py:188
  270.9 0.6 compare_reduce_fusion
  271.6 1.3 select_bitcast_fusion
  272.9 4.9 %custom-call.6 = f32[1,64,64]{1,2,0:T(8,128)S(1)} custom-call(f32[1,64,64]{2,1,0:T(8,128)S(1)} %get-tuple-element.28), custom_call_target="InvertDiagBlocksLowerTriangular" | custom-call | tf_op jit(solution)/shard_map/triangular_solve | solution.py:189
  277.8 1.6 fusion.26
  279.5 1.3 copy.79
  (52 shorter events, 2.5 us)
Async XLA Ops:
  1.7 24.0 %collective-permute-start = (f32[1,32,256]{2,1,0:T(8,128)S(1)}, f32[1,32,256]{2,1,0:T(8,128)S(1)}, u32[]{:S(2)}, u32[]{:S(2)}) collective-permute-start(f32[1,32,256]{2,1,0:T(8,128)S(1)} %get-tuple-element.57), channel_id=1, source_target_pairs={{0,1},{1,2},{2,3},{3,4},{4,5},{5,6},{6,7},{7,8},{8,9},{9,10},{10,1... | collective-permute-start | bytes 98312 | tf_op jit(solution)/shard_map/ppermute | solution.py:22
  5.6 20.1 %collective-permute-start.1 = (f32[1,32,256]{2,1,0:T(8,128)S(1)}, f32[1,32,256]{2,1,0:T(8,128)S(1)}, u32[]{:S(2)}, u32[]{:S(2)}) collective-permute-start(f32[1,32,256]{2,1,0:T(8,128)S(1)} %get-tuple-element.58), channel_id=1, source_target_pairs={{1,0},{2,1},{3,2},{4,3},{5,4},{6,5},{7,6},{8,7},{9,8},{10,9},{11,1... | collective-permute-start | bytes 98312 | tf_op jit(solution)/shard_map/ppermute | solution.py:24
  9.2 22.8 %all-to-all-start = ((f32[64,2,8,256]{3,2,1,0:T(8,128)}), f32[64,2,8,256]{3,2,1,0:T(8,128)S(1)}, u32[]{:S(2)}, u32[]{:S(2)}) async-start(f32[64,2,8,256]{3,2,1,0:T(8,128)} %slice.161), calls=%async_computation | async-start | bytes 2097152 | tf_op jit(solution)/shard_map/all_to_all | solution.py:157
  17.7 7.9 %copy-start.3 = (f32[8]{0:T(128)S(1)}, f32[8]{0:T(128)}, u32[]{:S(2)}) copy-start(f32[8]{0:T(128)} %param.8) | copy-start | bytes 100
  32.0 7.2 %copy-start = (f32[32,8,16,256]{3,1,2,0:T(8,128)S(1)}, f32[32,8,16,256]{3,1,2,0:T(8,128)}, u32[]{:S(2)}) copy-start(f32[32,8,16,256]{3,1,2,0:T(8,128)} %copy.86) | copy-start | bytes 12582916
  33.3 26.3 %collective-permute-start.2 = (f32[2,8,1,32,256]{4,3,2,1,0:T(8,128)}, f32[2,8,1,32,256]{4,3,2,1,0:T(8,128)S(1)}, u32[]{:S(2)}, u32[]{:S(2)}) collective-permute-start(f32[2,8,1,32,256]{4,3,2,1,0:T(8,128)} %get-tuple-element.47), channel_id=1, source_target_pairs={{0,1},{1,2},{2,3},{3,4},{4,5},{5,6},{6,7},{7,8},{8,9},{9,10},{10,1... | collective-permute-start | bytes 1572872 | tf_op jit(solution)/shard_map/ppermute | solution.py:22
  37.7 5.0 %copy-start.2 = (pred[128,128]{1,0:T(8,128)(4,1)S(1)}, pred[128,128]{1,0:T(8,128)(4,1)}, u32[]{:S(2)}) copy-start(pred[128,128]{1,0:T(8,128)(4,1)} %copy.65) | copy-start | bytes 49156
  37.7 21.9 %collective-permute-start.3 = (f32[2,8,1,32,256]{4,3,2,1,0:T(8,128)}, f32[2,8,1,32,256]{4,3,2,1,0:T(8,128)}, u32[]{:S(2)}, u32[]{:S(2)}) collective-permute-start(f32[2,8,1,32,256]{4,3,2,1,0:T(8,128)} %get-tuple-element.48), channel_id=1, source_target_pairs={{1,0},{2,1},{3,2},{4,3},{5,4},{6,5},{7,6},{8,7},{9,8},{10,9},{11,1... | collective-permute-start | bytes 1572872 | tf_op jit(solution)/shard_map/ppermute | solution.py:24
  64.2 24.7 %collective-permute-start.4 = (f32[2,8,1,32,256]{4,3,2,1,0:T(8,128)S(1)}, f32[2,8,1,32,256]{4,3,2,1,0:T(8,128)S(1)}, u32[]{:S(2)}, u32[]{:S(2)}) collective-permute-start(f32[2,8,1,32,256]{4,3,2,1,0:T(8,128)S(1)} %get-tuple-element.45), channel_id=1, source_target_pairs={{0,1},{1,2},{2,3},{3,4},{4,5},{5,6},{6,7},{7,8},{8,9},{9,10},{10,1... | collective-permute-start | bytes 1572872 | tf_op jit(solution)/shard_map/ppermute | solution.py:22
  68.2 20.6 %collective-permute-start.5 = (f32[2,8,1,32,256]{4,3,2,1,0:T(8,128)S(1)}, f32[2,8,1,32,256]{4,3,2,1,0:T(8,128)S(1)}, u32[]{:S(2)}, u32[]{:S(2)}) collective-permute-start(f32[2,8,1,32,256]{4,3,2,1,0:T(8,128)S(1)} %get-tuple-element.46), channel_id=1, source_target_pairs={{1,0},{2,1},{3,2},{4,3},{5,4},{6,5},{7,6},{8,7},{9,8},{10,9},{11,1... | collective-permute-start | bytes 1572872 | tf_op jit(solution)/shard_map/ppermute | solution.py:24
  92.0 12.6 %collective-permute-start.6 = (f32[2,8,1,32,256]{4,3,2,1,0:T(8,128)S(1)}, f32[2,8,1,32,256]{4,3,2,1,0:T(8,128)S(1)}, u32[]{:S(2)}, u32[]{:S(2)}) collective-permute-start(f32[2,8,1,32,256]{4,3,2,1,0:T(8,128)S(1)} %get-tuple-element.43), channel_id=1, source_target_pairs={{0,1},{1,2},{2,3},{3,4},{4,5},{5,6},{6,7},{7,8},{8,9},{9,10},{10,1... | collective-permute-start | bytes 1572872 | tf_op jit(solution)/shard_map/ppermute | solution.py:22
  96.1 19.3 %collective-permute-start.7 = (f32[2,8,1,32,256]{4,3,2,1,0:T(8,128)S(1)}, f32[2,8,1,32,256]{4,3,2,1,0:T(8,128)S(1)}, u32[]{:S(2)}, u32[]{:S(2)}) collective-permute-start(f32[2,8,1,32,256]{4,3,2,1,0:T(8,128)S(1)} %get-tuple-element.44), channel_id=1, source_target_pairs={{1,0},{2,1},{3,2},{4,3},{5,4},{6,5},{7,6},{8,7},{9,8},{10,9},{11,1... | collective-permute-start | bytes 1572872 | tf_op jit(solution)/shard_map/ppermute | solution.py:24
  149.6 8.2 %collective-permute-start.8 = (f32[417,128]{1,0:T(8,128)S(1)}, f32[417,128]{1,0:T(8,128)S(1)}, u32[]{:S(2)}, u32[]{:S(2)}) collective-permute-start(f32[417,128]{1,0:T(8,128)S(1)} %constant_dynamic-update-slice_fusion), channel_id=1, source_target_pairs={{0,1},{1,0},{2,3},{3,2},{4,5},{5,4},{6,7},{7,6},{8,9},{9,8},{10,11... | collective-permute-start | bytes 640520 | tf_op jit(solution)/shard_map/ppermute | solution.py:38
  157.9 12.4 %collective-permute-start.9 = (f32[417,128]{1,0:T(8,128)S(1)}, f32[417,128]{1,0:T(8,128)S(1)}, u32[]{:S(2)}, u32[]{:S(2)}) collective-permute-start(f32[417,128]{1,0:T(8,128)S(1)} %add.206), channel_id=1, source_target_pairs={{0,2},{1,3},{2,0},{3,1},{4,6},{5,7},{6,4},{7,5},{8,10},{9,11},{10,... | collective-permute-start | bytes 640520 | tf_op jit(solution)/shard_map/ppermute | solution.py:38
  170.3 15.4 %collective-permute-start.10 = (f32[417,128]{1,0:T(8,128)S(1)}, f32[417,128]{1,0:T(8,128)S(1)}, u32[]{:S(2)}, u32[]{:S(2)}) collective-permute-start(f32[417,128]{1,0:T(8,128)S(1)} %add.207), channel_id=1, source_target_pairs={{0,4},{1,5},{2,6},{3,7},{4,0},{5,1},{6,2},{7,3},{8,12},{9,13},{10,... | collective-permute-start | bytes 640520 | tf_op jit(solution)/shard_map/ppermute | solution.py:38
  185.7 19.0 %collective-permute-start.11 = (f32[417,128]{1,0:T(8,128)S(1)}, f32[417,128]{1,0:T(8,128)S(1)}, u32[]{:S(2)}, u32[]{:S(2)}) collective-permute-start(f32[417,128]{1,0:T(8,128)S(1)} %add.208), channel_id=1, source_target_pairs={{0,8},{1,9},{2,10},{3,11},{4,12},{5,13},{6,14},{7,15},{8,0},{9,1},... | collective-permute-start | bytes 640520 | tf_op jit(solution)/shard_map/ppermute | solution.py:38
  204.7 6.6 %collective-permute-start.12 = (f32[417,128]{1,0:T(8,128)S(1)}, f32[417,128]{1,0:T(8,128)S(1)}, u32[]{:S(2)}, u32[]{:S(2)}) collective-permute-start(f32[417,128]{1,0:T(8,128)S(1)} %add.209), channel_id=1, source_target_pairs={{0,16},{1,17},{2,18},{3,19},{4,20},{5,21},{6,22},{7,23},{8,24},{9,... | collective-permute-start | bytes 640520 | tf_op jit(solution)/shard_map/ppermute | solution.py:38
  211.4 9.9 %collective-permute-start.13 = (f32[417,128]{1,0:T(8,128)S(1)}, f32[417,128]{1,0:T(8,128)S(1)}, u32[]{:S(2)}, u32[]{:S(2)}) collective-permute-start(f32[417,128]{1,0:T(8,128)S(1)} %add.210), channel_id=1, source_target_pairs={{0,32},{1,33},{2,34},{3,35},{4,36},{5,37},{6,38},{7,39},{8,40},{9,... | collective-permute-start | bytes 640520 | tf_op jit(solution)/shard_map/ppermute | solution.py:38
  221.3 21.7 %collective-permute-start.14 = (f32[417,128]{1,0:T(8,128)S(1)}, f32[417,128]{1,0:T(8,128)S(1)}, u32[]{:S(2)}, u32[]{:S(2)}) collective-permute-start(f32[417,128]{1,0:T(8,128)S(1)} %add.211), channel_id=1, source_target_pairs={{0,64},{1,65},{2,66},{3,67},{4,68},{5,69},{6,70},{7,71},{8,72},{9,... | collective-permute-start | bytes 640520 | tf_op jit(solution)/shard_map/ppermute | solution.py:38
  243.0 4.9 %collective-permute-start.15 = (f32[417,128]{1,0:T(8,128)S(1)}, f32[417,128]{1,0:T(8,128)S(1)}, u32[]{:S(2)}, u32[]{:S(2)}) collective-permute-start(f32[417,128]{1,0:T(8,128)S(1)} %add.212), channel_id=1, source_target_pairs={{0,128},{1,129},{2,130},{3,131},{4,132},{5,133},{6,134},{7,135},{8... | collective-permute-start | bytes 640520 | tf_op jit(solution)/shard_map/ppermute | solution.py:38
  247.9 10.0 %collective-permute-start.16 = (f32[417,128]{1,0:T(8,128)S(1)}, f32[417,128]{1,0:T(8,128)S(1)}, u32[]{:S(2)}, u32[]{:S(2)}) collective-permute-start(f32[417,128]{1,0:T(8,128)S(1)} %add.213), channel_id=1, source_target_pairs={{0,256},{1,257},{2,258},{3,259},{4,260},{5,261},{6,262},{7,263},{8... | collective-permute-start | bytes 640520 | tf_op jit(solution)/shard_map/ppermute | solution.py:38
  258.7 6.0 %copy-start.1 = (f32[64,256]{1,0:T(8,128)}, f32[64,256]{1,0:T(8,128)S(1)}, u32[]{:S(2)}) copy-start(f32[64,256]{1,0:T(8,128)S(1)} %fusion.3) | copy-start | bytes 196612

commit v2 on v1

--- a/solution.py
+++ b/solution.py
@@ -28,15 +28,39 @@
     return cells
 
 
-def allsum(value):
+def exchange(value, axes, total, mask):
+    return lax.ppermute(value, axes, [(i, i ^ mask) for i in range(total)])
+
+
+def allsum(value, split_bits=()):
     axes = ("shift", "space")
     total = lax.axis_size("shift") * lax.axis_size("space")
     if total & (total - 1):
         return lax.psum(value, axes)
-    for bit in range(total.bit_length() - 1):
-        mask = 1 << bit
-        value = value + lax.ppermute(value, axes, [(i, i ^ mask) for i in range(total)])
-    return value
+    bits = [bit for bit in range(total.bit_length() - 1) if bit not in split_bits]
+    split_bits = [bit for bit in split_bits if (1 << bit) < total]
+    rows = value.shape[0]
+    parts = 1 << len(split_bits)
+    padded_rows = -(-rows // parts) * parts
+    value = jnp.pad(value, ((0, padded_rows - rows),) + ((0, 0),) * (value.ndim - 1))
+    me = lax.axis_index("shift") * lax.axis_size("space") + lax.axis_index("space")
+    for bit in split_bits:
+        side = (me >> bit) & 1
+        halves = value.reshape((2, value.shape[0] // 2) + value.shape[1:])
+        keep = lax.dynamic_index_in_dim(halves, side, 0, keepdims=False)
+        give = lax.dynamic_index_in_dim(halves, 1 - side, 0, keepdims=False)
+        value = keep + exchange(give, axes, total, 1 << bit)
+    for bit in bits:
+        value = value + exchange(value, axes, total, 1 << bit)
+    for bit in reversed(split_bits):
+        side = (me >> bit) & 1
+        other = exchange(value, axes, total, 1 << bit)
+        value = jnp.where(
+            side == 0,
+            jnp.concatenate([value, other], axis=0),
+            jnp.concatenate([other, value], axis=0),
+        )
+    return value[:rows]
 
 
 def pack_symmetric(full, half):
@@ -172,7 +196,7 @@
     regrouped = lax.all_to_all(merged, "shift", split_axis=2, concat_axis=0, tiled=True)
     columns = regrouped.reshape(new_count, slab_x * quarter * depth)
     own = jnp.concatenate([products(columns, flat_basis), products(columns, columns)], axis=1)
-    total = allsum(jnp.concatenate([own.reshape(-1, half), packed], axis=0)) * cell_weight
+    total = allsum(jnp.concatenate([own.reshape(-1, half), packed], axis=0), (3, 6)) * cell_weight
     sums = total[: own.size // half].reshape(own.shape)
     basis_gram = unpack_symmetric(total[own.size // half :], half)
     first_proj = sums[:, :basis_count]

time: 282 us -> 272 us (0.965)
  blocking collectives: 21.9 us -> 0 us
  starting transfers between devices: 89.9 us -> 98.7 us
    all_to_all x1 -> x0, blocking collectives: 21.9 us -> none  [local(): lax.all_to_all(merged, 'shift', split_axis=2, concat_axis=0, tiled=True)]
    all_to_all x0 -> x1, waiting for transfers between devices: none -> 15.1 us  [local(): lax.all_to_all(merged, 'shift', split_axis=2, concat_axis=0, tiled=True)]
    ppermute x4, waiting for transfers between devices: 40.3 us -> 54.7 us  [padded_2(): lax.ppermute(tail, axis, [(i, (i + 1) % count) for i in range(ends)])]
    ppermute x9 -> x11, waiting for transfers between devices: 47.8 us -> 33.6 us  [exchange(): return lax.ppermute(value, axes, [(i, i ^ mask) for i in range(total)])]
    ppermute x4, waiting for transfers between devices: 10.8 us -> 0.01 us  [padded_2(): lax.ppermute(head, axis, [((i + 1) % count, i) for i in range(ends)])]
    all_to_all x0 -> x1, starting transfers between devices: none -> 6.93 us  [local(): lax.all_to_all(merged, 'shift', split_axis=2, concat_axis=0, tiled=True)]
    ppermute x4, starting transfers between devices: 16.5 us -> 11.5 us  [padded_2(): lax.ppermute(tail, axis, [(i, (i + 1) % count) for i in range(ends)])]
    ppermute x9 -> x11, starting transfers between devices: 60.1 us -> 64.4 us  [exchange(): return lax.ppermute(value, axes, [(i, i ^ mask) for i in range(total)])]
  transfers between devices with their start and end apart: 18 -> 21, of which waited for: 14 -> 17; matrix products, arithmetic and copies ran while one was open for 6% -> 6% of each run, Pallas kernels for 0% -> 0%
where the time goes in v2:
time: 272 us; the launch traced here: 268 us
  waiting for transfers between devices  106 us (39%)
  starting transfers between devices  98.7 us (36%)
  other arithmetic  26.2 us (10%)
  local copies, waits for them, and re-layouts  18.5 us (7%)
  matrix products  18.2 us (7%)
    ppermute x11, starting transfers between devices, exchange(): return lax.ppermute(value, axes, [(i, i ^ mask) for i in range(total)])  64.4 us
    ppermute x4, waiting for transfers between devices, padded_2(): lax.ppermute(tail, axis, [(i, (i + 1) % count) for i in range(ends)])  54.7 us
    ppermute x11, waiting for transfers between devices, exchange(): return lax.ppermute(value, axes, [(i, i ^ mask) for i in range(total)])  33.6 us
    all_to_all x1, waiting for transfers between devices, local(): lax.all_to_all(merged, 'shift', split_axis=2, concat_axis=0, tiled=True)  15.1 us
    ppermute x4, starting transfers between devices, padded_2(): lax.ppermute(tail, axis, [(i, (i + 1) % count) for i in range(ends)])  11.5 us
    dot_general x6, matrix products, products(): lax.dot_general(left_side, right_side, (((1,), (1,)), ((), ())), precisio...  11.3 us
    all_to_all x1, starting transfers between devices, local(): lax.all_to_all(tail_columns, 'shift', split_axis=0, concat_axis=2, tiled=...  10.4 us
    unnamed x16, local copies, waits for them, and re-layouts  9.65 us
  transfers between devices with their start and end apart: 21, of which 17 were waited for; matrix products, arithmetic and copies ran while one was open for 6% of the time, Pallas kernels for 0%

profile of v2, /device:TPU:1, one launch (start us, length us, event | category | flops | bytes accessed | tf_op | source)
XLA Modules:
  0.0 268.5 jit_solution(16406364902230904183)
XLA Ops:
  0.7 2.3 slice.164
  3.0 10.4 %all-to-all-start = ((f32[64,2,8,256]{3,2,1,0:T(8,128)}), f32[64,2,8,256]{3,2,1,0:T(8,128)S(1)}, u32[]{:S(2)}, u32[]{:S(2)}) async-start(f32[64,2,8,256]{3,2,1,0:T(8,128)} %slice.164), calls=%async_computation | async-start | bytes 2097152 | tf_op jit(solution)/shard_map/all_to_all | solution.py:181
  13.5 1.3 collective-permute-start
  14.8 1.3 collective-permute-start.1
  16.1 7.9 %copy.92 = f32[32,8,16,256]{3,1,2,0:T(8,128)} copy(f32[32,8,16,256]{3,2,1,0:T(8,128)} %bitcast.73) | data formatting | bytes 8388608
  24.2 2.3 collective-permute-done
  26.8 2.3 all-to-all-done
  29.4 1.1 fusion.60
  30.4 2.0 collective-permute-start.2
  32.4 1.5 collective-permute-start.3
  33.9 3.5 %fusion.64 = f32[256,256]{1,0:T(8,128)S(1)} fusion(f32[256,4096]{1,0:T(8,128)S(1)} %bitcast.69), kind=kOutput, calls=%fused_computation.137 | convolution fusion | flops 3221225472 | bytes 4456448 | tf_op jit(solution)/shard_map/dot_general | solution.py:152
  37.5 0.7 fusion.62
  38.1 1.2 gather_fusion
  39.4 0.9 pad_maximum_fusion.6
  40.3 14.3 %collective-permute-done.2 = f32[2,8,1,32,256]{4,3,2,1,0:T(8,128)S(1)} collective-permute-done((f32[2,8,1,32,256]{4,3,2,1,0:T(8,128)}, f32[2,8,1,32,256]{4,3,2,1,0:T(8,128)S(1)}, u32[]{:S(2)}, u32[]{:S(2)}) %collective-permute-start.2) | collective-permute-done | bytes 524320 | tf_op jit(solution)/shard_map/ppermute | solution.py:22
  54.6 2.8 %select_maximum_fusion.4 = f32[2,8,4,34,258]{4,3,2,1,0:T(8,128)S(1)} fusion(f32[2,8,1,32,256]{4,3,2,1,0:T(8,128)} %collective-permute-done.3, f32[2,8,2,32,256]{4,3,2,1,0:T(8,128)S(1)} %multiply_multiply_fusion, f32[2,8,1,32,256]{4,3,2,1,0:T(8,128)S(1)} %collective-permute-done.2), kind=kLoop, calls=%fused_computation.10 | loop fusion | flops 8421120 | bytes 4342784 | tf_op jit(solution)/shard_map/concatenate | solution.py:20
  57.4 1.7 multiply_add_fusion.1
  59.2 4.0 %collective-permute-start.4 = (f32[2,8,1,32,256]{4,3,2,1,0:T(8,128)S(1)}, f32[2,8,1,32,256]{4,3,2,1,0:T(8,128)S(1)}, u32[]{:S(2)}, u32[]{:S(2)}) collective-permute-start(f32[2,8,1,32,256]{4,3,2,1,0:T(8,128)S(1)} %get-tuple-element.45), channel_id=1, source_target_pairs={{0,1},{1,2},{2,3},{3,4},{4,5},{5,6},{6,7},{7,8},{8,9},{9,10},{10,1... | collective-permute-start | bytes 1572872 | tf_op jit(solution)/shard_map/ppermute | solution.py:22
  63.2 1.3 collective-permute-start.5
  64.5 19.6 %collective-permute-done.4 = f32[2,8,1,32,256]{4,3,2,1,0:T(8,128)S(1)} collective-permute-done((f32[2,8,1,32,256]{4,3,2,1,0:T(8,128)S(1)}, f32[2,8,1,32,256]{4,3,2,1,0:T(8,128)S(1)}, u32[]{:S(2)}, u32[]{:S(2)}) %collective-permute-start.4) | collective-permute-done | bytes 524320 | tf_op jit(solution)/shard_map/ppermute | solution.py:22
  84.1 1.8 select_maximum_fusion.2
  86.0 1.3 multiply_add_fusion
  87.3 4.1 %collective-permute-start.6 = (f32[2,8,1,32,256]{4,3,2,1,0:T(8,128)S(1)}, f32[2,8,1,32,256]{4,3,2,1,0:T(8,128)S(1)}, u32[]{:S(2)}, u32[]{:S(2)}) collective-permute-start(f32[2,8,1,32,256]{4,3,2,1,0:T(8,128)S(1)} %get-tuple-element.43), channel_id=1, source_target_pairs={{0,1},{1,2},{2,3},{3,4},{4,5},{5,6},{6,7},{7,8},{8,9},{9,10},{10,1... | collective-permute-start | bytes 1572872 | tf_op jit(solution)/shard_map/ppermute | solution.py:22
  91.5 1.5 collective-permute-start.7
  93.0 18.4 %collective-permute-done.6 = f32[2,8,1,32,256]{4,3,2,1,0:T(8,128)S(1)} collective-permute-done((f32[2,8,1,32,256]{4,3,2,1,0:T(8,128)S(1)}, f32[2,8,1,32,256]{4,3,2,1,0:T(8,128)S(1)}, u32[]{:S(2)}, u32[]{:S(2)}) %collective-permute-start.6) | collective-permute-done | bytes 524320 | tf_op jit(solution)/shard_map/ppermute | solution.py:22
  111.3 1.8 select_maximum_fusion
  113.2 1.5 fusion.10
  114.7 1.8 copy.70
  116.4 6.9 %all-to-all-start.1 = ((f32[16,2,32,256]{3,1,0,2:T(2,128)}), f32[16,2,32,256]{3,1,0,2:T(2,128)S(1)}, u32[]{:S(2)}, u32[]{:S(2)}) async-start(f32[16,2,32,256]{3,1,0,2:T(2,128)} %copy.70), calls=%async_computation.1 | async-start | bytes 2097152 | tf_op jit(solution)/shard_map/all_to_all | solution.py:196
  123.4 15.1 %all-to-all-done.1 = f32[16,2,32,256]{3,1,0,2:T(2,128)S(1)} async-done(((f32[16,2,32,256]{3,1,0,2:T(2,128)}), f32[16,2,32,256]{3,1,0,2:T(2,128)S(1)}, u32[]{:S(2)}, u32[]{:S(2)}) %all-to-all-start.1) | async-done | bytes 1048608 | tf_op jit(solution)/shard_map/all_to_all | solution.py:196
  138.5 0.6 copy.99
  139.4 6.1 %fusion.65 = f32[64,256]{1,0:T(8,128)S(1)} fusion(f32[64,4096]{1,0:T(8,128)S(1)} %reshape.73, f32[256,4096]{1,0:T(8,128)} %bitcast.67), kind=kOutput, calls=%fused_computation.138 | convolution fusion | flops 805306368 | bytes 5308416 | tf_op jit(solution)/shard_map/dot_general | solution.py:152
  145.6 1.0 fusion.66
  146.7 17.9 %collective-permute-start.8 = (f32[210,128]{1,0:T(8,128)S(1)}, f32[210,128]{1,0:T(8,128)S(1)}, u32[]{:S(2)}, u32[]{:S(2)}) collective-permute-start(f32[210,128]{1,0:T(8,128)S(1)} %dynamic-slice_bitcast_fusion), channel_id=1, source_target_pairs={{0,8},{1,9},{2,10},{3,11},{4,12},{5,13},{6,14},{7,15},{8,0},{9,1},... | collective-permute-start | bytes 322568 | tf_op jit(solution)/shard_map/ppermute | solution.py:32
  164.7 3.7 %collective-permute-done.8 = f32[210,128]{1,0:T(8,128)S(1)} collective-permute-done((f32[210,128]{1,0:T(8,128)S(1)}, f32[210,128]{1,0:T(8,128)S(1)}, u32[]{:S(2)}, u32[]{:S(2)}) %collective-permute-start.8) | collective-permute-done | bytes 107552 | tf_op jit(solution)/shard_map/ppermute | solution.py:32
  168.5 5.8 %collective-permute-start.9 = (f32[105,128]{0,1:T(8,128)S(1)}, f32[105,128]{0,1:T(8,128)S(1)}, u32[]{:S(2)}, u32[]{:S(2)}) collective-permute-start(f32[105,128]{0,1:T(8,128)S(1)} %bitcast.79), channel_id=1, source_target_pairs={{0,64},{1,65},{2,66},{3,67},{4,68},{5,69},{6,70},{7,71},{8,72},{9,... | collective-permute-start | bytes 161288 | tf_op jit(solution)/shard_map/ppermute | solution.py:32
  174.5 3.0 %collective-permute-done.9 = f32[105,128]{0,1:T(8,128)S(1)} collective-permute-done((f32[105,128]{0,1:T(8,128)S(1)}, f32[105,128]{0,1:T(8,128)S(1)}, u32[]{:S(2)}, u32[]{:S(2)}) %collective-permute-start.9) | collective-permute-done | bytes 53792 | tf_op jit(solution)/shard_map/ppermute | solution.py:32
  177.5 1.9 collective-permute-start.10
  179.4 3.1 %collective-permute-done.10 = f32[105,128]{0,1:T(8,128)S(1)} collective-permute-done((f32[105,128]{0,1:T(8,128)S(1)}, f32[105,128]{0,1:T(8,128)S(1)}, u32[]{:S(2)}, u32[]{:S(2)}) %collective-permute-start.10) | collective-permute-done | bytes 53792 | tf_op jit(solution)/shard_map/ppermute | solution.py:32
  182.5 1.9 collective-permute-start.11
  184.4 3.1 %collective-permute-done.11 = f32[105,128]{0,1:T(8,128)S(1)} collective-permute-done((f32[105,128]{0,1:T(8,128)S(1)}, f32[105,128]{0,1:T(8,128)S(1)}, u32[]{:S(2)}, u32[]{:S(2)}) %collective-permute-start.11) | collective-permute-done | bytes 53792 | tf_op jit(solution)/shard_map/ppermute | solution.py:32
  187.5 1.9 collective-permute-start.12
  189.4 4.4 %collective-permute-done.12 = f32[105,128]{0,1:T(8,128)S(1)} collective-permute-done((f32[105,128]{0,1:T(8,128)S(1)}, f32[105,128]{0,1:T(8,128)S(1)}, u32[]{:S(2)}, u32[]{:S(2)}) %collective-permute-start.12) | collective-permute-done | bytes 53792 | tf_op jit(solution)/shard_map/ppermute | solution.py:32
  193.9 5.8 %collective-permute-start.13 = (f32[105,128]{0,1:T(8,128)S(1)}, f32[105,128]{0,1:T(8,128)S(1)}, u32[]{:S(2)}, u32[]{:S(2)}) collective-permute-start(f32[105,128]{0,1:T(8,128)S(1)} %add.236), channel_id=1, source_target_pairs={{0,16},{1,17},{2,18},{3,19},{4,20},{5,21},{6,22},{7,23},{8,24},{9,... | collective-permute-start | bytes 161288 | tf_op jit(solution)/shard_map/ppermute | solution.py:32
  199.7 1.6 collective-permute-done.13
  201.3 4.1 %collective-permute-start.14 = (f32[105,128]{0,1:T(8,128)S(1)}, f32[105,128]{0,1:T(8,128)S(1)}, u32[]{:S(2)}, u32[]{:S(2)}) collective-permute-start(f32[105,128]{0,1:T(8,128)S(1)} %add.237), channel_id=1, source_target_pairs={{0,32},{1,33},{2,34},{3,35},{4,36},{5,37},{6,38},{7,39},{8,40},{9,... | collective-permute-start | bytes 161288 | tf_op jit(solution)/shard_map/ppermute | solution.py:32
  205.4 1.9 collective-permute-done.14
  207.3 10.3 %collective-permute-start.15 = (f32[105,128]{0,1:T(8,128)S(1)}, f32[105,128]{0,1:T(8,128)S(1)}, u32[]{:S(2)}, u32[]{:S(2)}) collective-permute-start(f32[105,128]{0,1:T(8,128)S(1)} %add.238), channel_id=1, source_target_pairs={{0,128},{1,129},{2,130},{3,131},{4,132},{5,133},{6,134},{7,135},{8... | collective-permute-start | bytes 161288 | tf_op jit(solution)/shard_map/ppermute | solution.py:32
  217.6 0.9 collective-permute-done.15
  218.5 2.4 collective-permute-start.16
  220.9 4.1 %collective-permute-done.16 = f32[105,128]{0,1:T(8,128)S(1)} collective-permute-done((f32[105,128]{0,1:T(8,128)S(1)}, f32[105,128]{0,1:T(8,128)S(1)}, u32[]{:S(2)}, u32[]{:S(2)}) %collective-permute-start.16) | collective-permute-done | bytes 53792 | tf_op jit(solution)/shard_map/ppermute | solution.py:32
  225.0 6.8 %collective-permute-start.17 = (f32[105,128]{0,1:T(8,128)S(1)}, f32[105,128]{0,1:T(8,128)S(1)}, u32[]{:S(2)}, u32[]{:S(2)}) collective-permute-start(f32[105,128]{0,1:T(8,128)S(1)} %add.240), channel_id=1, source_target_pairs={{0,64},{1,65},{2,66},{3,67},{4,68},{5,69},{6,70},{7,71},{8,72},{9,... | collective-permute-start | bytes 161288 | tf_op jit(solution)/shard_map/ppermute | solution.py:32
  231.8 2.2 collective-permute-done.17
  234.2 5.5 %collective-permute-start.18 = (f32[210,128]{0,1:T(8,128)S(1)}, f32[210,128]{0,1:T(8,128)S(1)}, u32[]{:S(2)}, u32[]{:S(2)}) collective-permute-start(f32[210,128]{0,1:T(8,128)S(1)} %maximum_select_fusion), channel_id=1, source_target_pairs={{0,8},{1,9},{2,10},{3,11},{4,12},{5,13},{6,14},{7,15},{8,0},{9,1},... | collective-permute-start | bytes 322568 | tf_op jit(solution)/shard_map/ppermute | solution.py:32
  239.8 5.6 %collective-permute-done.18 = f32[210,128]{0,1:T(8,128)S(1)} collective-permute-done((f32[210,128]{0,1:T(8,128)S(1)}, f32[210,128]{0,1:T(8,128)S(1)}, u32[]{:S(2)}, u32[]{:S(2)}) %collective-permute-start.18) | collective-permute-done | bytes 107552 | tf_op jit(solution)/shard_map/ppermute | solution.py:32
  246.3 0.2 fusion.3
  246.8 4.8 %convolution_subtract_fusion = f32[64,4096]{1,0:T(8,128)S(1)} fusion(f32[64,4096]{1,0:T(8,128)S(1)} %reshape.73, f32[64,256]{1,0:T(8,128)S(1)} %fusion.3, f32[256,4096]{1,0:T(8,128)} %bitcast.68), kind=kOutput, calls=%fused_computation.5 | convolution fusion | flops 805568512 | bytes 6356992 | tf_op jit(solution)/shard_map/dot_general | solution.py:158
  252.4 5.8 %cholesky.16 = f32[64,64]{1,0:T(8,128)S(1)} custom-call(f32[64,64]{1,0:T(8,128)S(1)} %fusion.48), custom_call_target="Cholesky" | custom-call | tf_op jit(solution)/shard_map/jit(cholesky)/cholesky | solution.py:212
  258.3 0.6 compare_reduce_fusion
  259.0 1.3 select_bitcast_fusion
  260.2 4.9 %custom-call.6 = f32[1,64,64]{1,2,0:T(8,128)S(1)} custom-call(f32[1,64,64]{2,1,0:T(8,128)S(1)} %get-tuple-element.28), custom_call_target="InvertDiagBlocksLowerTriangular" | custom-call | tf_op jit(solution)/shard_map/triangular_solve | solution.py:213
  265.2 0.3 copy.93
  265.6 1.6 fusion.26
  267.2 1.3 copy.86
  (67 shorter events, 4.0 us)
Async XLA Ops:
  0.6 12.7 %copy-start.2 = (s32[2,32,256]{2,1,0:T(8,128)S(1)}, s32[2,32,256]{2,1,0:T(8,128)}, u32[]{:S(2)}) copy-start(s32[2,32,256]{2,1,0:T(8,128)} %param.5) | copy-start | bytes 196612
  0.6 12.7 %copy-start.3 = (f32[8]{0:T(128)S(1)}, f32[8]{0:T(128)}, u32[]{:S(2)}) copy-start(f32[8]{0:T(128)} %param.6) | copy-start | bytes 100
  0.7 12.7 %copy-start.4 = (f32[8]{0:T(128)S(1)}, f32[8]{0:T(128)}, u32[]{:S(2)}) copy-start(f32[8]{0:T(128)} %param.7) | copy-start | bytes 100
  3.0 26.2 %all-to-all-start = ((f32[64,2,8,256]{3,2,1,0:T(8,128)}), f32[64,2,8,256]{3,2,1,0:T(8,128)S(1)}, u32[]{:S(2)}, u32[]{:S(2)}) async-start(f32[64,2,8,256]{3,2,1,0:T(8,128)} %slice.164), calls=%async_computation | async-start | bytes 2097152 | tf_op jit(solution)/shard_map/all_to_all | solution.py:181
  13.5 13.0 %collective-permute-start = (f32[1,32,256]{2,1,0:T(8,128)S(1)}, f32[1,32,256]{2,1,0:T(8,128)S(1)}, u32[]{:S(2)}, u32[]{:S(2)}) collective-permute-start(f32[1,32,256]{2,1,0:T(8,128)S(1)} %get-tuple-element.59), channel_id=1, source_target_pairs={{0,1},{1,2},{2,3},{3,4},{4,5},{5,6},{6,7},{7,8},{8,9},{9,10},{10,1... | collective-permute-start | bytes 98312 | tf_op jit(solution)/shard_map/ppermute | solution.py:22
  14.8 11.7 %collective-permute-start.1 = (f32[1,32,256]{2,1,0:T(8,128)S(1)}, f32[1,32,256]{2,1,0:T(8,128)S(1)}, u32[]{:S(2)}, u32[]{:S(2)}) collective-permute-start(f32[1,32,256]{2,1,0:T(8,128)S(1)} %get-tuple-element.60), channel_id=1, source_target_pairs={{1,0},{2,1},{3,2},{4,3},{5,4},{6,5},{7,6},{8,7},{9,8},{10,9},{11,1... | collective-permute-start | bytes 98312 | tf_op jit(solution)/shard_map/ppermute | solution.py:24
  16.1 7.9 %copy-start.5 = (f32[8]{0:T(128)S(1)}, f32[8]{0:T(128)}, u32[]{:S(2)}) copy-start(f32[8]{0:T(128)} %param.8) | copy-start | bytes 100
  29.1 4.8 %copy-start = (f32[32,8,16,256]{3,1,2,0:T(8,128)S(1)}, f32[32,8,16,256]{3,1,2,0:T(8,128)}, u32[]{:S(2)}) copy-start(f32[32,8,16,256]{3,1,2,0:T(8,128)} %copy.92) | copy-start | bytes 12582916
  30.4 24.2 %collective-permute-start.2 = (f32[2,8,1,32,256]{4,3,2,1,0:T(8,128)}, f32[2,8,1,32,256]{4,3,2,1,0:T(8,128)S(1)}, u32[]{:S(2)}, u32[]{:S(2)}) collective-permute-start(f32[2,8,1,32,256]{4,3,2,1,0:T(8,128)} %get-tuple-element.47), channel_id=1, source_target_pairs={{0,1},{1,2},{2,3},{3,4},{4,5},{5,6},{6,7},{7,8},{8,9},{9,10},{10,1... | collective-permute-start | bytes 1572872 | tf_op jit(solution)/shard_map/ppermute | solution.py:22
  32.4 22.2 %collective-permute-start.3 = (f32[2,8,1,32,256]{4,3,2,1,0:T(8,128)}, f32[2,8,1,32,256]{4,3,2,1,0:T(8,128)}, u32[]{:S(2)}, u32[]{:S(2)}) collective-permute-start(f32[2,8,1,32,256]{4,3,2,1,0:T(8,128)} %get-tuple-element.48), channel_id=1, source_target_pairs={{1,0},{2,1},{3,2},{4,3},{5,4},{6,5},{7,6},{8,7},{9,8},{10,9},{11,1... | collective-permute-start | bytes 1572872 | tf_op jit(solution)/shard_map/ppermute | solution.py:24
  59.2 25.0 %collective-permute-start.4 = (f32[2,8,1,32,256]{4,3,2,1,0:T(8,128)S(1)}, f32[2,8,1,32,256]{4,3,2,1,0:T(8,128)S(1)}, u32[]{:S(2)}, u32[]{:S(2)}) collective-permute-start(f32[2,8,1,32,256]{4,3,2,1,0:T(8,128)S(1)} %get-tuple-element.45), channel_id=1, source_target_pairs={{0,1},{1,2},{2,3},{3,4},{4,5},{5,6},{6,7},{7,8},{8,9},{9,10},{10,1... | collective-permute-start | bytes 1572872 | tf_op jit(solution)/shard_map/ppermute | solution.py:22
  63.2 20.9 %collective-permute-start.5 = (f32[2,8,1,32,256]{4,3,2,1,0:T(8,128)S(1)}, f32[2,8,1,32,256]{4,3,2,1,0:T(8,128)S(1)}, u32[]{:S(2)}, u32[]{:S(2)}) collective-permute-start(f32[2,8,1,32,256]{4,3,2,1,0:T(8,128)S(1)} %get-tuple-element.46), channel_id=1, source_target_pairs={{1,0},{2,1},{3,2},{4,3},{5,4},{6,5},{7,6},{8,7},{9,8},{10,9},{11,1... | collective-permute-start | bytes 1572872 | tf_op jit(solution)/shard_map/ppermute | solution.py:24
  87.3 24.0 %collective-permute-start.6 = (f32[2,8,1,32,256]{4,3,2,1,0:T(8,128)S(1)}, f32[2,8,1,32,256]{4,3,2,1,0:T(8,128)S(1)}, u32[]{:S(2)}, u32[]{:S(2)}) collective-permute-start(f32[2,8,1,32,256]{4,3,2,1,0:T(8,128)S(1)} %get-tuple-element.43), channel_id=1, source_target_pairs={{0,1},{1,2},{2,3},{3,4},{4,5},{5,6},{6,7},{7,8},{8,9},{9,10},{10,1... | collective-permute-start | bytes 1572872 | tf_op jit(solution)/shard_map/ppermute | solution.py:22
  91.5 19.9 %collective-permute-start.7 = (f32[2,8,1,32,256]{4,3,2,1,0:T(8,128)S(1)}, f32[2,8,1,32,256]{4,3,2,1,0:T(8,128)S(1)}, u32[]{:S(2)}, u32[]{:S(2)}) collective-permute-start(f32[2,8,1,32,256]{4,3,2,1,0:T(8,128)S(1)} %get-tuple-element.44), channel_id=1, source_target_pairs={{1,0},{2,1},{3,2},{4,3},{5,4},{6,5},{7,6},{8,7},{9,8},{10,9},{11,1... | collective-permute-start | bytes 1572872 | tf_op jit(solution)/shard_map/ppermute | solution.py:24
  116.4 22.0 %all-to-all-start.1 = ((f32[16,2,32,256]{3,1,0,2:T(2,128)}), f32[16,2,32,256]{3,1,0,2:T(2,128)S(1)}, u32[]{:S(2)}, u32[]{:S(2)}) async-start(f32[16,2,32,256]{3,1,0,2:T(2,128)} %copy.70), calls=%async_computation.1 | async-start | bytes 2097152 | tf_op jit(solution)/shard_map/all_to_all | solution.py:196
  146.7 21.6 %collective-permute-start.8 = (f32[210,128]{1,0:T(8,128)S(1)}, f32[210,128]{1,0:T(8,128)S(1)}, u32[]{:S(2)}, u32[]{:S(2)}) collective-permute-start(f32[210,128]{1,0:T(8,128)S(1)} %dynamic-slice_bitcast_fusion), channel_id=1, source_target_pairs={{0,8},{1,9},{2,10},{3,11},{4,12},{5,13},{6,14},{7,15},{8,0},{9,1},... | collective-permute-start | bytes 322568 | tf_op jit(solution)/shard_map/ppermute | solution.py:32
  168.5 8.9 %collective-permute-start.9 = (f32[105,128]{0,1:T(8,128)S(1)}, f32[105,128]{0,1:T(8,128)S(1)}, u32[]{:S(2)}, u32[]{:S(2)}) collective-permute-start(f32[105,128]{0,1:T(8,128)S(1)} %bitcast.79), channel_id=1, source_target_pairs={{0,64},{1,65},{2,66},{3,67},{4,68},{5,69},{6,70},{7,71},{8,72},{9,... | collective-permute-start | bytes 161288 | tf_op jit(solution)/shard_map/ppermute | solution.py:32
  177.5 5.0 %collective-permute-start.10 = (f32[105,128]{0,1:T(8,128)S(1)}, f32[105,128]{0,1:T(8,128)S(1)}, u32[]{:S(2)}, u32[]{:S(2)}) collective-permute-start(f32[105,128]{0,1:T(8,128)S(1)} %bitcast_add_fusion.1), channel_id=1, source_target_pairs={{0,1},{1,0},{2,3},{3,2},{4,5},{5,4},{6,7},{7,6},{8,9},{9,8},{10,11... | collective-permute-start | bytes 161288 | tf_op jit(solution)/shard_map/ppermute | solution.py:32
  182.5 5.0 %collective-permute-start.11 = (f32[105,128]{0,1:T(8,128)S(1)}, f32[105,128]{0,1:T(8,128)S(1)}, u32[]{:S(2)}, u32[]{:S(2)}) collective-permute-start(f32[105,128]{0,1:T(8,128)S(1)} %add.234), channel_id=1, source_target_pairs={{0,2},{1,3},{2,0},{3,1},{4,6},{5,7},{6,4},{7,5},{8,10},{9,11},{10,... | collective-permute-start | bytes 161288 | tf_op jit(solution)/shard_map/ppermute | solution.py:32
  187.5 6.3 %collective-permute-start.12 = (f32[105,128]{0,1:T(8,128)S(1)}, f32[105,128]{0,1:T(8,128)S(1)}, u32[]{:S(2)}, u32[]{:S(2)}) collective-permute-start(f32[105,128]{0,1:T(8,128)S(1)} %add.235), channel_id=1, source_target_pairs={{0,4},{1,5},{2,6},{3,7},{4,0},{5,1},{6,2},{7,3},{8,12},{9,13},{10,... | collective-permute-start | bytes 161288 | tf_op jit(solution)/shard_map/ppermute | solution.py:32
  193.9 7.4 %collective-permute-start.13 = (f32[105,128]{0,1:T(8,128)S(1)}, f32[105,128]{0,1:T(8,128)S(1)}, u32[]{:S(2)}, u32[]{:S(2)}) collective-permute-start(f32[105,128]{0,1:T(8,128)S(1)} %add.236), channel_id=1, source_target_pairs={{0,16},{1,17},{2,18},{3,19},{4,20},{5,21},{6,22},{7,23},{8,24},{9,... | collective-permute-start | bytes 161288 | tf_op jit(solution)/shard_map/ppermute | solution.py:32
  201.3 6.0 %collective-permute-start.14 = (f32[105,128]{0,1:T(8,128)S(1)}, f32[105,128]{0,1:T(8,128)S(1)}, u32[]{:S(2)}, u32[]{:S(2)}) collective-permute-start(f32[105,128]{0,1:T(8,128)S(1)} %add.237), channel_id=1, source_target_pairs={{0,32},{1,33},{2,34},{3,35},{4,36},{5,37},{6,38},{7,39},{8,40},{9,... | collective-permute-start | bytes 161288 | tf_op jit(solution)/shard_map/ppermute | solution.py:32
  207.3 11.2 %collective-permute-start.15 = (f32[105,128]{0,1:T(8,128)S(1)}, f32[105,128]{0,1:T(8,128)S(1)}, u32[]{:S(2)}, u32[]{:S(2)}) collective-permute-start(f32[105,128]{0,1:T(8,128)S(1)} %add.238), channel_id=1, source_target_pairs={{0,128},{1,129},{2,130},{3,131},{4,132},{5,133},{6,134},{7,135},{8... | collective-permute-start | bytes 161288 | tf_op jit(solution)/shard_map/ppermute | solution.py:32
  218.5 6.5 %collective-permute-start.16 = (f32[105,128]{0,1:T(8,128)S(1)}, f32[105,128]{0,1:T(8,128)S(1)}, u32[]{:S(2)}, u32[]{:S(2)}) collective-permute-start(f32[105,128]{0,1:T(8,128)S(1)} %add.239), channel_id=1, source_target_pairs={{0,256},{1,257},{2,258},{3,259},{4,260},{5,261},{6,262},{7,263},{8... | collective-permute-start | bytes 161288 | tf_op jit(solution)/shard_map/ppermute | solution.py:32
  225.0 9.0 %collective-permute-start.17 = (f32[105,128]{0,1:T(8,128)S(1)}, f32[105,128]{0,1:T(8,128)S(1)}, u32[]{:S(2)}, u32[]{:S(2)}) collective-permute-start(f32[105,128]{0,1:T(8,128)S(1)} %add.240), channel_id=1, source_target_pairs={{0,64},{1,65},{2,66},{3,67},{4,68},{5,69},{6,70},{7,71},{8,72},{9,... | collective-permute-start | bytes 161288 | tf_op jit(solution)/shard_map/ppermute | solution.py:32
  234.2 11.1 %collective-permute-start.18 = (f32[210,128]{0,1:T(8,128)S(1)}, f32[210,128]{0,1:T(8,128)S(1)}, u32[]{:S(2)}, u32[]{:S(2)}) collective-permute-start(f32[210,128]{0,1:T(8,128)S(1)} %maximum_select_fusion), channel_id=1, source_target_pairs={{0,8},{1,9},{2,10},{3,11},{4,12},{5,13},{6,14},{7,15},{8,0},{9,1},... | collective-permute-start | bytes 322568 | tf_op jit(solution)/shard_map/ppermute | solution.py:32
  246.6 19.0 %copy-start.1 = (f32[64,256]{1,0:T(8,128)}, f32[64,256]{1,0:T(8,128)S(1)}, u32[]{:S(2)}) copy-start(f32[64,256]{1,0:T(8,128)S(1)} %fusion.3) | copy-start | bytes 196612

commit v3 on v2

--- a/solution.py
+++ b/solution.py
@@ -202,7 +202,6 @@
     first_proj = sums[:, :basis_count]
     second_proj = first_proj - matmul(first_proj, basis_gram)
     coefficients = first_proj + second_proj
-    columns = columns - matmul(coefficients, flat_basis)
     gram_matrix = (
         sums[:, basis_count:]
         - products(coefficients, first_proj)
@@ -210,7 +209,10 @@
         + products(matmul(coefficients, basis_gram), coefficients)
     )
     factor = jnp.linalg.cholesky(gram_matrix)
-    orthonormal = lax.linalg.triangular_solve(factor, columns, left_side=True, lower=True)
+    inverse = lax.linalg.triangular_solve(
+        factor, jnp.eye(new_count, dtype=factor.dtype), left_side=True, lower=True
+    )
+    orthonormal = matmul(inverse, columns) - matmul(matmul(inverse, coefficients), flat_basis)
     new_block = orthonormal.reshape(shifts_all, COLS, slab_x, quarter, depth)
     return (new_block, coefficients, factor)
 

time: 272 us -> 269 us (0.989)
  waiting for transfers between devices: 106 us -> 103 us
    ppermute x4, waiting for transfers between devices: 0.01 us -> 21.9 us  [padded_2(): lax.ppermute(head, axis, [((i + 1) % count, i) for i in range(ends)])]
    ppermute x4, waiting for transfers between devices: 54.7 us -> 34.3 us  [padded_2(): lax.ppermute(tail, axis, [(i, (i + 1) % count) for i in range(ends)])]
    ppermute x4, starting transfers between devices: 11.5 us -> 18.5 us  [padded_2(): lax.ppermute(tail, axis, [(i, (i + 1) % count) for i in range(ends)])]
    ppermute x11, starting transfers between devices: 64.4 us -> 59 us  [exchange(): return lax.ppermute(value, axes, [(i, i ^ mask) for i in range(total)])]
    ppermute x11, waiting for transfers between devices: 33.6 us -> 29.4 us  [exchange(): return lax.ppermute(value, axes, [(i, i ^ mask) for i in range(total)])]
    dot_general x3 -> x5, matrix products: 5.3 us -> 6.54 us  [matmul(): return jnp.dot(left_side, right_side, precision=lax.Precision.HIGHEST)]
    unnamed x16 -> x15, local copies, waits for them, and re-layouts: 9.65 us -> 9.32 us
  transfers between devices with their start and end apart: 21 -> 21, of which waited for: 17 -> 19; matrix products, arithmetic and copies ran while one was open for 6% -> 6% of each run, Pallas kernels for 0% -> 0%
where the time goes in v3:
time: 269 us; the launch traced here: 265 us
  waiting for transfers between devices  103 us (38%)
  starting transfers between devices  98.4 us (37%)
  other arithmetic  26.2 us (10%)
  local copies, waits for them, and re-layouts  18.1 us (7%)
  matrix products  18 us (7%)
    ppermute x11, starting transfers between devices, exchange(): return lax.ppermute(value, axes, [(i, i ^ mask) for i in range(total)])  59 us
    ppermute x4, waiting for transfers between devices, padded_2(): lax.ppermute(tail, axis, [(i, (i + 1) % count) for i in range(ends)])  34.3 us
    ppermute x11, waiting for transfers between devices, exchange(): return lax.ppermute(value, axes, [(i, i ^ mask) for i in range(total)])  29.4 us
    ppermute x4, waiting for transfers between devices, padded_2(): lax.ppermute(head, axis, [((i + 1) % count, i) for i in range(ends)])  21.9 us
    ppermute x4, starting transfers between devices, padded_2(): lax.ppermute(tail, axis, [(i, (i + 1) % count) for i in range(ends)])  18.5 us
    all_to_all x1, waiting for transfers between devices, local(): lax.all_to_all(merged, 'shift', split_axis=2, concat_axis=0, tiled=True)  15.1 us
    dot_general x6, matrix products, products(): lax.dot_general(left_side, right_side, (((1,), (1,)), ((), ())), precisio...  11.2 us
    all_to_all x1, starting transfers between devices, local(): lax.all_to_all(tail_columns, 'shift', split_axis=0, concat_axis=2, tiled=...  10.4 us
  transfers between devices with their start and end apart: 21, of which 19 were waited for; matrix products, arithmetic and copies ran while one was open for 6% of the time, Pallas kernels for 0%

profile of v3, /device:TPU:1, one launch (start us, length us, event | category | flops | bytes accessed | tf_op | source)
XLA Modules:
  0.0 264.6 jit_solution(13419354980157791750)
XLA Ops:
  0.7 2.3 slice.164
  3.0 10.4 %all-to-all-start = ((f32[64,2,8,256]{3,2,1,0:T(8,128)}), f32[64,2,8,256]{3,2,1,0:T(8,128)S(1)}, u32[]{:S(2)}, u32[]{:S(2)}) async-start(f32[64,2,8,256]{3,2,1,0:T(8,128)} %slice.164), calls=%async_computation | async-start | bytes 2097152 | tf_op jit(solution)/shard_map/all_to_all | solution.py:181
  13.5 1.3 collective-permute-start.1
  14.8 4.0 %collective-permute-start = (f32[1,32,256]{2,1,0:T(8,128)S(1)}, f32[1,32,256]{2,1,0:T(8,128)S(1)}, u32[]{:S(2)}, u32[]{:S(2)}) collective-permute-start(f32[1,32,256]{2,1,0:T(8,128)S(1)} %get-tuple-element.59), channel_id=1, source_target_pairs={{0,1},{1,2},{2,3},{3,4},{4,5},{5,6},{6,7},{7,8},{8,9},{9,10},{10,1... | collective-permute-start | bytes 98312 | tf_op jit(solution)/shard_map/ppermute | solution.py:22
  18.8 7.9 %copy.80 = f32[32,8,16,256]{3,1,2,0:T(8,128)} copy(f32[32,8,16,256]{3,2,1,0:T(8,128)} %bitcast.65) | data formatting | bytes 8388608
  27.2 1.8 all-to-all-done
  29.3 1.1 fusion.58
  30.4 1.4 collective-permute-start.3
  31.8 4.8 %collective-permute-start.2 = (f32[2,8,1,32,256]{4,3,2,1,0:T(8,128)}, f32[2,8,1,32,256]{4,3,2,1,0:T(8,128)}, u32[]{:S(2)}, u32[]{:S(2)}) collective-permute-start(f32[2,8,1,32,256]{4,3,2,1,0:T(8,128)} %get-tuple-element.47), channel_id=1, source_target_pairs={{0,1},{1,2},{2,3},{3,4},{4,5},{5,6},{6,7},{7,8},{8,9},{9,10},{10,1... | collective-permute-start | bytes 1572872 | tf_op jit(solution)/shard_map/ppermute | solution.py:22
  36.6 3.5 %fusion.62 = f32[256,256]{1,0:T(8,128)S(1)} fusion(f32[256,4096]{1,0:T(8,128)S(1)} %bitcast.61), kind=kOutput, calls=%fused_computation.135 | convolution fusion | flops 3221225472 | bytes 4456448 | tf_op jit(solution)/shard_map/dot_general | solution.py:152
  40.1 0.7 fusion.60
  40.8 1.2 gather_fusion
  42.0 0.9 pad_maximum_fusion.6
  42.9 2.4 collective-permute-done.3
  45.3 10.5 %collective-permute-done.2 = f32[2,8,1,32,256]{4,3,2,1,0:T(8,128)} collective-permute-done((f32[2,8,1,32,256]{4,3,2,1,0:T(8,128)}, f32[2,8,1,32,256]{4,3,2,1,0:T(8,128)}, u32[]{:S(2)}, u32[]{:S(2)}) %collective-permute-start.2) | collective-permute-done | bytes 524320 | tf_op jit(solution)/shard_map/ppermute | solution.py:22
  55.8 2.8 %select_maximum_fusion.4 = f32[2,8,4,34,258]{4,3,2,1,0:T(8,128)S(1)} fusion(f32[2,8,1,32,256]{4,3,2,1,0:T(8,128)S(1)} %collective-permute-done.3, f32[2,8,2,32,256]{4,3,2,1,0:T(8,128)S(1)} %multiply_multiply_fusion, f32[2,8,1,32,256]{4,3,2,1,0:T(8,128)} %collective-permute-done.2), kind=kLoop, calls=%fused_computation.10 | loop fusion | flops 8421120 | bytes 4342784 | tf_op jit(solution)/shard_map/concatenate | solution.py:20
  58.6 1.7 multiply_add_fusion.1
  60.3 1.3 collective-permute-start.5
  61.6 4.8 %collective-permute-start.4 = (f32[2,8,1,32,256]{4,3,2,1,0:T(8,128)S(1)}, f32[2,8,1,32,256]{4,3,2,1,0:T(8,128)S(1)}, u32[]{:S(2)}, u32[]{:S(2)}) collective-permute-start(f32[2,8,1,32,256]{4,3,2,1,0:T(8,128)S(1)} %get-tuple-element.45), channel_id=1, source_target_pairs={{0,1},{1,2},{2,3},{3,4},{4,5},{5,6},{6,7},{7,8},{8,9},{9,10},{10,1... | collective-permute-start | bytes 1572872 | tf_op jit(solution)/shard_map/ppermute | solution.py:22
  66.4 9.9 %collective-permute-done.5 = f32[2,8,1,32,256]{4,3,2,1,0:T(8,128)S(1)} collective-permute-done((f32[2,8,1,32,256]{4,3,2,1,0:T(8,128)S(1)}, f32[2,8,1,32,256]{4,3,2,1,0:T(8,128)S(1)}, u32[]{:S(2)}, u32[]{:S(2)}) %collective-permute-start.5) | collective-permute-done | bytes 524320 | tf_op jit(solution)/shard_map/ppermute | solution.py:24
  76.3 11.9 %collective-permute-done.4 = f32[2,8,1,32,256]{4,3,2,1,0:T(8,128)S(1)} collective-permute-done((f32[2,8,1,32,256]{4,3,2,1,0:T(8,128)S(1)}, f32[2,8,1,32,256]{4,3,2,1,0:T(8,128)S(1)}, u32[]{:S(2)}, u32[]{:S(2)}) %collective-permute-start.4) | collective-permute-done | bytes 524320 | tf_op jit(solution)/shard_map/ppermute | solution.py:22
  88.2 1.8 select_maximum_fusion.2
  90.0 1.3 multiply_add_fusion
  91.4 1.3 collective-permute-start.7
  92.7 5.0 %collective-permute-start.6 = (f32[2,8,1,32,256]{4,3,2,1,0:T(8,128)S(1)}, f32[2,8,1,32,256]{4,3,2,1,0:T(8,128)S(1)}, u32[]{:S(2)}, u32[]{:S(2)}) collective-permute-start(f32[2,8,1,32,256]{4,3,2,1,0:T(8,128)S(1)} %get-tuple-element.43), channel_id=1, source_target_pairs={{0,1},{1,2},{2,3},{3,4},{4,5},{5,6},{6,7},{7,8},{8,9},{9,10},{10,1... | collective-permute-start | bytes 1572872 | tf_op jit(solution)/shard_map/ppermute | solution.py:22
  97.7 9.7 %collective-permute-done.7 = f32[2,8,1,32,256]{4,3,2,1,0:T(8,128)S(1)} collective-permute-done((f32[2,8,1,32,256]{4,3,2,1,0:T(8,128)S(1)}, f32[2,8,1,32,256]{4,3,2,1,0:T(8,128)S(1)}, u32[]{:S(2)}, u32[]{:S(2)}) %collective-permute-start.7) | collective-permute-done | bytes 524320 | tf_op jit(solution)/shard_map/ppermute | solution.py:24
  107.3 11.9 %collective-permute-done.6 = f32[2,8,1,32,256]{4,3,2,1,0:T(8,128)S(1)} collective-permute-done((f32[2,8,1,32,256]{4,3,2,1,0:T(8,128)S(1)}, f32[2,8,1,32,256]{4,3,2,1,0:T(8,128)S(1)}, u32[]{:S(2)}, u32[]{:S(2)}) %collective-permute-start.6) | collective-permute-done | bytes 524320 | tf_op jit(solution)/shard_map/ppermute | solution.py:22
  119.2 1.8 select_maximum_fusion
  121.1 1.5 fusion.10
  122.6 1.8 copy.61
  124.4 5.3 %all-to-all-start.1 = ((f32[16,2,32,256]{3,1,0,2:T(2,128)}), f32[16,2,32,256]{3,1,0,2:T(2,128)S(1)}, u32[]{:S(2)}, u32[]{:S(2)}) async-start(f32[16,2,32,256]{3,1,0,2:T(2,128)} %copy.61), calls=%async_computation.1 | async-start | bytes 2097152 | tf_op jit(solution)/shard_map/all_to_all | solution.py:196
  129.7 15.1 %all-to-all-done.1 = f32[16,2,32,256]{3,1,0,2:T(2,128)S(1)} async-done(((f32[16,2,32,256]{3,1,0,2:T(2,128)}), f32[16,2,32,256]{3,1,0,2:T(2,128)S(1)}, u32[]{:S(2)}, u32[]{:S(2)}) %all-to-all-start.1) | async-done | bytes 1048608 | tf_op jit(solution)/shard_map/all_to_all | solution.py:196
  144.8 0.6 copy.82
  145.7 1.0 fusion.64
  146.7 6.1 %fusion.63 = f32[64,256]{1,0:T(8,128)S(1)} fusion(f32[64,4096]{1,0:T(8,128)S(1)} %reshape.72, f32[256,4096]{1,0:T(8,128)} %bitcast.59), kind=kOutput, calls=%fused_computation.136 | convolution fusion | flops 805306368 | bytes 5308416 | tf_op jit(solution)/shard_map/dot_general | solution.py:152
  153.0 6.5 %collective-permute-start.8 = (f32[210,128]{1,0:T(8,128)S(1)}, f32[210,128]{1,0:T(8,128)S(1)}, u32[]{:S(2)}, u32[]{:S(2)}) collective-permute-start(f32[210,128]{1,0:T(8,128)S(1)} %dynamic-slice_bitcast_fusion), channel_id=1, source_target_pairs={{0,8},{1,9},{2,10},{3,11},{4,12},{5,13},{6,14},{7,15},{8,0},{9,1},... | collective-permute-start | bytes 322568 | tf_op jit(solution)/shard_map/ppermute | solution.py:32
  159.5 3.0 %collective-permute-done.8 = f32[210,128]{1,0:T(8,128)S(1)} collective-permute-done((f32[210,128]{1,0:T(8,128)S(1)}, f32[210,128]{1,0:T(8,128)S(1)}, u32[]{:S(2)}, u32[]{:S(2)}) %collective-permute-start.8) | collective-permute-done | bytes 107552 | tf_op jit(solution)/shard_map/ppermute | solution.py:32
  162.7 9.6 %collective-permute-start.9 = (f32[105,128]{0,1:T(8,128)S(1)}, f32[105,128]{0,1:T(8,128)S(1)}, u32[]{:S(2)}, u32[]{:S(2)}) collective-permute-start(f32[105,128]{0,1:T(8,128)S(1)} %bitcast.70), channel_id=1, source_target_pairs={{0,64},{1,65},{2,66},{3,67},{4,68},{5,69},{6,70},{7,71},{8,72},{9,... | collective-permute-start | bytes 161288 | tf_op jit(solution)/shard_map/ppermute | solution.py:32
  172.4 1.5 collective-permute-done.9
  173.9 1.9 collective-permute-start.10
  175.8 3.1 %collective-permute-done.10 = f32[105,128]{0,1:T(8,128)S(1)} collective-permute-done((f32[105,128]{0,1:T(8,128)S(1)}, f32[105,128]{0,1:T(8,128)S(1)}, u32[]{:S(2)}, u32[]{:S(2)}) %collective-permute-start.10) | collective-permute-done | bytes 53792 | tf_op jit(solution)/shard_map/ppermute | solution.py:32
  178.9 1.9 collective-permute-start.11
  180.9 3.4 %collective-permute-done.11 = f32[105,128]{0,1:T(8,128)S(1)} collective-permute-done((f32[105,128]{0,1:T(8,128)S(1)}, f32[105,128]{0,1:T(8,128)S(1)}, u32[]{:S(2)}, u32[]{:S(2)}) %collective-permute-start.11) | collective-permute-done | bytes 53792 | tf_op jit(solution)/shard_map/ppermute | solution.py:32
  184.2 7.6 %collective-permute-start.12 = (f32[105,128]{0,1:T(8,128)S(1)}, f32[105,128]{0,1:T(8,128)S(1)}, u32[]{:S(2)}, u32[]{:S(2)}) collective-permute-start(f32[105,128]{0,1:T(8,128)S(1)} %add.235), channel_id=1, source_target_pairs={{0,4},{1,5},{2,6},{3,7},{4,0},{5,1},{6,2},{7,3},{8,12},{9,13},{10,... | collective-permute-start | bytes 161288 | tf_op jit(solution)/shard_map/ppermute | solution.py:32
  191.9 1.6 collective-permute-done.12
  193.6 3.1 %collective-permute-start.13 = (f32[105,128]{0,1:T(8,128)S(1)}, f32[105,128]{0,1:T(8,128)S(1)}, u32[]{:S(2)}, u32[]{:S(2)}) collective-permute-start(f32[105,128]{0,1:T(8,128)S(1)} %add.236), channel_id=1, source_target_pairs={{0,16},{1,17},{2,18},{3,19},{4,20},{5,21},{6,22},{7,23},{8,24},{9,... | collective-permute-start | bytes 161288 | tf_op jit(solution)/shard_map/ppermute | solution.py:32
  196.6 1.9 collective-permute-done.13
  198.6 6.2 %collective-permute-start.14 = (f32[105,128]{0,1:T(8,128)S(1)}, f32[105,128]{0,1:T(8,128)S(1)}, u32[]{:S(2)}, u32[]{:S(2)}) collective-permute-start(f32[105,128]{0,1:T(8,128)S(1)} %add.237), channel_id=1, source_target_pairs={{0,32},{1,33},{2,34},{3,35},{4,36},{5,37},{6,38},{7,39},{8,40},{9,... | collective-permute-start | bytes 161288 | tf_op jit(solution)/shard_map/ppermute | solution.py:32
  204.8 2.1 collective-permute-done.14
  206.9 8.0 %collective-permute-start.15 = (f32[105,128]{0,1:T(8,128)S(1)}, f32[105,128]{0,1:T(8,128)S(1)}, u32[]{:S(2)}, u32[]{:S(2)}) collective-permute-start(f32[105,128]{0,1:T(8,128)S(1)} %add.238), channel_id=1, source_target_pairs={{0,128},{1,129},{2,130},{3,131},{4,132},{5,133},{6,134},{7,135},{8... | collective-permute-start | bytes 161288 | tf_op jit(solution)/shard_map/ppermute | solution.py:32
  214.8 0.9 collective-permute-done.15
  215.7 2.5 collective-permute-start.16
  218.3 4.0 %collective-permute-done.16 = f32[105,128]{0,1:T(8,128)S(1)} collective-permute-done((f32[105,128]{0,1:T(8,128)S(1)}, f32[105,128]{0,1:T(8,128)S(1)}, u32[]{:S(2)}, u32[]{:S(2)}) %collective-permute-start.16) | collective-permute-done | bytes 53792 | tf_op jit(solution)/shard_map/ppermute | solution.py:32
  222.3 8.2 %collective-permute-start.17 = (f32[105,128]{0,1:T(8,128)S(1)}, f32[105,128]{0,1:T(8,128)S(1)}, u32[]{:S(2)}, u32[]{:S(2)}) collective-permute-start(f32[105,128]{0,1:T(8,128)S(1)} %add.240), channel_id=1, source_target_pairs={{0,64},{1,65},{2,66},{3,67},{4,68},{5,69},{6,70},{7,71},{8,72},{9,... | collective-permute-start | bytes 161288 | tf_op jit(solution)/shard_map/ppermute | solution.py:32
  230.5 1.6 collective-permute-done.17
  232.3 3.4 %collective-permute-start.18 = (f32[210,128]{0,1:T(8,128)S(1)}, f32[210,128]{0,1:T(8,128)S(1)}, u32[]{:S(2)}, u32[]{:S(2)}) collective-permute-start(f32[210,128]{0,1:T(8,128)S(1)} %maximum_select_fusion), channel_id=1, source_target_pairs={{0,8},{1,9},{2,10},{3,11},{4,12},{5,13},{6,14},{7,15},{8,0},{9,1},... | collective-permute-start | bytes 322568 | tf_op jit(solution)/shard_map/ppermute | solution.py:32
  235.7 6.3 %collective-permute-done.18 = f32[210,128]{0,1:T(8,128)S(1)} collective-permute-done((f32[210,128]{0,1:T(8,128)S(1)}, f32[210,128]{0,1:T(8,128)S(1)}, u32[]{:S(2)}, u32[]{:S(2)}) %collective-permute-start.18) | collective-permute-done | bytes 107552 | tf_op jit(solution)/shard_map/ppermute | solution.py:32
  244.3 5.8 %cholesky.17 = f32[64,64]{1,0:T(8,128)S(1)} custom-call(f32[64,64]{1,0:T(8,128)S(1)} %fusion.46), custom_call_target="Cholesky" | custom-call | tf_op jit(solution)/shard_map/jit(cholesky)/cholesky | solution.py:211
  250.2 0.6 compare_reduce_fusion
  250.8 1.3 select_bitcast_fusion
  252.1 4.9 %custom-call.6 = f32[1,64,64]{1,2,0:T(8,128)S(1)} custom-call(f32[1,64,64]{2,1,0:T(8,128)S(1)} %get-tuple-element.28), custom_call_target="InvertDiagBlocksLowerTriangular" | custom-call | tf_op jit(solution)/shard_map/triangular_solve | solution.py:212
  257.4 4.8 %fusion.66 = f32[64,4096]{1,0:T(8,128)S(1)} fusion(f32[64,256]{1,0:T(8,128)S(1)} %fusion.65, f32[256,4096]{1,0:T(8,128)} %bitcast.60), kind=kOutput, calls=%fused_computation.139 | convolution fusion | flops 805306368 | bytes 5308416 | tf_op jit(solution)/shard_map/dot_general | solution.py:158
  262.2 1.0 convolution_subtract_fusion
  263.3 1.3 copy.75
  (67 shorter events, 4.6 us)
Async XLA Ops:
  0.6 12.7 %copy-start.3 = (f32[8]{0:T(128)S(1)}, f32[8]{0:T(128)}, u32[]{:S(2)}) copy-start(f32[8]{0:T(128)} %param.6) | copy-start | bytes 100
  0.6 12.7 %copy-start.2 = (s32[2,32,256]{2,1,0:T(8,128)S(1)}, s32[2,32,256]{2,1,0:T(8,128)}, u32[]{:S(2)}) copy-start(s32[2,32,256]{2,1,0:T(8,128)} %param.5) | copy-start | bytes 196612
  0.7 12.7 %copy-start.4 = (f32[8]{0:T(128)S(1)}, f32[8]{0:T(128)}, u32[]{:S(2)}) copy-start(f32[8]{0:T(128)} %param.7) | copy-start | bytes 100
  3.0 26.1 %all-to-all-start = ((f32[64,2,8,256]{3,2,1,0:T(8,128)}), f32[64,2,8,256]{3,2,1,0:T(8,128)S(1)}, u32[]{:S(2)}, u32[]{:S(2)}) async-start(f32[64,2,8,256]{3,2,1,0:T(8,128)} %slice.164), calls=%async_computation | async-start | bytes 2097152 | tf_op jit(solution)/shard_map/all_to_all | solution.py:181
  13.5 13.3 %collective-permute-start.1 = (f32[1,32,256]{2,1,0:T(8,128)S(1)}, f32[1,32,256]{2,1,0:T(8,128)S(1)}, u32[]{:S(2)}, u32[]{:S(2)}) collective-permute-start(f32[1,32,256]{2,1,0:T(8,128)S(1)} %get-tuple-element.60), channel_id=1, source_target_pairs={{1,0},{2,1},{3,2},{4,3},{5,4},{6,5},{7,6},{8,7},{9,8},{10,9},{11,1... | collective-permute-start | bytes 98312 | tf_op jit(solution)/shard_map/ppermute | solution.py:24
  14.8 12.0 %collective-permute-start = (f32[1,32,256]{2,1,0:T(8,128)S(1)}, f32[1,32,256]{2,1,0:T(8,128)S(1)}, u32[]{:S(2)}, u32[]{:S(2)}) collective-permute-start(f32[1,32,256]{2,1,0:T(8,128)S(1)} %get-tuple-element.59), channel_id=1, source_target_pairs={{0,1},{1,2},{2,3},{3,4},{4,5},{5,6},{6,7},{7,8},{8,9},{9,10},{10,1... | collective-permute-start | bytes 98312 | tf_op jit(solution)/shard_map/ppermute | solution.py:22
  18.8 7.9 %copy-start.5 = (f32[8]{0:T(128)S(1)}, f32[8]{0:T(128)}, u32[]{:S(2)}) copy-start(f32[8]{0:T(128)} %param.8) | copy-start | bytes 100
  29.1 7.5 %copy-start = (f32[32,8,16,256]{3,1,2,0:T(8,128)S(1)}, f32[32,8,16,256]{3,1,2,0:T(8,128)}, u32[]{:S(2)}) copy-start(f32[32,8,16,256]{3,1,2,0:T(8,128)} %copy.80) | copy-start | bytes 12582916
  30.4 14.9 %collective-permute-start.3 = (f32[2,8,1,32,256]{4,3,2,1,0:T(8,128)}, f32[2,8,1,32,256]{4,3,2,1,0:T(8,128)S(1)}, u32[]{:S(2)}, u32[]{:S(2)}) collective-permute-start(f32[2,8,1,32,256]{4,3,2,1,0:T(8,128)} %get-tuple-element.48), channel_id=1, source_target_pairs={{1,0},{2,1},{3,2},{4,3},{5,4},{6,5},{7,6},{8,7},{9,8},{10,9},{11,1... | collective-permute-start | bytes 1572872 | tf_op jit(solution)/shard_map/ppermute | solution.py:24
  31.8 24.0 %collective-permute-start.2 = (f32[2,8,1,32,256]{4,3,2,1,0:T(8,128)}, f32[2,8,1,32,256]{4,3,2,1,0:T(8,128)}, u32[]{:S(2)}, u32[]{:S(2)}) collective-permute-start(f32[2,8,1,32,256]{4,3,2,1,0:T(8,128)} %get-tuple-element.47), channel_id=1, source_target_pairs={{0,1},{1,2},{2,3},{3,4},{4,5},{5,6},{6,7},{7,8},{8,9},{9,10},{10,1... | collective-permute-start | bytes 1572872 | tf_op jit(solution)/shard_map/ppermute | solution.py:22
  60.3 16.0 %collective-permute-start.5 = (f32[2,8,1,32,256]{4,3,2,1,0:T(8,128)S(1)}, f32[2,8,1,32,256]{4,3,2,1,0:T(8,128)S(1)}, u32[]{:S(2)}, u32[]{:S(2)}) collective-permute-start(f32[2,8,1,32,256]{4,3,2,1,0:T(8,128)S(1)} %get-tuple-element.46), channel_id=1, source_target_pairs={{1,0},{2,1},{3,2},{4,3},{5,4},{6,5},{7,6},{8,7},{9,8},{10,9},{11,1... | collective-permute-start | bytes 1572872 | tf_op jit(solution)/shard_map/ppermute | solution.py:24
  61.6 26.6 %collective-permute-start.4 = (f32[2,8,1,32,256]{4,3,2,1,0:T(8,128)S(1)}, f32[2,8,1,32,256]{4,3,2,1,0:T(8,128)S(1)}, u32[]{:S(2)}, u32[]{:S(2)}) collective-permute-start(f32[2,8,1,32,256]{4,3,2,1,0:T(8,128)S(1)} %get-tuple-element.45), channel_id=1, source_target_pairs={{0,1},{1,2},{2,3},{3,4},{4,5},{5,6},{6,7},{7,8},{8,9},{9,10},{10,1... | collective-permute-start | bytes 1572872 | tf_op jit(solution)/shard_map/ppermute | solution.py:22
  91.4 16.0 %collective-permute-start.7 = (f32[2,8,1,32,256]{4,3,2,1,0:T(8,128)S(1)}, f32[2,8,1,32,256]{4,3,2,1,0:T(8,128)S(1)}, u32[]{:S(2)}, u32[]{:S(2)}) collective-permute-start(f32[2,8,1,32,256]{4,3,2,1,0:T(8,128)S(1)} %get-tuple-element.44), channel_id=1, source_target_pairs={{1,0},{2,1},{3,2},{4,3},{5,4},{6,5},{7,6},{8,7},{9,8},{10,9},{11,1... | collective-permute-start | bytes 1572872 | tf_op jit(solution)/shard_map/ppermute | solution.py:24
  92.7 26.6 %collective-permute-start.6 = (f32[2,8,1,32,256]{4,3,2,1,0:T(8,128)S(1)}, f32[2,8,1,32,256]{4,3,2,1,0:T(8,128)S(1)}, u32[]{:S(2)}, u32[]{:S(2)}) collective-permute-start(f32[2,8,1,32,256]{4,3,2,1,0:T(8,128)S(1)} %get-tuple-element.43), channel_id=1, source_target_pairs={{0,1},{1,2},{2,3},{3,4},{4,5},{5,6},{6,7},{7,8},{8,9},{9,10},{10,1... | collective-permute-start | bytes 1572872 | tf_op jit(solution)/shard_map/ppermute | solution.py:22
  124.4 20.4 %all-to-all-start.1 = ((f32[16,2,32,256]{3,1,0,2:T(2,128)}), f32[16,2,32,256]{3,1,0,2:T(2,128)S(1)}, u32[]{:S(2)}, u32[]{:S(2)}) async-start(f32[16,2,32,256]{3,1,0,2:T(2,128)} %copy.61), calls=%async_computation.1 | async-start | bytes 2097152 | tf_op jit(solution)/shard_map/all_to_all | solution.py:196
  153.0 9.5 %collective-permute-start.8 = (f32[210,128]{1,0:T(8,128)S(1)}, f32[210,128]{1,0:T(8,128)S(1)}, u32[]{:S(2)}, u32[]{:S(2)}) collective-permute-start(f32[210,128]{1,0:T(8,128)S(1)} %dynamic-slice_bitcast_fusion), channel_id=1, source_target_pairs={{0,8},{1,9},{2,10},{3,11},{4,12},{5,13},{6,14},{7,15},{8,0},{9,1},... | collective-permute-start | bytes 322568 | tf_op jit(solution)/shard_map/ppermute | solution.py:32
  162.7 11.2 %collective-permute-start.9 = (f32[105,128]{0,1:T(8,128)S(1)}, f32[105,128]{0,1:T(8,128)S(1)}, u32[]{:S(2)}, u32[]{:S(2)}) collective-permute-start(f32[105,128]{0,1:T(8,128)S(1)} %bitcast.70), channel_id=1, source_target_pairs={{0,64},{1,65},{2,66},{3,67},{4,68},{5,69},{6,70},{7,71},{8,72},{9,... | collective-permute-start | bytes 161288 | tf_op jit(solution)/shard_map/ppermute | solution.py:32
  173.9 5.0 %collective-permute-start.10 = (f32[105,128]{0,1:T(8,128)S(1)}, f32[105,128]{0,1:T(8,128)S(1)}, u32[]{:S(2)}, u32[]{:S(2)}) collective-permute-start(f32[105,128]{0,1:T(8,128)S(1)} %bitcast_add_fusion.1), channel_id=1, source_target_pairs={{0,1},{1,0},{2,3},{3,2},{4,5},{5,4},{6,7},{7,6},{8,9},{9,8},{10,11... | collective-permute-start | bytes 161288 | tf_op jit(solution)/shard_map/ppermute | solution.py:32
  178.9 5.3 %collective-permute-start.11 = (f32[105,128]{0,1:T(8,128)S(1)}, f32[105,128]{0,1:T(8,128)S(1)}, u32[]{:S(2)}, u32[]{:S(2)}) collective-permute-start(f32[105,128]{0,1:T(8,128)S(1)} %add.234), channel_id=1, source_target_pairs={{0,2},{1,3},{2,0},{3,1},{4,6},{5,7},{6,4},{7,5},{8,10},{9,11},{10,... | collective-permute-start | bytes 161288 | tf_op jit(solution)/shard_map/ppermute | solution.py:32
  184.2 9.3 %collective-permute-start.12 = (f32[105,128]{0,1:T(8,128)S(1)}, f32[105,128]{0,1:T(8,128)S(1)}, u32[]{:S(2)}, u32[]{:S(2)}) collective-permute-start(f32[105,128]{0,1:T(8,128)S(1)} %add.235), channel_id=1, source_target_pairs={{0,4},{1,5},{2,6},{3,7},{4,0},{5,1},{6,2},{7,3},{8,12},{9,13},{10,... | collective-permute-start | bytes 161288 | tf_op jit(solution)/shard_map/ppermute | solution.py:32
  193.6 5.0 %collective-permute-start.13 = (f32[105,128]{0,1:T(8,128)S(1)}, f32[105,128]{0,1:T(8,128)S(1)}, u32[]{:S(2)}, u32[]{:S(2)}) collective-permute-start(f32[105,128]{0,1:T(8,128)S(1)} %add.236), channel_id=1, source_target_pairs={{0,16},{1,17},{2,18},{3,19},{4,20},{5,21},{6,22},{7,23},{8,24},{9,... | collective-permute-start | bytes 161288 | tf_op jit(solution)/shard_map/ppermute | solution.py:32
  198.6 8.3 %collective-permute-start.14 = (f32[105,128]{0,1:T(8,128)S(1)}, f32[105,128]{0,1:T(8,128)S(1)}, u32[]{:S(2)}, u32[]{:S(2)}) collective-permute-start(f32[105,128]{0,1:T(8,128)S(1)} %add.237), channel_id=1, source_target_pairs={{0,32},{1,33},{2,34},{3,35},{4,36},{5,37},{6,38},{7,39},{8,40},{9,... | collective-permute-start | bytes 161288 | tf_op jit(solution)/shard_map/ppermute | solution.py:32
  206.9 8.8 %collective-permute-start.15 = (f32[105,128]{0,1:T(8,128)S(1)}, f32[105,128]{0,1:T(8,128)S(1)}, u32[]{:S(2)}, u32[]{:S(2)}) collective-permute-start(f32[105,128]{0,1:T(8,128)S(1)} %add.238), channel_id=1, source_target_pairs={{0,128},{1,129},{2,130},{3,131},{4,132},{5,133},{6,134},{7,135},{8... | collective-permute-start | bytes 161288 | tf_op jit(solution)/shard_map/ppermute | solution.py:32
  215.7 6.5 %collective-permute-start.16 = (f32[105,128]{0,1:T(8,128)S(1)}, f32[105,128]{0,1:T(8,128)S(1)}, u32[]{:S(2)}, u32[]{:S(2)}) collective-permute-start(f32[105,128]{0,1:T(8,128)S(1)} %add.239), channel_id=1, source_target_pairs={{0,256},{1,257},{2,258},{3,259},{4,260},{5,261},{6,262},{7,263},{8... | collective-permute-start | bytes 161288 | tf_op jit(solution)/shard_map/ppermute | solution.py:32
  222.3 9.9 %collective-permute-start.17 = (f32[105,128]{0,1:T(8,128)S(1)}, f32[105,128]{0,1:T(8,128)S(1)}, u32[]{:S(2)}, u32[]{:S(2)}) collective-permute-start(f32[105,128]{0,1:T(8,128)S(1)} %add.240), channel_id=1, source_target_pairs={{0,64},{1,65},{2,66},{3,67},{4,68},{5,69},{6,70},{7,71},{8,72},{9,... | collective-permute-start | bytes 161288 | tf_op jit(solution)/shard_map/ppermute | solution.py:32
  232.3 9.7 %collective-permute-start.18 = (f32[210,128]{0,1:T(8,128)S(1)}, f32[210,128]{0,1:T(8,128)S(1)}, u32[]{:S(2)}, u32[]{:S(2)}) collective-permute-start(f32[210,128]{0,1:T(8,128)S(1)} %maximum_select_fusion), channel_id=1, source_target_pairs={{0,8},{1,9},{2,10},{3,11},{4,12},{5,13},{6,14},{7,15},{8,0},{9,1},... | collective-permute-start | bytes 322568 | tf_op jit(solution)/shard_map/ppermute | solution.py:32
  243.3 20.0 %copy-start.1 = (f32[64,256]{1,0:T(8,128)}, f32[64,256]{1,0:T(8,128)S(1)}, u32[]{:S(2)}) copy-start(f32[64,256]{1,0:T(8,128)S(1)} %fusion.3) | copy-start | bytes 196612

commit v4 on v3

--- a/solution.py
+++ b/solution.py
@@ -192,10 +192,19 @@
         return pack_symmetric(products(basis, basis), half)
 
     fields, packed = chebyshev(source, face_list, diagonal, padder, flat_basis, gram_of)
-    merged = fields.reshape(per_device * COLS, slab_x, full_y, depth)
-    regrouped = lax.all_to_all(merged, "shift", split_axis=2, concat_axis=0, tiled=True)
-    columns = regrouped.reshape(new_count, slab_x * quarter * depth)
-    own = jnp.concatenate([products(columns, flat_basis), products(columns, columns)], axis=1)
+    pieces = [
+        lax.all_to_all(fields[p], "shift", split_axis=2, concat_axis=0, tiled=True).reshape(
+            groups, COLS, slab_x * quarter * depth
+        )
+        for p in range(per_device)
+    ]
+    onto_basis = [
+        products(piece.reshape(groups * COLS, -1), flat_basis).reshape(groups, COLS, basis_count)
+        for piece in pieces
+    ]
+    columns = jnp.stack(pieces, axis=1).reshape(new_count, slab_x * quarter * depth)
+    onto_basis = jnp.stack(onto_basis, axis=1).reshape(new_count, basis_count)
+    own = jnp.concatenate([onto_basis, products(columns, columns)], axis=1)
     total = allsum(jnp.concatenate([own.reshape(-1, half), packed], axis=0), (3, 6)) * cell_weight
     sums = total[: own.size // half].reshape(own.shape)
     basis_gram = unpack_symmetric(total[own.size // half :], half)

time: 269 us -> 287 us (1.067)
  the two profiles are of different devices: /device:TPU:1 before, /device:TPU:34 now
where the time goes in v4:
time: 287 us; the launch traced here: 282 us
  waiting for transfers between devices  122 us (43%)
  starting transfers between devices  89.8 us (31%)
  other arithmetic  26.4 us (9%)
  matrix products  24.7 us (9%)
  local copies, waits for them, and re-layouts  18 us (6%)
    ppermute x11, waiting for transfers between devices, exchange(): return lax.ppermute(value, axes, [(i, i ^ mask) for i in range(total)])  54.6 us
    ppermute x11, starting transfers between devices, exchange(): return lax.ppermute(value, axes, [(i, i ^ mask) for i in range(total)])  41.7 us
    ppermute x4, waiting for transfers between devices, padded_2(): lax.ppermute(tail, axis, [(i, (i + 1) % count) for i in range(ends)])  29.4 us
    ppermute x4, starting transfers between devices, padded_2(): lax.ppermute(head, axis, [((i + 1) % count, i) for i in range(ends)])  27.2 us
    all_to_all x2, waiting for transfers between devices, local(): lax.all_to_all(fields[p], 'shift', split_axis=2, concat_axis=0, tiled=True)  19.4 us
    ppermute x4, waiting for transfers between devices, padded_2(): lax.ppermute(head, axis, [((i + 1) % count, i) for i in range(ends)])  18.3 us
    dot_general x7, matrix products, products(): lax.dot_general(left_side, right_side, (((1,), (1,)), ((), ())), precisio...  17.9 us
    ppermute x4, starting transfers between devices, padded_2(): lax.ppermute(tail, axis, [(i, (i + 1) % count) for i in range(ends)])  9.96 us
  transfers between devices with their start and end apart: 22, of which 20 were waited for; matrix products, arithmetic and copies ran while one was open for 6% of the time, Pallas kernels for 0%

profile of v4, /device:TPU:34, one launch (start us, length us, event | category | flops | bytes accessed | tf_op | source)
XLA Modules:
  0.0 282.1 jit_solution(16198766751774439074)
XLA Ops:
  0.7 2.3 slice.170
  3.0 3.5 %all-to-all-start = ((f32[64,2,8,256]{3,2,1,0:T(8,128)}), f32[64,2,8,256]{3,2,1,0:T(8,128)S(1)}, u32[]{:S(2)}, u32[]{:S(2)}) async-start(f32[64,2,8,256]{3,2,1,0:T(8,128)} %slice.170), calls=%async_computation | async-start | bytes 2097152 | tf_op jit(solution)/shard_map/all_to_all | solution.py:181
  6.7 3.2 %collective-permute-start.1 = (f32[1,32,256]{2,1,0:T(8,128)S(1)}, f32[1,32,256]{2,1,0:T(8,128)S(1)}, u32[]{:S(2)}, u32[]{:S(2)}) collective-permute-start(f32[1,32,256]{2,1,0:T(8,128)S(1)} %get-tuple-element.62), channel_id=1, source_target_pairs={{1,0},{2,1},{3,2},{4,3},{5,4},{6,5},{7,6},{8,7},{9,8},{10,9},{11,1... | collective-permute-start | bytes 98312 | tf_op jit(solution)/shard_map/ppermute | solution.py:24
  9.9 3.7 %collective-permute-start = (f32[1,32,256]{2,1,0:T(8,128)S(1)}, f32[1,32,256]{2,1,0:T(8,128)S(1)}, u32[]{:S(2)}, u32[]{:S(2)}) collective-permute-start(f32[1,32,256]{2,1,0:T(8,128)S(1)} %get-tuple-element.61), channel_id=1, source_target_pairs={{0,1},{1,2},{2,3},{3,4},{4,5},{5,6},{6,7},{7,8},{8,9},{9,10},{10,1... | collective-permute-start | bytes 98312 | tf_op jit(solution)/shard_map/ppermute | solution.py:22
  13.7 7.9 %copy.119 = f32[32,8,16,256]{3,1,2,0:T(8,128)} copy(f32[32,8,16,256]{3,2,1,0:T(8,128)} %bitcast.85) | data formatting | bytes 8388608
  21.7 1.1 collective-permute-done
  23.5 1.1 fusion.72
  24.6 8.3 %collective-permute-start.3 = (f32[2,8,1,32,256]{4,3,2,1,0:T(8,128)}, f32[2,8,1,32,256]{4,3,2,1,0:T(8,128)S(1)}, u32[]{:S(2)}, u32[]{:S(2)}) collective-permute-start(f32[2,8,1,32,256]{4,3,2,1,0:T(8,128)} %get-tuple-element.50), channel_id=1, source_target_pairs={{1,0},{2,1},{3,2},{4,3},{5,4},{6,5},{7,6},{8,7},{9,8},{10,9},{11,1... | collective-permute-start | bytes 1572872 | tf_op jit(solution)/shard_map/ppermute | solution.py:24
  32.8 2.4 collective-permute-start.2
  35.2 3.5 %fusion.76 = f32[256,256]{1,0:T(8,128)S(1)} fusion(f32[256,4096]{1,0:T(8,128)S(1)} %bitcast.84), kind=kOutput, calls=%fused_computation.148 | convolution fusion | flops 3221225472 | bytes 4456448 | tf_op jit(solution)/shard_map/dot_general | solution.py:152
  39.5 1.2 gather_fusion
  41.6 3.0 %collective-permute-done.3 = f32[2,8,1,32,256]{4,3,2,1,0:T(8,128)S(1)} collective-permute-done((f32[2,8,1,32,256]{4,3,2,1,0:T(8,128)}, f32[2,8,1,32,256]{4,3,2,1,0:T(8,128)S(1)}, u32[]{:S(2)}, u32[]{:S(2)}) %collective-permute-start.3) | collective-permute-done | bytes 524320 | tf_op jit(solution)/shard_map/ppermute | solution.py:24
  44.6 8.3 %collective-permute-done.2 = f32[2,8,1,32,256]{4,3,2,1,0:T(8,128)} collective-permute-done((f32[2,8,1,32,256]{4,3,2,1,0:T(8,128)}, f32[2,8,1,32,256]{4,3,2,1,0:T(8,128)}, u32[]{:S(2)}, u32[]{:S(2)}) %collective-permute-start.2) | collective-permute-done | bytes 524320 | tf_op jit(solution)/shard_map/ppermute | solution.py:22
  52.9 2.8 select_maximum_fusion.4
  55.7 1.7 multiply_add_fusion.1
  57.5 7.9 %collective-permute-start.5 = (f32[2,8,1,32,256]{4,3,2,1,0:T(8,128)S(1)}, f32[2,8,1,32,256]{4,3,2,1,0:T(8,128)S(1)}, u32[]{:S(2)}, u32[]{:S(2)}) collective-permute-start(f32[2,8,1,32,256]{4,3,2,1,0:T(8,128)S(1)} %get-tuple-element.48), channel_id=1, source_target_pairs={{1,0},{2,1},{3,2},{4,3},{5,4},{6,5},{7,6},{8,7},{9,8},{10,9},{11,1... | collective-permute-start | bytes 1572872 | tf_op jit(solution)/shard_map/ppermute | solution.py:24
  65.4 1.9 collective-permute-start.4
  67.3 8.1 %collective-permute-done.5 = f32[2,8,1,32,256]{4,3,2,1,0:T(8,128)S(1)} collective-permute-done((f32[2,8,1,32,256]{4,3,2,1,0:T(8,128)S(1)}, f32[2,8,1,32,256]{4,3,2,1,0:T(8,128)S(1)}, u32[]{:S(2)}, u32[]{:S(2)}) %collective-permute-start.5) | collective-permute-done | bytes 524320 | tf_op jit(solution)/shard_map/ppermute | solution.py:24
  75.4 10.0 %collective-permute-done.4 = f32[2,8,1,32,256]{4,3,2,1,0:T(8,128)S(1)} collective-permute-done((f32[2,8,1,32,256]{4,3,2,1,0:T(8,128)S(1)}, f32[2,8,1,32,256]{4,3,2,1,0:T(8,128)S(1)}, u32[]{:S(2)}, u32[]{:S(2)}) %collective-permute-start.4) | collective-permute-done | bytes 524320 | tf_op jit(solution)/shard_map/ppermute | solution.py:22
  85.4 1.8 select_maximum_fusion.2
  87.2 1.3 multiply_add_fusion
  88.6 7.9 %collective-permute-start.7 = (f32[2,8,1,32,256]{4,3,2,1,0:T(8,128)S(1)}, f32[2,8,1,32,256]{4,3,2,1,0:T(8,128)S(1)}, u32[]{:S(2)}, u32[]{:S(2)}) collective-permute-start(f32[2,8,1,32,256]{4,3,2,1,0:T(8,128)S(1)} %get-tuple-element.46), channel_id=1, source_target_pairs={{1,0},{2,1},{3,2},{4,3},{5,4},{6,5},{7,6},{8,7},{9,8},{10,9},{11,1... | collective-permute-start | bytes 1572872 | tf_op jit(solution)/shard_map/ppermute | solution.py:24
  96.5 1.9 collective-permute-start.6
  98.4 7.2 %collective-permute-done.7 = f32[2,8,1,32,256]{4,3,2,1,0:T(8,128)S(1)} collective-permute-done((f32[2,8,1,32,256]{4,3,2,1,0:T(8,128)S(1)}, f32[2,8,1,32,256]{4,3,2,1,0:T(8,128)S(1)}, u32[]{:S(2)}, u32[]{:S(2)}) %collective-permute-start.7) | collective-permute-done | bytes 524320 | tf_op jit(solution)/shard_map/ppermute | solution.py:24
  105.6 10.0 %collective-permute-done.6 = f32[2,8,1,32,256]{4,3,2,1,0:T(8,128)S(1)} collective-permute-done((f32[2,8,1,32,256]{4,3,2,1,0:T(8,128)S(1)}, f32[2,8,1,32,256]{4,3,2,1,0:T(8,128)S(1)}, u32[]{:S(2)}, u32[]{:S(2)}) %collective-permute-start.6) | collective-permute-done | bytes 524320 | tf_op jit(solution)/shard_map/ppermute | solution.py:22
  115.6 1.8 select_maximum_fusion
  117.4 1.5 fusion.20
  119.0 1.2 copy.82
  120.2 3.8 %all-to-all-start.2 = ((f32[8,2,32,256]{3,1,0,2:T(2,128)}), f32[8,2,32,256]{3,1,0,2:T(2,128)S(1)}, u32[]{:S(2)}, u32[]{:S(2)}) async-start(f32[8,2,32,256]{3,1,0,2:T(2,128)} %copy.82), calls=%async_computation.2 | async-start | bytes 1048576 | tf_op jit(solution)/shard_map/all_to_all | solution.py:196
  123.9 1.2 copy.78
  125.1 9.1 %all-to-all-done.2 = f32[8,2,32,256]{3,1,0,2:T(2,128)S(1)} async-done(((f32[8,2,32,256]{3,1,0,2:T(2,128)}), f32[8,2,32,256]{3,1,0,2:T(2,128)S(1)}, u32[]{:S(2)}, u32[]{:S(2)}) %all-to-all-start.2) | async-done | bytes 524320 | tf_op jit(solution)/shard_map/all_to_all | solution.py:196
  134.3 3.6 %all-to-all-start.1 = ((f32[8,2,32,256]{3,1,0,2:T(2,128)}), f32[8,2,32,256]{3,1,0,2:T(2,128)S(1)}, u32[]{:S(2)}, u32[]{:S(2)}) async-start(f32[8,2,32,256]{3,1,0,2:T(2,128)} %copy.78), calls=%async_computation.1 | async-start | bytes 1048576 | tf_op jit(solution)/shard_map/all_to_all | solution.py:196
  138.0 10.2 %all-to-all-done.1 = f32[8,2,32,256]{3,1,0,2:T(2,128)S(1)} async-done(((f32[8,2,32,256]{3,1,0,2:T(2,128)}), f32[8,2,32,256]{3,1,0,2:T(2,128)S(1)}, u32[]{:S(2)}, u32[]{:S(2)}) %all-to-all-start.1) | async-done | bytes 524320 | tf_op jit(solution)/shard_map/all_to_all | solution.py:196
  148.3 7.5 %fusion.11 = f32[4,1,8,256]{3,2,0,1:T(8,128)S(1)} fusion(f32[256,2,8,256,1]{3,2,1,0,4:T(8,128)} %bitcast.86, f32[8,2,4,8,256]{4,1,0,3,2:T(2,128)S(1)} %bitcast.94), kind=kOutput, calls=%fused_computation.22 | convolution fusion | flops 402653184 | bytes 4751360 | tf_op jit(solution)/shard_map/dot_general | solution.py:152
  155.8 5.2 %fusion.8 = f32[4,1,8,256]{3,2,0,1:T(8,128)S(1)} fusion(f32[256,2,8,256,1]{3,2,1,0,4:T(8,128)S(1)} %bitcast.87, f32[8,2,4,8,256]{4,1,0,3,2:T(2,128)S(1)} %bitcast.96), kind=kOutput, calls=%fused_computation.21 | convolution fusion | flops 402653184 | bytes 4751360 | tf_op jit(solution)/shard_map/dot_general | solution.py:152
  161.2 1.0 fusion.77
  162.4 11.0 %collective-permute-start.8 = (f32[210,128]{1,0:T(8,128)S(1)}, f32[210,128]{1,0:T(8,128)S(1)}, u32[]{:S(2)}, u32[]{:S(2)}) collective-permute-start(f32[210,128]{1,0:T(8,128)S(1)} %dynamic-slice_bitcast_fusion), channel_id=1, source_target_pairs={{0,8},{1,9},{2,10},{3,11},{4,12},{5,13},{6,14},{7,15},{8,0},{9,1},... | collective-permute-start | bytes 322568 | tf_op jit(solution)/shard_map/ppermute | solution.py:32
  173.4 4.5 %collective-permute-done.8 = f32[210,128]{1,0:T(8,128)S(1)} collective-permute-done((f32[210,128]{1,0:T(8,128)S(1)}, f32[210,128]{1,0:T(8,128)S(1)}, u32[]{:S(2)}, u32[]{:S(2)}) %collective-permute-start.8) | collective-permute-done | bytes 107552 | tf_op jit(solution)/shard_map/ppermute | solution.py:32
  178.1 1.9 collective-permute-start.9
  180.1 8.7 %collective-permute-done.9 = f32[105,128]{0,1:T(8,128)S(1)} collective-permute-done((f32[105,128]{0,1:T(8,128)S(1)}, f32[105,128]{0,1:T(8,128)S(1)}, u32[]{:S(2)}, u32[]{:S(2)}) %collective-permute-start.9) | collective-permute-done | bytes 53792 | tf_op jit(solution)/shard_map/ppermute | solution.py:32
  188.8 5.1 %collective-permute-start.10 = (f32[105,128]{0,1:T(8,128)S(1)}, f32[105,128]{0,1:T(8,128)S(1)}, u32[]{:S(2)}, u32[]{:S(2)}) collective-permute-start(f32[105,128]{0,1:T(8,128)S(1)} %bitcast_add_fusion.1), channel_id=1, source_target_pairs={{0,1},{1,0},{2,3},{3,2},{4,5},{5,4},{6,7},{7,6},{8,9},{9,8},{10,11... | collective-permute-start | bytes 161288 | tf_op jit(solution)/shard_map/ppermute | solution.py:32
  193.9 2.2 collective-permute-done.10
  196.1 1.9 collective-permute-start.11
  198.1 4.2 %collective-permute-done.11 = f32[105,128]{0,1:T(8,128)S(1)} collective-permute-done((f32[105,128]{0,1:T(8,128)S(1)}, f32[105,128]{0,1:T(8,128)S(1)}, u32[]{:S(2)}, u32[]{:S(2)}) %collective-permute-start.11) | collective-permute-done | bytes 53792 | tf_op jit(solution)/shard_map/ppermute | solution.py:32
  202.3 7.1 %collective-permute-start.12 = (f32[105,128]{0,1:T(8,128)S(1)}, f32[105,128]{0,1:T(8,128)S(1)}, u32[]{:S(2)}, u32[]{:S(2)}) collective-permute-start(f32[105,128]{0,1:T(8,128)S(1)} %add.235), channel_id=1, source_target_pairs={{0,4},{1,5},{2,6},{3,7},{4,0},{5,1},{6,2},{7,3},{8,12},{9,13},{10,... | collective-permute-start | bytes 161288 | tf_op jit(solution)/shard_map/ppermute | solution.py:32
  209.4 2.2 collective-permute-done.12
  211.7 1.9 collective-permute-start.13
  213.6 4.9 %collective-permute-done.13 = f32[105,128]{0,1:T(8,128)S(1)} collective-permute-done((f32[105,128]{0,1:T(8,128)S(1)}, f32[105,128]{0,1:T(8,128)S(1)}, u32[]{:S(2)}, u32[]{:S(2)}) %collective-permute-start.13) | collective-permute-done | bytes 53792 | tf_op jit(solution)/shard_map/ppermute | solution.py:32
  218.6 1.9 collective-permute-start.14
  220.5 5.2 %collective-permute-done.14 = f32[105,128]{0,1:T(8,128)S(1)} collective-permute-done((f32[105,128]{0,1:T(8,128)S(1)}, f32[105,128]{0,1:T(8,128)S(1)}, u32[]{:S(2)}, u32[]{:S(2)}) %collective-permute-start.14) | collective-permute-done | bytes 53792 | tf_op jit(solution)/shard_map/ppermute | solution.py:32
  225.7 1.9 collective-permute-start.15
  227.7 1.2 collective-permute-done.15
  228.9 2.5 collective-permute-start.16
  231.4 5.2 %collective-permute-done.16 = f32[105,128]{0,1:T(8,128)S(1)} collective-permute-done((f32[105,128]{0,1:T(8,128)S(1)}, f32[105,128]{0,1:T(8,128)S(1)}, u32[]{:S(2)}, u32[]{:S(2)}) %collective-permute-start.16) | collective-permute-done | bytes 53792 | tf_op jit(solution)/shard_map/ppermute | solution.py:32
  236.6 1.9 collective-permute-start.17
  238.5 8.4 %collective-permute-done.17 = f32[105,128]{0,1:T(8,128)S(1)} collective-permute-done((f32[105,128]{0,1:T(8,128)S(1)}, f32[105,128]{0,1:T(8,128)S(1)}, u32[]{:S(2)}, u32[]{:S(2)}) %collective-permute-start.17) | collective-permute-done | bytes 53792 | tf_op jit(solution)/shard_map/ppermute | solution.py:32
  247.1 4.6 %collective-permute-start.18 = (f32[210,128]{0,1:T(8,128)S(1)}, f32[210,128]{0,1:T(8,128)S(1)}, u32[]{:S(2)}, u32[]{:S(2)}) collective-permute-start(f32[210,128]{0,1:T(8,128)S(1)} %maximum_select_fusion), channel_id=1, source_target_pairs={{0,8},{1,9},{2,10},{3,11},{4,12},{5,13},{6,14},{7,15},{8,0},{9,1},... | collective-permute-start | bytes 322568 | tf_op jit(solution)/shard_map/ppermute | solution.py:32
  251.7 7.6 %collective-permute-done.18 = f32[210,128]{0,1:T(8,128)S(1)} collective-permute-done((f32[210,128]{0,1:T(8,128)S(1)}, f32[210,128]{0,1:T(8,128)S(1)}, u32[]{:S(2)}, u32[]{:S(2)}) %collective-permute-start.18) | collective-permute-done | bytes 107552 | tf_op jit(solution)/shard_map/ppermute | solution.py:32
  261.6 5.8 %cholesky.17 = f32[64,64]{1,0:T(8,128)S(1)} custom-call(f32[64,64]{1,0:T(8,128)S(1)} %fusion.60), custom_call_target="Cholesky" | custom-call | tf_op jit(solution)/shard_map/jit(cholesky)/cholesky | solution.py:220
  268.1 1.3 select_bitcast_fusion
  269.4 4.9 %custom-call.6 = f32[1,64,64]{1,2,0:T(8,128)S(1)} custom-call(f32[1,64,64]{2,1,0:T(8,128)S(1)} %get-tuple-element.28), custom_call_target="InvertDiagBlocksLowerTriangular" | custom-call | tf_op jit(solution)/shard_map/triangular_solve | solution.py:221
  274.7 4.8 %fusion.79 = f32[64,4096]{1,0:T(8,128)S(1)} fusion(f32[64,256]{1,0:T(8,128)S(1)} %fusion.78, f32[256,4096]{1,0:T(8,128)} %bitcast.83), kind=kOutput, calls=%fused_computation.151 | convolution fusion | flops 805306368 | bytes 5308416 | tf_op jit(solution)/shard_map/dot_general | solution.py:158
  279.5 1.0 convolution_subtract_fusion
  280.6 1.3 copy.98
  (76 shorter events, 6.8 us)
Async XLA Ops:
  0.6 5.9 %copy-start.4 = (f32[8]{0:T(128)S(1)}, f32[8]{0:T(128)}, u32[]{:S(2)}) copy-start(f32[8]{0:T(128)} %param.6) | copy-start | bytes 100
  0.6 5.9 %copy-start.3 = (s32[2,32,256]{2,1,0:T(8,128)S(1)}, s32[2,32,256]{2,1,0:T(8,128)}, u32[]{:S(2)}) copy-start(s32[2,32,256]{2,1,0:T(8,128)} %param.5) | copy-start | bytes 196612
  0.7 5.9 %copy-start.5 = (f32[8]{0:T(128)S(1)}, f32[8]{0:T(128)}, u32[]{:S(2)}) copy-start(f32[8]{0:T(128)} %param.7) | copy-start | bytes 100
  3.0 20.2 %all-to-all-start = ((f32[64,2,8,256]{3,2,1,0:T(8,128)}), f32[64,2,8,256]{3,2,1,0:T(8,128)S(1)}, u32[]{:S(2)}, u32[]{:S(2)}) async-start(f32[64,2,8,256]{3,2,1,0:T(8,128)} %slice.170), calls=%async_computation | async-start | bytes 2097152 | tf_op jit(solution)/shard_map/all_to_all | solution.py:181
  6.7 15.0 %collective-permute-start.1 = (f32[1,32,256]{2,1,0:T(8,128)S(1)}, f32[1,32,256]{2,1,0:T(8,128)S(1)}, u32[]{:S(2)}, u32[]{:S(2)}) collective-permute-start(f32[1,32,256]{2,1,0:T(8,128)S(1)} %get-tuple-element.62), channel_id=1, source_target_pairs={{1,0},{2,1},{3,2},{4,3},{5,4},{6,5},{7,6},{8,7},{9,8},{10,9},{11,1... | collective-permute-start | bytes 98312 | tf_op jit(solution)/shard_map/ppermute | solution.py:24
  9.9 12.9 %collective-permute-start = (f32[1,32,256]{2,1,0:T(8,128)S(1)}, f32[1,32,256]{2,1,0:T(8,128)S(1)}, u32[]{:S(2)}, u32[]{:S(2)}) collective-permute-start(f32[1,32,256]{2,1,0:T(8,128)S(1)} %get-tuple-element.61), channel_id=1, source_target_pairs={{0,1},{1,2},{2,3},{3,4},{4,5},{5,6},{6,7},{7,8},{8,9},{9,10},{10,1... | collective-permute-start | bytes 98312 | tf_op jit(solution)/shard_map/ppermute | solution.py:22
  13.7 8.0 %copy-start.6 = (f32[8]{0:T(128)S(1)}, f32[8]{0:T(128)}, u32[]{:S(2)}) copy-start(f32[8]{0:T(128)} %param.8) | copy-start | bytes 100
  23.2 12.1 %copy-start = (f32[32,8,16,256]{3,1,2,0:T(8,128)S(1)}, f32[32,8,16,256]{3,1,2,0:T(8,128)}, u32[]{:S(2)}) copy-start(f32[32,8,16,256]{3,1,2,0:T(8,128)} %copy.119) | copy-start | bytes 12582916
  24.6 20.0 %collective-permute-start.3 = (f32[2,8,1,32,256]{4,3,2,1,0:T(8,128)}, f32[2,8,1,32,256]{4,3,2,1,0:T(8,128)S(1)}, u32[]{:S(2)}, u32[]{:S(2)}) collective-permute-start(f32[2,8,1,32,256]{4,3,2,1,0:T(8,128)} %get-tuple-element.50), channel_id=1, source_target_pairs={{1,0},{2,1},{3,2},{4,3},{5,4},{6,5},{7,6},{8,7},{9,8},{10,9},{11,1... | collective-permute-start | bytes 1572872 | tf_op jit(solution)/shard_map/ppermute | solution.py:24
  32.8 20.1 %collective-permute-start.2 = (f32[2,8,1,32,256]{4,3,2,1,0:T(8,128)}, f32[2,8,1,32,256]{4,3,2,1,0:T(8,128)}, u32[]{:S(2)}, u32[]{:S(2)}) collective-permute-start(f32[2,8,1,32,256]{4,3,2,1,0:T(8,128)} %get-tuple-element.49), channel_id=1, source_target_pairs={{0,1},{1,2},{2,3},{3,4},{4,5},{5,6},{6,7},{7,8},{8,9},{9,10},{10,1... | collective-permute-start | bytes 1572872 | tf_op jit(solution)/shard_map/ppermute | solution.py:22
  57.5 17.9 %collective-permute-start.5 = (f32[2,8,1,32,256]{4,3,2,1,0:T(8,128)S(1)}, f32[2,8,1,32,256]{4,3,2,1,0:T(8,128)S(1)}, u32[]{:S(2)}, u32[]{:S(2)}) collective-permute-start(f32[2,8,1,32,256]{4,3,2,1,0:T(8,128)S(1)} %get-tuple-element.48), channel_id=1, source_target_pairs={{1,0},{2,1},{3,2},{4,3},{5,4},{6,5},{7,6},{8,7},{9,8},{10,9},{11,1... | collective-permute-start | bytes 1572872 | tf_op jit(solution)/shard_map/ppermute | solution.py:24
  65.4 20.0 %collective-permute-start.4 = (f32[2,8,1,32,256]{4,3,2,1,0:T(8,128)S(1)}, f32[2,8,1,32,256]{4,3,2,1,0:T(8,128)S(1)}, u32[]{:S(2)}, u32[]{:S(2)}) collective-permute-start(f32[2,8,1,32,256]{4,3,2,1,0:T(8,128)S(1)} %get-tuple-element.47), channel_id=1, source_target_pairs={{0,1},{1,2},{2,3},{3,4},{4,5},{5,6},{6,7},{7,8},{8,9},{9,10},{10,1... | collective-permute-start | bytes 1572872 | tf_op jit(solution)/shard_map/ppermute | solution.py:22
  88.6 17.0 %collective-permute-start.7 = (f32[2,8,1,32,256]{4,3,2,1,0:T(8,128)S(1)}, f32[2,8,1,32,256]{4,3,2,1,0:T(8,128)S(1)}, u32[]{:S(2)}, u32[]{:S(2)}) collective-permute-start(f32[2,8,1,32,256]{4,3,2,1,0:T(8,128)S(1)} %get-tuple-element.46), channel_id=1, source_target_pairs={{1,0},{2,1},{3,2},{4,3},{5,4},{6,5},{7,6},{8,7},{9,8},{10,9},{11,1... | collective-permute-start | bytes 1572872 | tf_op jit(solution)/shard_map/ppermute | solution.py:24
  96.5 19.1 %collective-permute-start.6 = (f32[2,8,1,32,256]{4,3,2,1,0:T(8,128)S(1)}, f32[2,8,1,32,256]{4,3,2,1,0:T(8,128)S(1)}, u32[]{:S(2)}, u32[]{:S(2)}) collective-permute-start(f32[2,8,1,32,256]{4,3,2,1,0:T(8,128)S(1)} %get-tuple-element.45), channel_id=1, source_target_pairs={{0,1},{1,2},{2,3},{3,4},{4,5},{5,6},{6,7},{7,8},{8,9},{9,10},{10,1... | collective-permute-start | bytes 1572872 | tf_op jit(solution)/shard_map/ppermute | solution.py:22
  120.2 14.1 %all-to-all-start.2 = ((f32[8,2,32,256]{3,1,0,2:T(2,128)}), f32[8,2,32,256]{3,1,0,2:T(2,128)S(1)}, u32[]{:S(2)}, u32[]{:S(2)}) async-start(f32[8,2,32,256]{3,1,0,2:T(2,128)} %copy.82), calls=%async_computation.2 | async-start | bytes 1048576 | tf_op jit(solution)/shard_map/all_to_all | solution.py:196
  134.3 13.9 %all-to-all-start.1 = ((f32[8,2,32,256]{3,1,0,2:T(2,128)}), f32[8,2,32,256]{3,1,0,2:T(2,128)S(1)}, u32[]{:S(2)}, u32[]{:S(2)}) async-start(f32[8,2,32,256]{3,1,0,2:T(2,128)} %copy.78), calls=%async_computation.1 | async-start | bytes 1048576 | tf_op jit(solution)/shard_map/all_to_all | solution.py:196
  148.2 7.6 %copy-start.1 = (f32[256,2,8,256]{3,2,1,0:T(8,128)S(1)}, f32[256,2,8,256]{3,2,1,0:T(8,128)}, u32[]{:S(2)}) copy-start(f32[256,2,8,256]{3,2,1,0:T(8,128)} %param.9) | copy-start | bytes 12582916
  162.4 15.5 %collective-permute-start.8 = (f32[210,128]{1,0:T(8,128)S(1)}, f32[210,128]{1,0:T(8,128)S(1)}, u32[]{:S(2)}, u32[]{:S(2)}) collective-permute-start(f32[210,128]{1,0:T(8,128)S(1)} %dynamic-slice_bitcast_fusion), channel_id=1, source_target_pairs={{0,8},{1,9},{2,10},{3,11},{4,12},{5,13},{6,14},{7,15},{8,0},{9,1},... | collective-permute-start | bytes 322568 | tf_op jit(solution)/shard_map/ppermute | solution.py:32
  178.1 10.7 %collective-permute-start.9 = (f32[105,128]{0,1:T(8,128)S(1)}, f32[105,128]{0,1:T(8,128)S(1)}, u32[]{:S(2)}, u32[]{:S(2)}) collective-permute-start(f32[105,128]{0,1:T(8,128)S(1)} %bitcast.102), channel_id=1, source_target_pairs={{0,64},{1,65},{2,66},{3,67},{4,68},{5,69},{6,70},{7,71},{8,72},{9,... | collective-permute-start | bytes 161288 | tf_op jit(solution)/shard_map/ppermute | solution.py:32
  188.8 7.3 %collective-permute-start.10 = (f32[105,128]{0,1:T(8,128)S(1)}, f32[105,128]{0,1:T(8,128)S(1)}, u32[]{:S(2)}, u32[]{:S(2)}) collective-permute-start(f32[105,128]{0,1:T(8,128)S(1)} %bitcast_add_fusion.1), channel_id=1, source_target_pairs={{0,1},{1,0},{2,3},{3,2},{4,5},{5,4},{6,7},{7,6},{8,9},{9,8},{10,11... | collective-permute-start | bytes 161288 | tf_op jit(solution)/shard_map/ppermute | solution.py:32
  196.1 6.2 %collective-permute-start.11 = (f32[105,128]{0,1:T(8,128)S(1)}, f32[105,128]{0,1:T(8,128)S(1)}, u32[]{:S(2)}, u32[]{:S(2)}) collective-permute-start(f32[105,128]{0,1:T(8,128)S(1)} %add.234), channel_id=1, source_target_pairs={{0,2},{1,3},{2,0},{3,1},{4,6},{5,7},{6,4},{7,5},{8,10},{9,11},{10,... | collective-permute-start | bytes 161288 | tf_op jit(solution)/shard_map/ppermute | solution.py:32
  202.3 9.4 %collective-permute-start.12 = (f32[105,128]{0,1:T(8,128)S(1)}, f32[105,128]{0,1:T(8,128)S(1)}, u32[]{:S(2)}, u32[]{:S(2)}) collective-permute-start(f32[105,128]{0,1:T(8,128)S(1)} %add.235), channel_id=1, source_target_pairs={{0,4},{1,5},{2,6},{3,7},{4,0},{5,1},{6,2},{7,3},{8,12},{9,13},{10,... | collective-permute-start | bytes 161288 | tf_op jit(solution)/shard_map/ppermute | solution.py:32
  211.7 6.9 %collective-permute-start.13 = (f32[105,128]{0,1:T(8,128)S(1)}, f32[105,128]{0,1:T(8,128)S(1)}, u32[]{:S(2)}, u32[]{:S(2)}) collective-permute-start(f32[105,128]{0,1:T(8,128)S(1)} %add.236), channel_id=1, source_target_pairs={{0,16},{1,17},{2,18},{3,19},{4,20},{5,21},{6,22},{7,23},{8,24},{9,... | collective-permute-start | bytes 161288 | tf_op jit(solution)/shard_map/ppermute | solution.py:32
  218.6 7.2 %collective-permute-start.14 = (f32[105,128]{0,1:T(8,128)S(1)}, f32[105,128]{0,1:T(8,128)S(1)}, u32[]{:S(2)}, u32[]{:S(2)}) collective-permute-start(f32[105,128]{0,1:T(8,128)S(1)} %add.237), channel_id=1, source_target_pairs={{0,32},{1,33},{2,34},{3,35},{4,36},{5,37},{6,38},{7,39},{8,40},{9,... | collective-permute-start | bytes 161288 | tf_op jit(solution)/shard_map/ppermute | solution.py:32
  225.7 3.1 %collective-permute-start.15 = (f32[105,128]{0,1:T(8,128)S(1)}, f32[105,128]{0,1:T(8,128)S(1)}, u32[]{:S(2)}, u32[]{:S(2)}) collective-permute-start(f32[105,128]{0,1:T(8,128)S(1)} %add.238), channel_id=1, source_target_pairs={{0,128},{1,129},{2,130},{3,131},{4,132},{5,133},{6,134},{7,135},{8... | collective-permute-start | bytes 161288 | tf_op jit(solution)/shard_map/ppermute | solution.py:32
  228.9 7.7 %collective-permute-start.16 = (f32[105,128]{0,1:T(8,128)S(1)}, f32[105,128]{0,1:T(8,128)S(1)}, u32[]{:S(2)}, u32[]{:S(2)}) collective-permute-start(f32[105,128]{0,1:T(8,128)S(1)} %add.239), channel_id=1, source_target_pairs={{0,256},{1,257},{2,258},{3,259},{4,260},{5,261},{6,262},{7,263},{8... | collective-permute-start | bytes 161288 | tf_op jit(solution)/shard_map/ppermute | solution.py:32
  236.6 10.4 %collective-permute-start.17 = (f32[105,128]{0,1:T(8,128)S(1)}, f32[105,128]{0,1:T(8,128)S(1)}, u32[]{:S(2)}, u32[]{:S(2)}) collective-permute-start(f32[105,128]{0,1:T(8,128)S(1)} %add.240), channel_id=1, source_target_pairs={{0,64},{1,65},{2,66},{3,67},{4,68},{5,69},{6,70},{7,71},{8,72},{9,... | collective-permute-start | bytes 161288 | tf_op jit(solution)/shard_map/ppermute | solution.py:32
  247.1 12.2 %collective-permute-start.18 = (f32[210,128]{0,1:T(8,128)S(1)}, f32[210,128]{0,1:T(8,128)S(1)}, u32[]{:S(2)}, u32[]{:S(2)}) collective-permute-start(f32[210,128]{0,1:T(8,128)S(1)} %maximum_select_fusion), channel_id=1, source_target_pairs={{0,8},{1,9},{2,10},{3,11},{4,12},{5,13},{6,14},{7,15},{8,0},{9,1},... | collective-permute-start | bytes 322568 | tf_op jit(solution)/shard_map/ppermute | solution.py:32
  260.6 20.0 %copy-start.2 = (f32[64,256]{1,0:T(8,128)}, f32[64,256]{1,0:T(8,128)S(1)}, u32[]{:S(2)}) copy-start(f32[64,256]{1,0:T(8,128)S(1)} %fusion.7) | copy-start | bytes 196612

commit v5 on v3

--- a/solution.py
+++ b/solution.py
@@ -196,7 +196,7 @@
     regrouped = lax.all_to_all(merged, "shift", split_axis=2, concat_axis=0, tiled=True)
     columns = regrouped.reshape(new_count, slab_x * quarter * depth)
     own = jnp.concatenate([products(columns, flat_basis), products(columns, columns)], axis=1)
-    total = allsum(jnp.concatenate([own.reshape(-1, half), packed], axis=0), (3, 6)) * cell_weight
+    total = allsum(jnp.concatenate([own.reshape(-1, half), packed], axis=0), (7, 3, 6)) * cell_weight
     sums = total[: own.size // half].reshape(own.shape)
     basis_gram = unpack_symmetric(total[own.size // half :], half)
     first_proj = sums[:, :basis_count]

time: 269 us -> 269 us (level); the launches traced: 265 us -> 268 us
  starting transfers between devices: 98.4 us -> 102 us
    ppermute x11 -> x12, starting transfers between devices: 59 us -> 62.6 us  [exchange(): return lax.ppermute(value, axes, [(i, i ^ mask) for i in range(total)])]
    ppermute x11 -> x12, waiting for transfers between devices: 29.4 us -> 29 us  [exchange(): return lax.ppermute(value, axes, [(i, i ^ mask) for i in range(total)])]
  transfers between devices with their start and end apart: 21 -> 22, of which waited for: 19 -> 20; matrix products, arithmetic and copies ran while one was open for 6% -> 6% of each run, Pallas kernels for 0% -> 0%
where the time goes in v5:
time: 269 us; the launch traced here: 268 us
  starting transfers between devices  102 us (38%)
  waiting for transfers between devices  102 us (38%)
  other arithmetic  26.3 us (10%)
  local copies, waits for them, and re-layouts  18.1 us (7%)
  matrix products  18 us (7%)
    ppermute x12, starting transfers between devices, exchange(): return lax.ppermute(value, axes, [(i, i ^ mask) for i in range(total)])  62.6 us
    ppermute x4, waiting for transfers between devices, padded_2(): lax.ppermute(tail, axis, [(i, (i + 1) % count) for i in range(ends)])  34.3 us
    ppermute x12, waiting for transfers between devices, exchange(): return lax.ppermute(value, axes, [(i, i ^ mask) for i in range(total)])  29 us
    ppermute x4, waiting for transfers between devices, padded_2(): lax.ppermute(head, axis, [((i + 1) % count, i) for i in range(ends)])  21.9 us
    ppermute x4, starting transfers between devices, padded_2(): lax.ppermute(tail, axis, [(i, (i + 1) % count) for i in range(ends)])  18.5 us
    all_to_all x1, waiting for transfers between devices, local(): lax.all_to_all(merged, 'shift', split_axis=2, concat_axis=0, tiled=True)  15.1 us
    dot_general x6, matrix products, products(): lax.dot_general(left_side, right_side, (((1,), (1,)), ((), ())), precisio...  11.2 us
    all_to_all x1, starting transfers between devices, local(): lax.all_to_all(tail_columns, 'shift', split_axis=0, concat_axis=2, tiled=...  10.4 us
  transfers between devices with their start and end apart: 22, of which 20 were waited for; matrix products, arithmetic and copies ran while one was open for 6% of the time, Pallas kernels for 0%

profile of v5, /device:TPU:1, one launch (start us, length us, event | category | flops | bytes accessed | tf_op | source)
XLA Modules:
  0.0 268.0 jit_solution(16383459858613946145)
XLA Ops:
  0.7 2.3 slice.164
  3.0 10.4 %all-to-all-start = ((f32[64,2,8,256]{3,2,1,0:T(8,128)}), f32[64,2,8,256]{3,2,1,0:T(8,128)S(1)}, u32[]{:S(2)}, u32[]{:S(2)}) async-start(f32[64,2,8,256]{3,2,1,0:T(8,128)} %slice.164), calls=%async_computation | async-start | bytes 2097152 | tf_op jit(solution)/shard_map/all_to_all | solution.py:181
  13.5 1.3 collective-permute-start.1
  14.8 4.0 %collective-permute-start = (f32[1,32,256]{2,1,0:T(8,128)S(1)}, f32[1,32,256]{2,1,0:T(8,128)S(1)}, u32[]{:S(2)}, u32[]{:S(2)}) collective-permute-start(f32[1,32,256]{2,1,0:T(8,128)S(1)} %get-tuple-element.57), channel_id=1, source_target_pairs={{0,1},{1,2},{2,3},{3,4},{4,5},{5,6},{6,7},{7,8},{8,9},{9,10},{10,1... | collective-permute-start | bytes 98312 | tf_op jit(solution)/shard_map/ppermute | solution.py:22
  18.8 7.9 %copy.80 = f32[32,8,16,256]{3,1,2,0:T(8,128)} copy(f32[32,8,16,256]{3,2,1,0:T(8,128)} %bitcast.69) | data formatting | bytes 8388608
  27.2 1.8 all-to-all-done
  29.3 1.1 fusion.58
  30.4 1.4 collective-permute-start.3
  31.8 4.8 %collective-permute-start.2 = (f32[2,8,1,32,256]{4,3,2,1,0:T(8,128)}, f32[2,8,1,32,256]{4,3,2,1,0:T(8,128)}, u32[]{:S(2)}, u32[]{:S(2)}) collective-permute-start(f32[2,8,1,32,256]{4,3,2,1,0:T(8,128)} %get-tuple-element.47), channel_id=1, source_target_pairs={{0,1},{1,2},{2,3},{3,4},{4,5},{5,6},{6,7},{7,8},{8,9},{9,10},{10,1... | collective-permute-start | bytes 1572872 | tf_op jit(solution)/shard_map/ppermute | solution.py:22
  36.6 3.5 %fusion.62 = f32[256,256]{1,0:T(8,128)S(1)} fusion(f32[256,4096]{1,0:T(8,128)S(1)} %bitcast.65), kind=kOutput, calls=%fused_computation.138 | convolution fusion | flops 3221225472 | bytes 4456448 | tf_op jit(solution)/shard_map/dot_general | solution.py:152
  40.1 0.7 fusion.60
  40.8 1.2 gather_fusion
  42.0 0.9 pad_maximum_fusion.6
  42.9 2.3 collective-permute-done.3
  45.3 10.5 %collective-permute-done.2 = f32[2,8,1,32,256]{4,3,2,1,0:T(8,128)} collective-permute-done((f32[2,8,1,32,256]{4,3,2,1,0:T(8,128)}, f32[2,8,1,32,256]{4,3,2,1,0:T(8,128)}, u32[]{:S(2)}, u32[]{:S(2)}) %collective-permute-start.2) | collective-permute-done | bytes 524320 | tf_op jit(solution)/shard_map/ppermute | solution.py:22
  55.8 2.8 %select_maximum_fusion.4 = f32[2,8,4,34,258]{4,3,2,1,0:T(8,128)S(1)} fusion(f32[2,8,1,32,256]{4,3,2,1,0:T(8,128)S(1)} %collective-permute-done.3, f32[2,8,2,32,256]{4,3,2,1,0:T(8,128)S(1)} %multiply_multiply_fusion, f32[2,8,1,32,256]{4,3,2,1,0:T(8,128)} %collective-permute-done.2), kind=kLoop, calls=%fused_computation.10 | loop fusion | flops 8421120 | bytes 4342784 | tf_op jit(solution)/shard_map/concatenate | solution.py:20
  58.6 1.7 multiply_add_fusion.1
  60.3 1.3 collective-permute-start.5
  61.6 4.8 %collective-permute-start.4 = (f32[2,8,1,32,256]{4,3,2,1,0:T(8,128)S(1)}, f32[2,8,1,32,256]{4,3,2,1,0:T(8,128)S(1)}, u32[]{:S(2)}, u32[]{:S(2)}) collective-permute-start(f32[2,8,1,32,256]{4,3,2,1,0:T(8,128)S(1)} %get-tuple-element.45), channel_id=1, source_target_pairs={{0,1},{1,2},{2,3},{3,4},{4,5},{5,6},{6,7},{7,8},{8,9},{9,10},{10,1... | collective-permute-start | bytes 1572872 | tf_op jit(solution)/shard_map/ppermute | solution.py:22
  66.4 9.9 %collective-permute-done.5 = f32[2,8,1,32,256]{4,3,2,1,0:T(8,128)S(1)} collective-permute-done((f32[2,8,1,32,256]{4,3,2,1,0:T(8,128)S(1)}, f32[2,8,1,32,256]{4,3,2,1,0:T(8,128)S(1)}, u32[]{:S(2)}, u32[]{:S(2)}) %collective-permute-start.5) | collective-permute-done | bytes 524320 | tf_op jit(solution)/shard_map/ppermute | solution.py:24
  76.3 11.9 %collective-permute-done.4 = f32[2,8,1,32,256]{4,3,2,1,0:T(8,128)S(1)} collective-permute-done((f32[2,8,1,32,256]{4,3,2,1,0:T(8,128)S(1)}, f32[2,8,1,32,256]{4,3,2,1,0:T(8,128)S(1)}, u32[]{:S(2)}, u32[]{:S(2)}) %collective-permute-start.4) | collective-permute-done | bytes 524320 | tf_op jit(solution)/shard_map/ppermute | solution.py:22
  88.2 1.8 select_maximum_fusion.2
  90.0 1.3 multiply_add_fusion
  91.4 1.3 collective-permute-start.7
  92.7 5.0 %collective-permute-start.6 = (f32[2,8,1,32,256]{4,3,2,1,0:T(8,128)S(1)}, f32[2,8,1,32,256]{4,3,2,1,0:T(8,128)S(1)}, u32[]{:S(2)}, u32[]{:S(2)}) collective-permute-start(f32[2,8,1,32,256]{4,3,2,1,0:T(8,128)S(1)} %get-tuple-element.43), channel_id=1, source_target_pairs={{0,1},{1,2},{2,3},{3,4},{4,5},{5,6},{6,7},{7,8},{8,9},{9,10},{10,1... | collective-permute-start | bytes 1572872 | tf_op jit(solution)/shard_map/ppermute | solution.py:22
  97.7 9.7 %collective-permute-done.7 = f32[2,8,1,32,256]{4,3,2,1,0:T(8,128)S(1)} collective-permute-done((f32[2,8,1,32,256]{4,3,2,1,0:T(8,128)S(1)}, f32[2,8,1,32,256]{4,3,2,1,0:T(8,128)S(1)}, u32[]{:S(2)}, u32[]{:S(2)}) %collective-permute-start.7) | collective-permute-done | bytes 524320 | tf_op jit(solution)/shard_map/ppermute | solution.py:24
  107.3 11.9 %collective-permute-done.6 = f32[2,8,1,32,256]{4,3,2,1,0:T(8,128)S(1)} collective-permute-done((f32[2,8,1,32,256]{4,3,2,1,0:T(8,128)S(1)}, f32[2,8,1,32,256]{4,3,2,1,0:T(8,128)S(1)}, u32[]{:S(2)}, u32[]{:S(2)}) %collective-permute-start.6) | collective-permute-done | bytes 524320 | tf_op jit(solution)/shard_map/ppermute | solution.py:22
  119.2 1.8 select_maximum_fusion
  121.1 1.5 fusion.10
  122.6 1.8 copy.61
  124.4 5.3 %all-to-all-start.1 = ((f32[16,2,32,256]{3,1,0,2:T(2,128)}), f32[16,2,32,256]{3,1,0,2:T(2,128)S(1)}, u32[]{:S(2)}, u32[]{:S(2)}) async-start(f32[16,2,32,256]{3,1,0,2:T(2,128)} %copy.61), calls=%async_computation.1 | async-start | bytes 2097152 | tf_op jit(solution)/shard_map/all_to_all | solution.py:196
  129.6 15.1 %all-to-all-done.1 = f32[16,2,32,256]{3,1,0,2:T(2,128)S(1)} async-done(((f32[16,2,32,256]{3,1,0,2:T(2,128)}), f32[16,2,32,256]{3,1,0,2:T(2,128)S(1)}, u32[]{:S(2)}, u32[]{:S(2)}) %all-to-all-start.1) | async-done | bytes 1048608 | tf_op jit(solution)/shard_map/all_to_all | solution.py:196
  145.7 1.0 fusion.64
  146.7 6.1 %fusion.63 = f32[64,256]{1,0:T(8,128)S(1)} fusion(f32[64,4096]{1,0:T(8,128)S(1)} %reshape.75, f32[256,4096]{1,0:T(8,128)} %bitcast.63), kind=kOutput, calls=%fused_computation.139 | convolution fusion | flops 805306368 | bytes 5308416 | tf_op jit(solution)/shard_map/dot_general | solution.py:152
  153.0 2.8 %collective-permute-start.8 = (f32[212,128]{1,0:T(8,128)S(1)}, f32[212,128]{1,0:T(8,128)S(1)}, u32[]{:S(2)}, u32[]{:S(2)}) collective-permute-start(f32[212,128]{1,0:T(8,128)S(1)} %dynamic-slice_bitcast_fusion), channel_id=1, source_target_pairs={{0,128},{1,129},{2,130},{3,131},{4,132},{5,133},{6,134},{7,135},{8... | collective-permute-start | bytes 325640 | tf_op jit(solution)/shard_map/ppermute | solution.py:32
  155.8 0.9 collective-permute-done.8
  156.8 6.5 %collective-permute-start.9 = (f32[106,128]{1,0:T(8,128)S(1)}, f32[106,128]{1,0:T(8,128)S(1)}, u32[]{:S(2)}, u32[]{:S(2)}) collective-permute-start(f32[106,128]{1,0:T(8,128)S(1)} %dynamic-slice_bitcast_fusion.1), channel_id=1, source_target_pairs={{0,8},{1,9},{2,10},{3,11},{4,12},{5,13},{6,14},{7,15},{8,0},{9,1},... | collective-permute-start | bytes 162824 | tf_op jit(solution)/shard_map/ppermute | solution.py:32
  163.3 2.4 collective-permute-done.9
  165.8 9.6 %collective-permute-start.10 = (f32[53,128]{0,1:T(8,128)S(1)}, f32[53,128]{0,1:T(8,128)S(1)}, u32[]{:S(2)}, u32[]{:S(2)}) collective-permute-start(f32[53,128]{0,1:T(8,128)S(1)} %bitcast.74), channel_id=1, source_target_pairs={{0,64},{1,65},{2,66},{3,67},{4,68},{5,69},{6,70},{7,71},{8,72},{9,... | collective-permute-start | bytes 81416 | tf_op jit(solution)/shard_map/ppermute | solution.py:32
  175.6 1.5 collective-permute-done.10
  177.1 1.9 collective-permute-start.11
  179.0 3.1 %collective-permute-done.11 = f32[53,128]{0,1:T(8,128)S(1)} collective-permute-done((f32[53,128]{0,1:T(8,128)S(1)}, f32[53,128]{0,1:T(8,128)S(1)}, u32[]{:S(2)}, u32[]{:S(2)}) %collective-permute-start.11) | collective-permute-done | bytes 27168 | tf_op jit(solution)/shard_map/ppermute | solution.py:32
  182.1 1.9 collective-permute-start.12
  184.1 3.1 %collective-permute-done.12 = f32[53,128]{0,1:T(8,128)S(1)} collective-permute-done((f32[53,128]{0,1:T(8,128)S(1)}, f32[53,128]{0,1:T(8,128)S(1)}, u32[]{:S(2)}, u32[]{:S(2)}) %collective-permute-start.12) | collective-permute-done | bytes 27168 | tf_op jit(solution)/shard_map/ppermute | solution.py:32
  187.2 6.2 %collective-permute-start.13 = (f32[53,128]{0,1:T(8,128)S(1)}, f32[53,128]{0,1:T(8,128)S(1)}, u32[]{:S(2)}, u32[]{:S(2)}) collective-permute-start(f32[53,128]{0,1:T(8,128)S(1)} %add.246), channel_id=1, source_target_pairs={{0,4},{1,5},{2,6},{3,7},{4,0},{5,1},{6,2},{7,3},{8,12},{9,13},{10,... | collective-permute-start | bytes 81416 | tf_op jit(solution)/shard_map/ppermute | solution.py:32
  193.3 1.6 collective-permute-done.13
  195.0 3.0 %collective-permute-start.14 = (f32[53,128]{0,1:T(8,128)S(1)}, f32[53,128]{0,1:T(8,128)S(1)}, u32[]{:S(2)}, u32[]{:S(2)}) collective-permute-start(f32[53,128]{0,1:T(8,128)S(1)} %add.247), channel_id=1, source_target_pairs={{0,16},{1,17},{2,18},{3,19},{4,20},{5,21},{6,22},{7,23},{8,24},{9,... | collective-permute-start | bytes 81416 | tf_op jit(solution)/shard_map/ppermute | solution.py:32
  198.1 2.0 collective-permute-done.14
  200.0 6.1 %collective-permute-start.15 = (f32[53,128]{0,1:T(8,128)S(1)}, f32[53,128]{0,1:T(8,128)S(1)}, u32[]{:S(2)}, u32[]{:S(2)}) collective-permute-start(f32[53,128]{0,1:T(8,128)S(1)} %add.248), channel_id=1, source_target_pairs={{0,32},{1,33},{2,34},{3,35},{4,36},{5,37},{6,38},{7,39},{8,40},{9,... | collective-permute-start | bytes 81416 | tf_op jit(solution)/shard_map/ppermute | solution.py:32
  206.2 2.1 collective-permute-done.15
  208.3 2.6 collective-permute-start.16
  210.9 3.9 %collective-permute-done.16 = f32[53,128]{0,1:T(8,128)S(1)} collective-permute-done((f32[53,128]{0,1:T(8,128)S(1)}, f32[53,128]{0,1:T(8,128)S(1)}, u32[]{:S(2)}, u32[]{:S(2)}) %collective-permute-start.16) | collective-permute-done | bytes 27168 | tf_op jit(solution)/shard_map/ppermute | solution.py:32
  214.8 5.3 %collective-permute-start.17 = (f32[53,128]{0,1:T(8,128)S(1)}, f32[53,128]{0,1:T(8,128)S(1)}, u32[]{:S(2)}, u32[]{:S(2)}) collective-permute-start(f32[53,128]{0,1:T(8,128)S(1)} %add.250), channel_id=1, source_target_pairs={{0,64},{1,65},{2,66},{3,67},{4,68},{5,69},{6,70},{7,71},{8,72},{9,... | collective-permute-start | bytes 81416 | tf_op jit(solution)/shard_map/ppermute | solution.py:32
  220.1 3.7 %collective-permute-done.17 = f32[53,128]{0,1:T(8,128)S(1)} collective-permute-done((f32[53,128]{0,1:T(8,128)S(1)}, f32[53,128]{0,1:T(8,128)S(1)}, u32[]{:S(2)}, u32[]{:S(2)}) %collective-permute-start.17) | collective-permute-done | bytes 27168 | tf_op jit(solution)/shard_map/ppermute | solution.py:32
  223.9 4.9 %collective-permute-start.18 = (f32[106,128]{0,1:T(8,128)S(1)}, f32[106,128]{0,1:T(8,128)S(1)}, u32[]{:S(2)}, u32[]{:S(2)}) collective-permute-start(f32[106,128]{0,1:T(8,128)S(1)} %maximum_select_fusion.1), channel_id=1, source_target_pairs={{0,8},{1,9},{2,10},{3,11},{4,12},{5,13},{6,14},{7,15},{8,0},{9,1},... | collective-permute-start | bytes 162824 | tf_op jit(solution)/shard_map/ppermute | solution.py:32
  228.8 4.0 %collective-permute-done.18 = f32[106,128]{0,1:T(8,128)S(1)} collective-permute-done((f32[106,128]{0,1:T(8,128)S(1)}, f32[106,128]{0,1:T(8,128)S(1)}, u32[]{:S(2)}, u32[]{:S(2)}) %collective-permute-start.18) | collective-permute-done | bytes 54304 | tf_op jit(solution)/shard_map/ppermute | solution.py:32
  233.0 11.6 %collective-permute-start.19 = (f32[212,128]{0,1:T(8,128)S(1)}, f32[212,128]{0,1:T(8,128)S(1)}, u32[]{:S(2)}, u32[]{:S(2)}) collective-permute-start(f32[212,128]{0,1:T(8,128)S(1)} %maximum_select_fusion), channel_id=1, source_target_pairs={{0,128},{1,129},{2,130},{3,131},{4,132},{5,133},{6,134},{7,135},{8... | collective-permute-start | bytes 325640 | tf_op jit(solution)/shard_map/ppermute | solution.py:32
  244.7 0.7 collective-permute-done.19
  247.7 5.8 %cholesky.17 = f32[64,64]{1,0:T(8,128)S(1)} custom-call(f32[64,64]{1,0:T(8,128)S(1)} %fusion.46), custom_call_target="Cholesky" | custom-call | tf_op jit(solution)/shard_map/jit(cholesky)/cholesky | solution.py:211
  254.2 1.3 select_bitcast_fusion
  255.5 4.9 %custom-call.6 = f32[1,64,64]{1,2,0:T(8,128)S(1)} custom-call(f32[1,64,64]{2,1,0:T(8,128)S(1)} %get-tuple-element.28), custom_call_target="InvertDiagBlocksLowerTriangular" | custom-call | tf_op jit(solution)/shard_map/triangular_solve | solution.py:212
  260.8 4.8 %fusion.66 = f32[64,4096]{1,0:T(8,128)S(1)} fusion(f32[64,256]{1,0:T(8,128)S(1)} %fusion.65, f32[256,4096]{1,0:T(8,128)} %bitcast.64), kind=kOutput, calls=%fused_computation.142 | convolution fusion | flops 805306368 | bytes 5308416 | tf_op jit(solution)/shard_map/dot_general | solution.py:158
  265.6 1.0 convolution_subtract_fusion
  266.7 1.3 copy.75
  (72 shorter events, 6.0 us)
Async XLA Ops:
  0.6 12.7 %copy-start.3 = (f32[8]{0:T(128)S(1)}, f32[8]{0:T(128)}, u32[]{:S(2)}) copy-start(f32[8]{0:T(128)} %param.6) | copy-start | bytes 100
  0.6 12.7 %copy-start.2 = (s32[2,32,256]{2,1,0:T(8,128)S(1)}, s32[2,32,256]{2,1,0:T(8,128)}, u32[]{:S(2)}) copy-start(s32[2,32,256]{2,1,0:T(8,128)} %param.5) | copy-start | bytes 196612
  0.7 12.7 %copy-start.4 = (f32[8]{0:T(128)S(1)}, f32[8]{0:T(128)}, u32[]{:S(2)}) copy-start(f32[8]{0:T(128)} %param.7) | copy-start | bytes 100
  3.0 26.1 %all-to-all-start = ((f32[64,2,8,256]{3,2,1,0:T(8,128)}), f32[64,2,8,256]{3,2,1,0:T(8,128)S(1)}, u32[]{:S(2)}, u32[]{:S(2)}) async-start(f32[64,2,8,256]{3,2,1,0:T(8,128)} %slice.164), calls=%async_computation | async-start | bytes 2097152 | tf_op jit(solution)/shard_map/all_to_all | solution.py:181
  13.5 13.3 %collective-permute-start.1 = (f32[1,32,256]{2,1,0:T(8,128)S(1)}, f32[1,32,256]{2,1,0:T(8,128)S(1)}, u32[]{:S(2)}, u32[]{:S(2)}) collective-permute-start(f32[1,32,256]{2,1,0:T(8,128)S(1)} %get-tuple-element.58), channel_id=1, source_target_pairs={{1,0},{2,1},{3,2},{4,3},{5,4},{6,5},{7,6},{8,7},{9,8},{10,9},{11,1... | collective-permute-start | bytes 98312 | tf_op jit(solution)/shard_map/ppermute | solution.py:24
  14.8 12.1 %collective-permute-start = (f32[1,32,256]{2,1,0:T(8,128)S(1)}, f32[1,32,256]{2,1,0:T(8,128)S(1)}, u32[]{:S(2)}, u32[]{:S(2)}) collective-permute-start(f32[1,32,256]{2,1,0:T(8,128)S(1)} %get-tuple-element.57), channel_id=1, source_target_pairs={{0,1},{1,2},{2,3},{3,4},{4,5},{5,6},{6,7},{7,8},{8,9},{9,10},{10,1... | collective-permute-start | bytes 98312 | tf_op jit(solution)/shard_map/ppermute | solution.py:22
  18.8 8.0 %copy-start.5 = (f32[8]{0:T(128)S(1)}, f32[8]{0:T(128)}, u32[]{:S(2)}) copy-start(f32[8]{0:T(128)} %param.8) | copy-start | bytes 100
  29.1 7.5 %copy-start = (f32[32,8,16,256]{3,1,2,0:T(8,128)S(1)}, f32[32,8,16,256]{3,1,2,0:T(8,128)}, u32[]{:S(2)}) copy-start(f32[32,8,16,256]{3,1,2,0:T(8,128)} %copy.80) | copy-start | bytes 12582916
  30.4 14.9 %collective-permute-start.3 = (f32[2,8,1,32,256]{4,3,2,1,0:T(8,128)}, f32[2,8,1,32,256]{4,3,2,1,0:T(8,128)S(1)}, u32[]{:S(2)}, u32[]{:S(2)}) collective-permute-start(f32[2,8,1,32,256]{4,3,2,1,0:T(8,128)} %get-tuple-element.48), channel_id=1, source_target_pairs={{1,0},{2,1},{3,2},{4,3},{5,4},{6,5},{7,6},{8,7},{9,8},{10,9},{11,1... | collective-permute-start | bytes 1572872 | tf_op jit(solution)/shard_map/ppermute | solution.py:24
  31.8 24.0 %collective-permute-start.2 = (f32[2,8,1,32,256]{4,3,2,1,0:T(8,128)}, f32[2,8,1,32,256]{4,3,2,1,0:T(8,128)}, u32[]{:S(2)}, u32[]{:S(2)}) collective-permute-start(f32[2,8,1,32,256]{4,3,2,1,0:T(8,128)} %get-tuple-element.47), channel_id=1, source_target_pairs={{0,1},{1,2},{2,3},{3,4},{4,5},{5,6},{6,7},{7,8},{8,9},{9,10},{10,1... | collective-permute-start | bytes 1572872 | tf_op jit(solution)/shard_map/ppermute | solution.py:22
  60.3 16.0 %collective-permute-start.5 = (f32[2,8,1,32,256]{4,3,2,1,0:T(8,128)S(1)}, f32[2,8,1,32,256]{4,3,2,1,0:T(8,128)S(1)}, u32[]{:S(2)}, u32[]{:S(2)}) collective-permute-start(f32[2,8,1,32,256]{4,3,2,1,0:T(8,128)S(1)} %get-tuple-element.46), channel_id=1, source_target_pairs={{1,0},{2,1},{3,2},{4,3},{5,4},{6,5},{7,6},{8,7},{9,8},{10,9},{11,1... | collective-permute-start | bytes 1572872 | tf_op jit(solution)/shard_map/ppermute | solution.py:24
  61.6 26.6 %collective-permute-start.4 = (f32[2,8,1,32,256]{4,3,2,1,0:T(8,128)S(1)}, f32[2,8,1,32,256]{4,3,2,1,0:T(8,128)S(1)}, u32[]{:S(2)}, u32[]{:S(2)}) collective-permute-start(f32[2,8,1,32,256]{4,3,2,1,0:T(8,128)S(1)} %get-tuple-element.45), channel_id=1, source_target_pairs={{0,1},{1,2},{2,3},{3,4},{4,5},{5,6},{6,7},{7,8},{8,9},{9,10},{10,1... | collective-permute-start | bytes 1572872 | tf_op jit(solution)/shard_map/ppermute | solution.py:22
  91.4 16.0 %collective-permute-start.7 = (f32[2,8,1,32,256]{4,3,2,1,0:T(8,128)S(1)}, f32[2,8,1,32,256]{4,3,2,1,0:T(8,128)S(1)}, u32[]{:S(2)}, u32[]{:S(2)}) collective-permute-start(f32[2,8,1,32,256]{4,3,2,1,0:T(8,128)S(1)} %get-tuple-element.44), channel_id=1, source_target_pairs={{1,0},{2,1},{3,2},{4,3},{5,4},{6,5},{7,6},{8,7},{9,8},{10,9},{11,1... | collective-permute-start | bytes 1572872 | tf_op jit(solution)/shard_map/ppermute | solution.py:24
  92.7 26.6 %collective-permute-start.6 = (f32[2,8,1,32,256]{4,3,2,1,0:T(8,128)S(1)}, f32[2,8,1,32,256]{4,3,2,1,0:T(8,128)S(1)}, u32[]{:S(2)}, u32[]{:S(2)}) collective-permute-start(f32[2,8,1,32,256]{4,3,2,1,0:T(8,128)S(1)} %get-tuple-element.43), channel_id=1, source_target_pairs={{0,1},{1,2},{2,3},{3,4},{4,5},{5,6},{6,7},{7,8},{8,9},{9,10},{10,1... | collective-permute-start | bytes 1572872 | tf_op jit(solution)/shard_map/ppermute | solution.py:22
  124.4 20.4 %all-to-all-start.1 = ((f32[16,2,32,256]{3,1,0,2:T(2,128)}), f32[16,2,32,256]{3,1,0,2:T(2,128)S(1)}, u32[]{:S(2)}, u32[]{:S(2)}) async-start(f32[16,2,32,256]{3,1,0,2:T(2,128)} %copy.61), calls=%async_computation.1 | async-start | bytes 2097152 | tf_op jit(solution)/shard_map/all_to_all | solution.py:196
  153.0 3.7 %collective-permute-start.8 = (f32[212,128]{1,0:T(8,128)S(1)}, f32[212,128]{1,0:T(8,128)S(1)}, u32[]{:S(2)}, u32[]{:S(2)}) collective-permute-start(f32[212,128]{1,0:T(8,128)S(1)} %dynamic-slice_bitcast_fusion), channel_id=1, source_target_pairs={{0,128},{1,129},{2,130},{3,131},{4,132},{5,133},{6,134},{7,135},{8... | collective-permute-start | bytes 325640 | tf_op jit(solution)/shard_map/ppermute | solution.py:32
  156.8 8.9 %collective-permute-start.9 = (f32[106,128]{1,0:T(8,128)S(1)}, f32[106,128]{1,0:T(8,128)S(1)}, u32[]{:S(2)}, u32[]{:S(2)}) collective-permute-start(f32[106,128]{1,0:T(8,128)S(1)} %dynamic-slice_bitcast_fusion.1), channel_id=1, source_target_pairs={{0,8},{1,9},{2,10},{3,11},{4,12},{5,13},{6,14},{7,15},{8,0},{9,1},... | collective-permute-start | bytes 162824 | tf_op jit(solution)/shard_map/ppermute | solution.py:32
  165.8 11.3 %collective-permute-start.10 = (f32[53,128]{0,1:T(8,128)S(1)}, f32[53,128]{0,1:T(8,128)S(1)}, u32[]{:S(2)}, u32[]{:S(2)}) collective-permute-start(f32[53,128]{0,1:T(8,128)S(1)} %bitcast.74), channel_id=1, source_target_pairs={{0,64},{1,65},{2,66},{3,67},{4,68},{5,69},{6,70},{7,71},{8,72},{9,... | collective-permute-start | bytes 81416 | tf_op jit(solution)/shard_map/ppermute | solution.py:32
  177.1 5.0 %collective-permute-start.11 = (f32[53,128]{0,1:T(8,128)S(1)}, f32[53,128]{0,1:T(8,128)S(1)}, u32[]{:S(2)}, u32[]{:S(2)}) collective-permute-start(f32[53,128]{0,1:T(8,128)S(1)} %bitcast_add_fusion.1), channel_id=1, source_target_pairs={{0,1},{1,0},{2,3},{3,2},{4,5},{5,4},{6,7},{7,6},{8,9},{9,8},{10,11... | collective-permute-start | bytes 81416 | tf_op jit(solution)/shard_map/ppermute | solution.py:32
  182.1 5.0 %collective-permute-start.12 = (f32[53,128]{0,1:T(8,128)S(1)}, f32[53,128]{0,1:T(8,128)S(1)}, u32[]{:S(2)}, u32[]{:S(2)}) collective-permute-start(f32[53,128]{0,1:T(8,128)S(1)} %add.245), channel_id=1, source_target_pairs={{0,2},{1,3},{2,0},{3,1},{4,6},{5,7},{6,4},{7,5},{8,10},{9,11},{10,... | collective-permute-start | bytes 81416 | tf_op jit(solution)/shard_map/ppermute | solution.py:32
  187.2 7.8 %collective-permute-start.13 = (f32[53,128]{0,1:T(8,128)S(1)}, f32[53,128]{0,1:T(8,128)S(1)}, u32[]{:S(2)}, u32[]{:S(2)}) collective-permute-start(f32[53,128]{0,1:T(8,128)S(1)} %add.246), channel_id=1, source_target_pairs={{0,4},{1,5},{2,6},{3,7},{4,0},{5,1},{6,2},{7,3},{8,12},{9,13},{10,... | collective-permute-start | bytes 81416 | tf_op jit(solution)/shard_map/ppermute | solution.py:32
  195.0 5.0 %collective-permute-start.14 = (f32[53,128]{0,1:T(8,128)S(1)}, f32[53,128]{0,1:T(8,128)S(1)}, u32[]{:S(2)}, u32[]{:S(2)}) collective-permute-start(f32[53,128]{0,1:T(8,128)S(1)} %add.247), channel_id=1, source_target_pairs={{0,16},{1,17},{2,18},{3,19},{4,20},{5,21},{6,22},{7,23},{8,24},{9,... | collective-permute-start | bytes 81416 | tf_op jit(solution)/shard_map/ppermute | solution.py:32
  200.0 8.2 %collective-permute-start.15 = (f32[53,128]{0,1:T(8,128)S(1)}, f32[53,128]{0,1:T(8,128)S(1)}, u32[]{:S(2)}, u32[]{:S(2)}) collective-permute-start(f32[53,128]{0,1:T(8,128)S(1)} %add.248), channel_id=1, source_target_pairs={{0,32},{1,33},{2,34},{3,35},{4,36},{5,37},{6,38},{7,39},{8,40},{9,... | collective-permute-start | bytes 81416 | tf_op jit(solution)/shard_map/ppermute | solution.py:32
  208.3 6.5 %collective-permute-start.16 = (f32[53,128]{0,1:T(8,128)S(1)}, f32[53,128]{0,1:T(8,128)S(1)}, u32[]{:S(2)}, u32[]{:S(2)}) collective-permute-start(f32[53,128]{0,1:T(8,128)S(1)} %add.249), channel_id=1, source_target_pairs={{0,256},{1,257},{2,258},{3,259},{4,260},{5,261},{6,262},{7,263},{8... | collective-permute-start | bytes 81416 | tf_op jit(solution)/shard_map/ppermute | solution.py:32
  214.8 9.0 %collective-permute-start.17 = (f32[53,128]{0,1:T(8,128)S(1)}, f32[53,128]{0,1:T(8,128)S(1)}, u32[]{:S(2)}, u32[]{:S(2)}) collective-permute-start(f32[53,128]{0,1:T(8,128)S(1)} %add.250), channel_id=1, source_target_pairs={{0,64},{1,65},{2,66},{3,67},{4,68},{5,69},{6,70},{7,71},{8,72},{9,... | collective-permute-start | bytes 81416 | tf_op jit(solution)/shard_map/ppermute | solution.py:32
  223.9 9.0 %collective-permute-start.18 = (f32[106,128]{0,1:T(8,128)S(1)}, f32[106,128]{0,1:T(8,128)S(1)}, u32[]{:S(2)}, u32[]{:S(2)}) collective-permute-start(f32[106,128]{0,1:T(8,128)S(1)} %maximum_select_fusion.1), channel_id=1, source_target_pairs={{0,8},{1,9},{2,10},{3,11},{4,12},{5,13},{6,14},{7,15},{8,0},{9,1},... | collective-permute-start | bytes 162824 | tf_op jit(solution)/shard_map/ppermute | solution.py:32
  233.0 12.3 %collective-permute-start.19 = (f32[212,128]{0,1:T(8,128)S(1)}, f32[212,128]{0,1:T(8,128)S(1)}, u32[]{:S(2)}, u32[]{:S(2)}) collective-permute-start(f32[212,128]{0,1:T(8,128)S(1)} %maximum_select_fusion), channel_id=1, source_target_pairs={{0,128},{1,129},{2,130},{3,131},{4,132},{5,133},{6,134},{7,135},{8... | collective-permute-start | bytes 325640 | tf_op jit(solution)/shard_map/ppermute | solution.py:32
  246.7 20.0 %copy-start.1 = (f32[64,256]{1,0:T(8,128)}, f32[64,256]{1,0:T(8,128)S(1)}, u32[]{:S(2)}) copy-start(f32[64,256]{1,0:T(8,128)S(1)} %fusion.3) | copy-start | bytes 196612

commit v6 on v5

--- a/solution.py
+++ b/solution.py
@@ -208,7 +208,7 @@
         - products(first_proj, coefficients)
         + products(matmul(coefficients, basis_gram), coefficients)
     )
-    factor = jnp.linalg.cholesky(gram_matrix)
+    factor = lax.linalg.cholesky(gram_matrix, symmetrize_input=False)
     inverse = lax.linalg.triangular_solve(
         factor, jnp.eye(new_count, dtype=factor.dtype), left_side=True, lower=True
     )

time: 269 us -> 269 us (level)
    unnamed x15 -> x14, local copies, waits for them, and re-layouts: 9.33 us -> 9.26 us
where the time goes in v6:
time: 269 us; the launch traced here: 268 us
  starting transfers between devices  102 us (38%)
  waiting for transfers between devices  102 us (38%)
  other arithmetic  26.3 us (10%)
  matrix products  18 us (7%)
  local copies, waits for them, and re-layouts  17.9 us (7%)
    ppermute x12, starting transfers between devices, exchange(): return lax.ppermute(value, axes, [(i, i ^ mask) for i in range(total)])  62.6 us
    ppermute x4, waiting for transfers between devices, padded_2(): lax.ppermute(tail, axis, [(i, (i + 1) % count) for i in range(ends)])  34.3 us
    ppermute x12, waiting for transfers between devices, exchange(): return lax.ppermute(value, axes, [(i, i ^ mask) for i in range(total)])  29 us
    ppermute x4, waiting for transfers between devices, padded_2(): lax.ppermute(head, axis, [((i + 1) % count, i) for i in range(ends)])  21.9 us
    ppermute x4, starting transfers between devices, padded_2(): lax.ppermute(tail, axis, [(i, (i + 1) % count) for i in range(ends)])  18.5 us
    all_to_all x1, waiting for transfers between devices, local(): lax.all_to_all(merged, 'shift', split_axis=2, concat_axis=0, tiled=True)  15.1 us
    dot_general x6, matrix products, products(): lax.dot_general(left_side, right_side, (((1,), (1,)), ((), ())), precisio...  11.2 us
    all_to_all x1, starting transfers between devices, local(): lax.all_to_all(tail_columns, 'shift', split_axis=0, concat_axis=2, tiled=...  10.4 us
  transfers between devices with their start and end apart: 22, of which 20 were waited for; matrix products, arithmetic and copies ran while one was open for 6% of the time, Pallas kernels for 0%

profile of v6, /device:TPU:1, one launch (start us, length us, event | category | flops | bytes accessed | tf_op | source)
XLA Modules:
  0.0 267.8 jit_solution(13321241273461968848)
XLA Ops:
  0.7 2.3 slice.162
  3.0 10.4 %all-to-all-start = ((f32[64,2,8,256]{3,2,1,0:T(8,128)}), f32[64,2,8,256]{3,2,1,0:T(8,128)S(1)}, u32[]{:S(2)}, u32[]{:S(2)}) async-start(f32[64,2,8,256]{3,2,1,0:T(8,128)} %slice.162), calls=%async_computation | async-start | bytes 2097152 | tf_op jit(solution)/shard_map/all_to_all | solution.py:181
  13.5 1.3 collective-permute-start.1
  14.8 4.0 %collective-permute-start = (f32[1,32,256]{2,1,0:T(8,128)S(1)}, f32[1,32,256]{2,1,0:T(8,128)S(1)}, u32[]{:S(2)}, u32[]{:S(2)}) collective-permute-start(f32[1,32,256]{2,1,0:T(8,128)S(1)} %get-tuple-element.57), channel_id=1, source_target_pairs={{0,1},{1,2},{2,3},{3,4},{4,5},{5,6},{6,7},{7,8},{8,9},{9,10},{10,1... | collective-permute-start | bytes 98312 | tf_op jit(solution)/shard_map/ppermute | solution.py:22
  18.8 7.9 %copy.51 = f32[32,8,16,256]{3,1,2,0:T(8,128)} copy(f32[32,8,16,256]{3,2,1,0:T(8,128)} %bitcast.65) | data formatting | bytes 8388608
  27.2 1.8 all-to-all-done
  29.3 1.1 fusion.57
  30.4 1.4 collective-permute-start.3
  31.8 4.8 %collective-permute-start.2 = (f32[2,8,1,32,256]{4,3,2,1,0:T(8,128)}, f32[2,8,1,32,256]{4,3,2,1,0:T(8,128)}, u32[]{:S(2)}, u32[]{:S(2)}) collective-permute-start(f32[2,8,1,32,256]{4,3,2,1,0:T(8,128)} %get-tuple-element.47), channel_id=1, source_target_pairs={{0,1},{1,2},{2,3},{3,4},{4,5},{5,6},{6,7},{7,8},{8,9},{9,10},{10,1... | collective-permute-start | bytes 1572872 | tf_op jit(solution)/shard_map/ppermute | solution.py:22
  36.6 3.5 %fusion.61 = f32[256,256]{1,0:T(8,128)S(1)} fusion(f32[256,4096]{1,0:T(8,128)S(1)} %bitcast.61), kind=kOutput, calls=%fused_computation.136 | convolution fusion | flops 3221225472 | bytes 4456448 | tf_op jit(solution)/shard_map/dot_general | solution.py:152
  40.1 0.7 fusion.59
  40.8 1.2 gather_fusion
  42.0 0.9 pad_maximum_fusion.6
  42.9 2.3 collective-permute-done.3
  45.3 10.5 %collective-permute-done.2 = f32[2,8,1,32,256]{4,3,2,1,0:T(8,128)} collective-permute-done((f32[2,8,1,32,256]{4,3,2,1,0:T(8,128)}, f32[2,8,1,32,256]{4,3,2,1,0:T(8,128)}, u32[]{:S(2)}, u32[]{:S(2)}) %collective-permute-start.2) | collective-permute-done | bytes 524320 | tf_op jit(solution)/shard_map/ppermute | solution.py:22
  55.8 2.8 %select_maximum_fusion.4 = f32[2,8,4,34,258]{4,3,2,1,0:T(8,128)S(1)} fusion(f32[2,8,1,32,256]{4,3,2,1,0:T(8,128)S(1)} %collective-permute-done.3, f32[2,8,2,32,256]{4,3,2,1,0:T(8,128)S(1)} %multiply_multiply_fusion, f32[2,8,1,32,256]{4,3,2,1,0:T(8,128)} %collective-permute-done.2), kind=kLoop, calls=%fused_computation.10 | loop fusion | flops 8421120 | bytes 4342784 | tf_op jit(solution)/shard_map/concatenate | solution.py:20
  58.6 1.7 multiply_add_fusion.1
  60.3 1.3 collective-permute-start.5
  61.6 4.8 %collective-permute-start.4 = (f32[2,8,1,32,256]{4,3,2,1,0:T(8,128)S(1)}, f32[2,8,1,32,256]{4,3,2,1,0:T(8,128)S(1)}, u32[]{:S(2)}, u32[]{:S(2)}) collective-permute-start(f32[2,8,1,32,256]{4,3,2,1,0:T(8,128)S(1)} %get-tuple-element.45), channel_id=1, source_target_pairs={{0,1},{1,2},{2,3},{3,4},{4,5},{5,6},{6,7},{7,8},{8,9},{9,10},{10,1... | collective-permute-start | bytes 1572872 | tf_op jit(solution)/shard_map/ppermute | solution.py:22
  66.4 9.9 %collective-permute-done.5 = f32[2,8,1,32,256]{4,3,2,1,0:T(8,128)S(1)} collective-permute-done((f32[2,8,1,32,256]{4,3,2,1,0:T(8,128)S(1)}, f32[2,8,1,32,256]{4,3,2,1,0:T(8,128)S(1)}, u32[]{:S(2)}, u32[]{:S(2)}) %collective-permute-start.5) | collective-permute-done | bytes 524320 | tf_op jit(solution)/shard_map/ppermute | solution.py:24
  76.3 11.9 %collective-permute-done.4 = f32[2,8,1,32,256]{4,3,2,1,0:T(8,128)S(1)} collective-permute-done((f32[2,8,1,32,256]{4,3,2,1,0:T(8,128)S(1)}, f32[2,8,1,32,256]{4,3,2,1,0:T(8,128)S(1)}, u32[]{:S(2)}, u32[]{:S(2)}) %collective-permute-start.4) | collective-permute-done | bytes 524320 | tf_op jit(solution)/shard_map/ppermute | solution.py:22
  88.2 1.8 select_maximum_fusion.2
  90.0 1.3 multiply_add_fusion
  91.4 1.3 collective-permute-start.7
  92.7 5.0 %collective-permute-start.6 = (f32[2,8,1,32,256]{4,3,2,1,0:T(8,128)S(1)}, f32[2,8,1,32,256]{4,3,2,1,0:T(8,128)S(1)}, u32[]{:S(2)}, u32[]{:S(2)}) collective-permute-start(f32[2,8,1,32,256]{4,3,2,1,0:T(8,128)S(1)} %get-tuple-element.43), channel_id=1, source_target_pairs={{0,1},{1,2},{2,3},{3,4},{4,5},{5,6},{6,7},{7,8},{8,9},{9,10},{10,1... | collective-permute-start | bytes 1572872 | tf_op jit(solution)/shard_map/ppermute | solution.py:22
  97.7 9.7 %collective-permute-done.7 = f32[2,8,1,32,256]{4,3,2,1,0:T(8,128)S(1)} collective-permute-done((f32[2,8,1,32,256]{4,3,2,1,0:T(8,128)S(1)}, f32[2,8,1,32,256]{4,3,2,1,0:T(8,128)S(1)}, u32[]{:S(2)}, u32[]{:S(2)}) %collective-permute-start.7) | collective-permute-done | bytes 524320 | tf_op jit(solution)/shard_map/ppermute | solution.py:24
  107.3 11.9 %collective-permute-done.6 = f32[2,8,1,32,256]{4,3,2,1,0:T(8,128)S(1)} collective-permute-done((f32[2,8,1,32,256]{4,3,2,1,0:T(8,128)S(1)}, f32[2,8,1,32,256]{4,3,2,1,0:T(8,128)S(1)}, u32[]{:S(2)}, u32[]{:S(2)}) %collective-permute-start.6) | collective-permute-done | bytes 524320 | tf_op jit(solution)/shard_map/ppermute | solution.py:22
  119.2 1.8 select_maximum_fusion
  121.1 1.5 fusion.10
  122.6 1.8 copy.41
  124.4 5.3 %all-to-all-start.1 = ((f32[16,2,32,256]{3,1,0,2:T(2,128)}), f32[16,2,32,256]{3,1,0,2:T(2,128)S(1)}, u32[]{:S(2)}, u32[]{:S(2)}) async-start(f32[16,2,32,256]{3,1,0,2:T(2,128)} %copy.41), calls=%async_computation.1 | async-start | bytes 2097152 | tf_op jit(solution)/shard_map/all_to_all | solution.py:196
  129.6 15.1 %all-to-all-done.1 = f32[16,2,32,256]{3,1,0,2:T(2,128)S(1)} async-done(((f32[16,2,32,256]{3,1,0,2:T(2,128)}), f32[16,2,32,256]{3,1,0,2:T(2,128)S(1)}, u32[]{:S(2)}, u32[]{:S(2)}) %all-to-all-start.1) | async-done | bytes 1048608 | tf_op jit(solution)/shard_map/all_to_all | solution.py:196
  145.7 1.0 fusion.63
  146.7 6.1 %fusion.62 = f32[64,256]{1,0:T(8,128)S(1)} fusion(f32[64,4096]{1,0:T(8,128)S(1)} %reshape.74, f32[256,4096]{1,0:T(8,128)} %bitcast.59), kind=kOutput, calls=%fused_computation.137 | convolution fusion | flops 805306368 | bytes 5308416 | tf_op jit(solution)/shard_map/dot_general | solution.py:152
  153.0 2.8 %collective-permute-start.8 = (f32[212,128]{1,0:T(8,128)S(1)}, f32[212,128]{1,0:T(8,128)S(1)}, u32[]{:S(2)}, u32[]{:S(2)}) collective-permute-start(f32[212,128]{1,0:T(8,128)S(1)} %dynamic-slice_bitcast_fusion), channel_id=1, source_target_pairs={{0,128},{1,129},{2,130},{3,131},{4,132},{5,133},{6,134},{7,135},{8... | collective-permute-start | bytes 325640 | tf_op jit(solution)/shard_map/ppermute | solution.py:32
  155.8 0.9 collective-permute-done.8
  156.8 6.5 %collective-permute-start.9 = (f32[106,128]{1,0:T(8,128)S(1)}, f32[106,128]{1,0:T(8,128)S(1)}, u32[]{:S(2)}, u32[]{:S(2)}) collective-permute-start(f32[106,128]{1,0:T(8,128)S(1)} %dynamic-slice_bitcast_fusion.1), channel_id=1, source_target_pairs={{0,8},{1,9},{2,10},{3,11},{4,12},{5,13},{6,14},{7,15},{8,0},{9,1},... | collective-permute-start | bytes 162824 | tf_op jit(solution)/shard_map/ppermute | solution.py:32
  163.3 2.4 collective-permute-done.9
  165.8 9.6 %collective-permute-start.10 = (f32[53,128]{0,1:T(8,128)S(1)}, f32[53,128]{0,1:T(8,128)S(1)}, u32[]{:S(2)}, u32[]{:S(2)}) collective-permute-start(f32[53,128]{0,1:T(8,128)S(1)} %bitcast.70), channel_id=1, source_target_pairs={{0,64},{1,65},{2,66},{3,67},{4,68},{5,69},{6,70},{7,71},{8,72},{9,... | collective-permute-start | bytes 81416 | tf_op jit(solution)/shard_map/ppermute | solution.py:32
  175.6 1.5 collective-permute-done.10
  177.1 1.9 collective-permute-start.11
  179.0 3.1 %collective-permute-done.11 = f32[53,128]{0,1:T(8,128)S(1)} collective-permute-done((f32[53,128]{0,1:T(8,128)S(1)}, f32[53,128]{0,1:T(8,128)S(1)}, u32[]{:S(2)}, u32[]{:S(2)}) %collective-permute-start.11) | collective-permute-done | bytes 27168 | tf_op jit(solution)/shard_map/ppermute | solution.py:32
  182.1 1.9 collective-permute-start.12
  184.1 3.1 %collective-permute-done.12 = f32[53,128]{0,1:T(8,128)S(1)} collective-permute-done((f32[53,128]{0,1:T(8,128)S(1)}, f32[53,128]{0,1:T(8,128)S(1)}, u32[]{:S(2)}, u32[]{:S(2)}) %collective-permute-start.12) | collective-permute-done | bytes 27168 | tf_op jit(solution)/shard_map/ppermute | solution.py:32
  187.2 6.2 %collective-permute-start.13 = (f32[53,128]{0,1:T(8,128)S(1)}, f32[53,128]{0,1:T(8,128)S(1)}, u32[]{:S(2)}, u32[]{:S(2)}) collective-permute-start(f32[53,128]{0,1:T(8,128)S(1)} %add.241), channel_id=1, source_target_pairs={{0,4},{1,5},{2,6},{3,7},{4,0},{5,1},{6,2},{7,3},{8,12},{9,13},{10,... | collective-permute-start | bytes 81416 | tf_op jit(solution)/shard_map/ppermute | solution.py:32
  193.3 1.6 collective-permute-done.13
  195.0 3.0 %collective-permute-start.14 = (f32[53,128]{0,1:T(8,128)S(1)}, f32[53,128]{0,1:T(8,128)S(1)}, u32[]{:S(2)}, u32[]{:S(2)}) collective-permute-start(f32[53,128]{0,1:T(8,128)S(1)} %add.242), channel_id=1, source_target_pairs={{0,16},{1,17},{2,18},{3,19},{4,20},{5,21},{6,22},{7,23},{8,24},{9,... | collective-permute-start | bytes 81416 | tf_op jit(solution)/shard_map/ppermute | solution.py:32
  198.1 2.0 collective-permute-done.14
  200.0 6.1 %collective-permute-start.15 = (f32[53,128]{0,1:T(8,128)S(1)}, f32[53,128]{0,1:T(8,128)S(1)}, u32[]{:S(2)}, u32[]{:S(2)}) collective-permute-start(f32[53,128]{0,1:T(8,128)S(1)} %add.243), channel_id=1, source_target_pairs={{0,32},{1,33},{2,34},{3,35},{4,36},{5,37},{6,38},{7,39},{8,40},{9,... | collective-permute-start | bytes 81416 | tf_op jit(solution)/shard_map/ppermute | solution.py:32
  206.2 2.1 collective-permute-done.15
  208.3 2.6 collective-permute-start.16
  210.9 3.9 %collective-permute-done.16 = f32[53,128]{0,1:T(8,128)S(1)} collective-permute-done((f32[53,128]{0,1:T(8,128)S(1)}, f32[53,128]{0,1:T(8,128)S(1)}, u32[]{:S(2)}, u32[]{:S(2)}) %collective-permute-start.16) | collective-permute-done | bytes 27168 | tf_op jit(solution)/shard_map/ppermute | solution.py:32
  214.8 5.3 %collective-permute-start.17 = (f32[53,128]{0,1:T(8,128)S(1)}, f32[53,128]{0,1:T(8,128)S(1)}, u32[]{:S(2)}, u32[]{:S(2)}) collective-permute-start(f32[53,128]{0,1:T(8,128)S(1)} %add.245), channel_id=1, source_target_pairs={{0,64},{1,65},{2,66},{3,67},{4,68},{5,69},{6,70},{7,71},{8,72},{9,... | collective-permute-start | bytes 81416 | tf_op jit(solution)/shard_map/ppermute | solution.py:32
  220.1 3.7 %collective-permute-done.17 = f32[53,128]{0,1:T(8,128)S(1)} collective-permute-done((f32[53,128]{0,1:T(8,128)S(1)}, f32[53,128]{0,1:T(8,128)S(1)}, u32[]{:S(2)}, u32[]{:S(2)}) %collective-permute-start.17) | collective-permute-done | bytes 27168 | tf_op jit(solution)/shard_map/ppermute | solution.py:32
  223.9 4.9 %collective-permute-start.18 = (f32[106,128]{0,1:T(8,128)S(1)}, f32[106,128]{0,1:T(8,128)S(1)}, u32[]{:S(2)}, u32[]{:S(2)}) collective-permute-start(f32[106,128]{0,1:T(8,128)S(1)} %maximum_select_fusion.1), channel_id=1, source_target_pairs={{0,8},{1,9},{2,10},{3,11},{4,12},{5,13},{6,14},{7,15},{8,0},{9,1},... | collective-permute-start | bytes 162824 | tf_op jit(solution)/shard_map/ppermute | solution.py:32
  228.8 4.0 %collective-permute-done.18 = f32[106,128]{0,1:T(8,128)S(1)} collective-permute-done((f32[106,128]{0,1:T(8,128)S(1)}, f32[106,128]{0,1:T(8,128)S(1)}, u32[]{:S(2)}, u32[]{:S(2)}) %collective-permute-start.18) | collective-permute-done | bytes 54304 | tf_op jit(solution)/shard_map/ppermute | solution.py:32
  233.0 11.6 %collective-permute-start.19 = (f32[212,128]{0,1:T(8,128)S(1)}, f32[212,128]{0,1:T(8,128)S(1)}, u32[]{:S(2)}, u32[]{:S(2)}) collective-permute-start(f32[212,128]{0,1:T(8,128)S(1)} %maximum_select_fusion), channel_id=1, source_target_pairs={{0,128},{1,129},{2,130},{3,131},{4,132},{5,133},{6,134},{7,135},{8... | collective-permute-start | bytes 325640 | tf_op jit(solution)/shard_map/ppermute | solution.py:32
  244.7 0.7 collective-permute-done.19
  247.5 5.8 %cholesky.17 = f32[64,64]{1,0:T(8,128)S(1)} custom-call(f32[64,64]{1,0:T(8,128)S(1)} %convolution_add_fusion), custom_call_target="Cholesky" | custom-call | tf_op jit(solution)/shard_map/cholesky | solution.py:211
  254.0 1.3 select_bitcast_fusion
  255.3 4.9 %custom-call.5 = f32[1,64,64]{1,2,0:T(8,128)S(1)} custom-call(f32[1,64,64]{2,1,0:T(8,128)S(1)} %get-tuple-element.28), custom_call_target="InvertDiagBlocksLowerTriangular" | custom-call | tf_op jit(solution)/shard_map/triangular_solve | solution.py:212
  260.6 4.8 %fusion.65 = f32[64,4096]{1,0:T(8,128)S(1)} fusion(f32[64,256]{1,0:T(8,128)S(1)} %fusion.64, f32[256,4096]{1,0:T(8,128)} %bitcast.60), kind=kOutput, calls=%fused_computation.140 | convolution fusion | flops 805306368 | bytes 5308416 | tf_op jit(solution)/shard_map/dot_general | solution.py:158
  265.4 1.0 convolution_subtract_fusion
  266.5 1.3 copy.50
  (68 shorter events, 5.8 us)
Async XLA Ops:
  0.6 12.7 %copy-start.3 = (f32[8]{0:T(128)S(1)}, f32[8]{0:T(128)}, u32[]{:S(2)}) copy-start(f32[8]{0:T(128)} %param.6) | copy-start | bytes 100
  0.6 12.7 %copy-start.2 = (s32[2,32,256]{2,1,0:T(8,128)S(1)}, s32[2,32,256]{2,1,0:T(8,128)}, u32[]{:S(2)}) copy-start(s32[2,32,256]{2,1,0:T(8,128)} %param.5) | copy-start | bytes 196612
  0.7 12.7 %copy-start.4 = (f32[8]{0:T(128)S(1)}, f32[8]{0:T(128)}, u32[]{:S(2)}) copy-start(f32[8]{0:T(128)} %param.7) | copy-start | bytes 100
  3.0 26.1 %all-to-all-start = ((f32[64,2,8,256]{3,2,1,0:T(8,128)}), f32[64,2,8,256]{3,2,1,0:T(8,128)S(1)}, u32[]{:S(2)}, u32[]{:S(2)}) async-start(f32[64,2,8,256]{3,2,1,0:T(8,128)} %slice.162), calls=%async_computation | async-start | bytes 2097152 | tf_op jit(solution)/shard_map/all_to_all | solution.py:181
  13.5 13.3 %collective-permute-start.1 = (f32[1,32,256]{2,1,0:T(8,128)S(1)}, f32[1,32,256]{2,1,0:T(8,128)S(1)}, u32[]{:S(2)}, u32[]{:S(2)}) collective-permute-start(f32[1,32,256]{2,1,0:T(8,128)S(1)} %get-tuple-element.58), channel_id=1, source_target_pairs={{1,0},{2,1},{3,2},{4,3},{5,4},{6,5},{7,6},{8,7},{9,8},{10,9},{11,1... | collective-permute-start | bytes 98312 | tf_op jit(solution)/shard_map/ppermute | solution.py:24
  14.8 12.1 %collective-permute-start = (f32[1,32,256]{2,1,0:T(8,128)S(1)}, f32[1,32,256]{2,1,0:T(8,128)S(1)}, u32[]{:S(2)}, u32[]{:S(2)}) collective-permute-start(f32[1,32,256]{2,1,0:T(8,128)S(1)} %get-tuple-element.57), channel_id=1, source_target_pairs={{0,1},{1,2},{2,3},{3,4},{4,5},{5,6},{6,7},{7,8},{8,9},{9,10},{10,1... | collective-permute-start | bytes 98312 | tf_op jit(solution)/shard_map/ppermute | solution.py:22
  18.8 8.0 %copy-start.5 = (f32[8]{0:T(128)S(1)}, f32[8]{0:T(128)}, u32[]{:S(2)}) copy-start(f32[8]{0:T(128)} %param.8) | copy-start | bytes 100
  29.1 7.5 %copy-start = (f32[32,8,16,256]{3,1,2,0:T(8,128)S(1)}, f32[32,8,16,256]{3,1,2,0:T(8,128)}, u32[]{:S(2)}) copy-start(f32[32,8,16,256]{3,1,2,0:T(8,128)} %copy.51) | copy-start | bytes 12582916
  30.4 14.9 %collective-permute-start.3 = (f32[2,8,1,32,256]{4,3,2,1,0:T(8,128)}, f32[2,8,1,32,256]{4,3,2,1,0:T(8,128)S(1)}, u32[]{:S(2)}, u32[]{:S(2)}) collective-permute-start(f32[2,8,1,32,256]{4,3,2,1,0:T(8,128)} %get-tuple-element.48), channel_id=1, source_target_pairs={{1,0},{2,1},{3,2},{4,3},{5,4},{6,5},{7,6},{8,7},{9,8},{10,9},{11,1... | collective-permute-start | bytes 1572872 | tf_op jit(solution)/shard_map/ppermute | solution.py:24
  31.8 24.0 %collective-permute-start.2 = (f32[2,8,1,32,256]{4,3,2,1,0:T(8,128)}, f32[2,8,1,32,256]{4,3,2,1,0:T(8,128)}, u32[]{:S(2)}, u32[]{:S(2)}) collective-permute-start(f32[2,8,1,32,256]{4,3,2,1,0:T(8,128)} %get-tuple-element.47), channel_id=1, source_target_pairs={{0,1},{1,2},{2,3},{3,4},{4,5},{5,6},{6,7},{7,8},{8,9},{9,10},{10,1... | collective-permute-start | bytes 1572872 | tf_op jit(solution)/shard_map/ppermute | solution.py:22
  60.3 16.0 %collective-permute-start.5 = (f32[2,8,1,32,256]{4,3,2,1,0:T(8,128)S(1)}, f32[2,8,1,32,256]{4,3,2,1,0:T(8,128)S(1)}, u32[]{:S(2)}, u32[]{:S(2)}) collective-permute-start(f32[2,8,1,32,256]{4,3,2,1,0:T(8,128)S(1)} %get-tuple-element.46), channel_id=1, source_target_pairs={{1,0},{2,1},{3,2},{4,3},{5,4},{6,5},{7,6},{8,7},{9,8},{10,9},{11,1... | collective-permute-start | bytes 1572872 | tf_op jit(solution)/shard_map/ppermute | solution.py:24
  61.6 26.6 %collective-permute-start.4 = (f32[2,8,1,32,256]{4,3,2,1,0:T(8,128)S(1)}, f32[2,8,1,32,256]{4,3,2,1,0:T(8,128)S(1)}, u32[]{:S(2)}, u32[]{:S(2)}) collective-permute-start(f32[2,8,1,32,256]{4,3,2,1,0:T(8,128)S(1)} %get-tuple-element.45), channel_id=1, source_target_pairs={{0,1},{1,2},{2,3},{3,4},{4,5},{5,6},{6,7},{7,8},{8,9},{9,10},{10,1... | collective-permute-start | bytes 1572872 | tf_op jit(solution)/shard_map/ppermute | solution.py:22
  91.4 16.0 %collective-permute-start.7 = (f32[2,8,1,32,256]{4,3,2,1,0:T(8,128)S(1)}, f32[2,8,1,32,256]{4,3,2,1,0:T(8,128)S(1)}, u32[]{:S(2)}, u32[]{:S(2)}) collective-permute-start(f32[2,8,1,32,256]{4,3,2,1,0:T(8,128)S(1)} %get-tuple-element.44), channel_id=1, source_target_pairs={{1,0},{2,1},{3,2},{4,3},{5,4},{6,5},{7,6},{8,7},{9,8},{10,9},{11,1... | collective-permute-start | bytes 1572872 | tf_op jit(solution)/shard_map/ppermute | solution.py:24
  92.7 26.6 %collective-permute-start.6 = (f32[2,8,1,32,256]{4,3,2,1,0:T(8,128)S(1)}, f32[2,8,1,32,256]{4,3,2,1,0:T(8,128)S(1)}, u32[]{:S(2)}, u32[]{:S(2)}) collective-permute-start(f32[2,8,1,32,256]{4,3,2,1,0:T(8,128)S(1)} %get-tuple-element.43), channel_id=1, source_target_pairs={{0,1},{1,2},{2,3},{3,4},{4,5},{5,6},{6,7},{7,8},{8,9},{9,10},{10,1... | collective-permute-start | bytes 1572872 | tf_op jit(solution)/shard_map/ppermute | solution.py:22
  124.4 20.4 %all-to-all-start.1 = ((f32[16,2,32,256]{3,1,0,2:T(2,128)}), f32[16,2,32,256]{3,1,0,2:T(2,128)S(1)}, u32[]{:S(2)}, u32[]{:S(2)}) async-start(f32[16,2,32,256]{3,1,0,2:T(2,128)} %copy.41), calls=%async_computation.1 | async-start | bytes 2097152 | tf_op jit(solution)/shard_map/all_to_all | solution.py:196
  153.0 3.7 %collective-permute-start.8 = (f32[212,128]{1,0:T(8,128)S(1)}, f32[212,128]{1,0:T(8,128)S(1)}, u32[]{:S(2)}, u32[]{:S(2)}) collective-permute-start(f32[212,128]{1,0:T(8,128)S(1)} %dynamic-slice_bitcast_fusion), channel_id=1, source_target_pairs={{0,128},{1,129},{2,130},{3,131},{4,132},{5,133},{6,134},{7,135},{8... | collective-permute-start | bytes 325640 | tf_op jit(solution)/shard_map/ppermute | solution.py:32
  156.8 8.9 %collective-permute-start.9 = (f32[106,128]{1,0:T(8,128)S(1)}, f32[106,128]{1,0:T(8,128)S(1)}, u32[]{:S(2)}, u32[]{:S(2)}) collective-permute-start(f32[106,128]{1,0:T(8,128)S(1)} %dynamic-slice_bitcast_fusion.1), channel_id=1, source_target_pairs={{0,8},{1,9},{2,10},{3,11},{4,12},{5,13},{6,14},{7,15},{8,0},{9,1},... | collective-permute-start | bytes 162824 | tf_op jit(solution)/shard_map/ppermute | solution.py:32
  165.8 11.3 %collective-permute-start.10 = (f32[53,128]{0,1:T(8,128)S(1)}, f32[53,128]{0,1:T(8,128)S(1)}, u32[]{:S(2)}, u32[]{:S(2)}) collective-permute-start(f32[53,128]{0,1:T(8,128)S(1)} %bitcast.70), channel_id=1, source_target_pairs={{0,64},{1,65},{2,66},{3,67},{4,68},{5,69},{6,70},{7,71},{8,72},{9,... | collective-permute-start | bytes 81416 | tf_op jit(solution)/shard_map/ppermute | solution.py:32
  177.1 5.0 %collective-permute-start.11 = (f32[53,128]{0,1:T(8,128)S(1)}, f32[53,128]{0,1:T(8,128)S(1)}, u32[]{:S(2)}, u32[]{:S(2)}) collective-permute-start(f32[53,128]{0,1:T(8,128)S(1)} %bitcast_add_fusion.1), channel_id=1, source_target_pairs={{0,1},{1,0},{2,3},{3,2},{4,5},{5,4},{6,7},{7,6},{8,9},{9,8},{10,11... | collective-permute-start | bytes 81416 | tf_op jit(solution)/shard_map/ppermute | solution.py:32
  182.1 5.0 %collective-permute-start.12 = (f32[53,128]{0,1:T(8,128)S(1)}, f32[53,128]{0,1:T(8,128)S(1)}, u32[]{:S(2)}, u32[]{:S(2)}) collective-permute-start(f32[53,128]{0,1:T(8,128)S(1)} %add.240), channel_id=1, source_target_pairs={{0,2},{1,3},{2,0},{3,1},{4,6},{5,7},{6,4},{7,5},{8,10},{9,11},{10,... | collective-permute-start | bytes 81416 | tf_op jit(solution)/shard_map/ppermute | solution.py:32
  187.2 7.8 %collective-permute-start.13 = (f32[53,128]{0,1:T(8,128)S(1)}, f32[53,128]{0,1:T(8,128)S(1)}, u32[]{:S(2)}, u32[]{:S(2)}) collective-permute-start(f32[53,128]{0,1:T(8,128)S(1)} %add.241), channel_id=1, source_target_pairs={{0,4},{1,5},{2,6},{3,7},{4,0},{5,1},{6,2},{7,3},{8,12},{9,13},{10,... | collective-permute-start | bytes 81416 | tf_op jit(solution)/shard_map/ppermute | solution.py:32
  195.0 5.0 %collective-permute-start.14 = (f32[53,128]{0,1:T(8,128)S(1)}, f32[53,128]{0,1:T(8,128)S(1)}, u32[]{:S(2)}, u32[]{:S(2)}) collective-permute-start(f32[53,128]{0,1:T(8,128)S(1)} %add.242), channel_id=1, source_target_pairs={{0,16},{1,17},{2,18},{3,19},{4,20},{5,21},{6,22},{7,23},{8,24},{9,... | collective-permute-start | bytes 81416 | tf_op jit(solution)/shard_map/ppermute | solution.py:32
  200.0 8.2 %collective-permute-start.15 = (f32[53,128]{0,1:T(8,128)S(1)}, f32[53,128]{0,1:T(8,128)S(1)}, u32[]{:S(2)}, u32[]{:S(2)}) collective-permute-start(f32[53,128]{0,1:T(8,128)S(1)} %add.243), channel_id=1, source_target_pairs={{0,32},{1,33},{2,34},{3,35},{4,36},{5,37},{6,38},{7,39},{8,40},{9,... | collective-permute-start | bytes 81416 | tf_op jit(solution)/shard_map/ppermute | solution.py:32
  208.3 6.5 %collective-permute-start.16 = (f32[53,128]{0,1:T(8,128)S(1)}, f32[53,128]{0,1:T(8,128)S(1)}, u32[]{:S(2)}, u32[]{:S(2)}) collective-permute-start(f32[53,128]{0,1:T(8,128)S(1)} %add.244), channel_id=1, source_target_pairs={{0,256},{1,257},{2,258},{3,259},{4,260},{5,261},{6,262},{7,263},{8... | collective-permute-start | bytes 81416 | tf_op jit(solution)/shard_map/ppermute | solution.py:32
  214.8 9.0 %collective-permute-start.17 = (f32[53,128]{0,1:T(8,128)S(1)}, f32[53,128]{0,1:T(8,128)S(1)}, u32[]{:S(2)}, u32[]{:S(2)}) collective-permute-start(f32[53,128]{0,1:T(8,128)S(1)} %add.245), channel_id=1, source_target_pairs={{0,64},{1,65},{2,66},{3,67},{4,68},{5,69},{6,70},{7,71},{8,72},{9,... | collective-permute-start | bytes 81416 | tf_op jit(solution)/shard_map/ppermute | solution.py:32
  223.9 9.0 %collective-permute-start.18 = (f32[106,128]{0,1:T(8,128)S(1)}, f32[106,128]{0,1:T(8,128)S(1)}, u32[]{:S(2)}, u32[]{:S(2)}) collective-permute-start(f32[106,128]{0,1:T(8,128)S(1)} %maximum_select_fusion.1), channel_id=1, source_target_pairs={{0,8},{1,9},{2,10},{3,11},{4,12},{5,13},{6,14},{7,15},{8,0},{9,1},... | collective-permute-start | bytes 162824 | tf_op jit(solution)/shard_map/ppermute | solution.py:32
  233.0 12.3 %collective-permute-start.19 = (f32[212,128]{0,1:T(8,128)S(1)}, f32[212,128]{0,1:T(8,128)S(1)}, u32[]{:S(2)}, u32[]{:S(2)}) collective-permute-start(f32[212,128]{0,1:T(8,128)S(1)} %maximum_select_fusion), channel_id=1, source_target_pairs={{0,128},{1,129},{2,130},{3,131},{4,132},{5,133},{6,134},{7,135},{8... | collective-permute-start | bytes 325640 | tf_op jit(solution)/shard_map/ppermute | solution.py:32
  246.6 19.9 %copy-start.1 = (f32[64,256]{1,0:T(8,128)}, f32[64,256]{1,0:T(8,128)S(1)}, u32[]{:S(2)}) copy-start(f32[64,256]{1,0:T(8,128)S(1)} %fusion.3) | copy-start | bytes 196612
